TPU v7x, 32 devices: a whole 2x2x4 slice. The times are simulated.
32 devices in a mesh: group: 2 (over x), strip: 16 (over z, y, core).
Axes of the slice: x: 2, y: 2, z: 4, core: 2. Of those that a mesh axis runs over, the one named last changes fastest.
Arguments:
- strip_fields: float32 [3, 64, 128, 128], P(None, ('group', 'strip')), may hold values from -18 to 18
- strip_riser: int32 [64, 1], P('group'), may hold values from 0 to 3; in each aligned block of 2 rows (0 to 1, 2 to 3, ...) at most 2 rows name the same one
- strip_node: int32 [64], P('group'), may hold values from 0 to 1023
- riser_owner: int32 [2, 4], P('group'), may hold values from 0 to 15, as said below
- pivot_inv: float32 [32, 8, 128, 128], P(('group', 'strip')), may hold values from -0.2 to 1
- lower_block: float32 [32, 7, 128, 128], P(('group', 'strip')), may hold values from -0.109375 to 0.109375
- upper_block: float32 [32, 7, 128, 128], P(('group', 'strip')), may hold values from -0.109375 to 0.109375
Outputs:
- vorticity: float32 [64, 128, 128], P(('group', 'strip'))
- displacement: float32 [32, 16, 1024], P(('group', 'strip'))
Inputs may be any that keep to these rules, and one draw needn't show every extreme that they name: `strip_riser`: in each aligned block of 2 strips (the strips of one device) no riser is named more than 2 times, and some block names one riser exactly 2 times. `riser_owner`: the 4 owners in a row are distinct devices.
All inputs are finite; a program needn't handle non-finite values.
Results may differ from a plain program's by a relative error of at most 0.0003.
Values sent between devices are 32-bit elements; how exact they have to be, the bound alone decides.
No kernel may reach another device: no remote copies, remote signals or barrier semaphores. Data moves between devices by JAX's collectives and lax.ppermute only.
A program may use at most 64 MiB of HBM per device.

v0:
```python
import jax
import jax.numpy as jnp
from jax import lax
from jax.sharding import PartitionSpec as P

NSUB = 8
COUPLED = 2


TIME_STEP = 0.25
VISCOSITY = 0.05
COUPLING = 0.5
EXACT_DOT = lax.Precision.HIGHEST


def make_kernels(grid_cells):
    centre = jnp.arange(grid_cells, dtype=jnp.float32) - grid_cells / 2.0 + 0.5
    near_x = (centre / (grid_cells / 16.0))[None, :]
    near_y = (centre / (grid_cells / 16.0))[:, None]
    bell_near = jnp.exp(-(near_x * near_x + near_y * near_y) / 2.0)
    source_x = -near_x * bell_near
    source_y = -near_y * bell_near
    wide_x = (centre / (grid_cells / 8.0))[None, :]
    wide_y = (centre / (grid_cells / 8.0))[:, None]
    bell_wide = jnp.exp(-(wide_x * wide_x + wide_y * wide_y) / 2.0)
    lift_kernel = -wide_x * bell_wide
    drag_kernel = wide_y * bell_wide
    lift_kernel = lift_kernel / jnp.sqrt(jnp.sum(lift_kernel * lift_kernel))
    drag_kernel = drag_kernel / jnp.sqrt(jnp.sum(drag_kernel * drag_kernel))
    return (source_x, source_y, lift_kernel, drag_kernel)


def strip_step(vorticity, flow_x, flow_y, motion, kernels, substeps):
    source_x, source_y, lift_kernel, drag_kernel = kernels
    halves = motion.reshape(motion.shape[0], 2, substeps)
    earlier = jnp.concatenate([jnp.zeros_like(halves[:, :, :1]), halves[:, :, :-1]], axis=2)
    velocity = halves - earlier
    lift_rows = []
    drag_rows = []
    for substep in range(substeps):
        right_cell = jnp.roll(vorticity, -1, axis=2)
        left_cell = jnp.roll(vorticity, 1, axis=2)
        upper_cell = jnp.roll(vorticity, -1, axis=1)
        lower_cell = jnp.roll(vorticity, 1, axis=1)
        laplacian = right_cell + left_cell + upper_cell + lower_cell - 4.0 * vorticity
        tendency = (
            VISCOSITY * laplacian
            - flow_x * (0.5 * (right_cell - left_cell))
            - flow_y * (0.5 * (upper_cell - lower_cell))
        )
        forcing = (
            velocity[:, 0, substep][:, None, None] * source_x
            - velocity[:, 1, substep][:, None, None] * source_y
        )
        vorticity = vorticity + TIME_STEP * tendency + COUPLING * forcing
        lift_rows.append(jnp.sum(vorticity * lift_kernel, axis=(1, 2)))
        drag_rows.append(jnp.sum(vorticity * drag_kernel, axis=(1, 2)))
    return (vorticity, jnp.stack(lift_rows + drag_rows, axis=1))


def apply_block(vectors, matrix):
    return lax.dot_general(vectors, matrix, (((1,), (1,)), ((), ())), precision=EXACT_DOT)


def first_contract(left_side, right_side):
    return lax.dot_general(left_side, right_side, (((0,), (0,)), ((), ())), precision=EXACT_DOT)


def beam_solve(beam_load, pivot_inv, lower_block, upper_block):
    block_count = pivot_inv.shape[0]
    block_size = pivot_inv.shape[1]
    blocks = beam_load.reshape(beam_load.shape[0], block_count, block_size)
    carried = [blocks[:, 0]]
    for block_index in range(1, block_count):
        pivoted = apply_block(carried[-1], pivot_inv[block_index - 1])
        carried.append(blocks[:, block_index] - apply_block(pivoted, lower_block[block_index - 1]))
    solved = [apply_block(carried[-1], pivot_inv[block_count - 1])]
    for block_index in range(block_count - 2, -1, -1):
        remainder = carried[block_index] - apply_block(solved[0], upper_block[block_index])
        solved.insert(0, apply_block(remainder, pivot_inv[block_index]))
    return jnp.concatenate(solved, axis=1)


def local(strip_fields, strip_riser, strip_node, riser_owner, pivot_inv, lower_block, upper_block):
    devices = lax.axis_size("strip")
    position = lax.axis_index("strip")
    per_device = strip_fields.shape[1]
    grid_cells = strip_fields.shape[2]
    node_count = pivot_inv.shape[1] * pivot_inv.shape[2]
    riser_count = riser_owner.shape[1]
    substeps = NSUB
    total_strips = per_device * devices * lax.axis_size("group")
    kernels = make_kernels(grid_cells)
    riser_match = (
        strip_riser[:, 0][:, None] == jnp.arange(riser_count, dtype=jnp.int32)[None, :]
    ).astype(jnp.int32)
    owner_index = jnp.sum(riser_match * riser_owner[0][None, :], axis=1)
    owned_here = owner_index == position
    node_hit = (
        owned_here[:, None]
        & (strip_node[:, None] == jnp.arange(node_count, dtype=jnp.int32)[None, :])
    ).astype(jnp.float32)
    local_owner = lax.dynamic_slice_in_dim(owner_index, position * per_device, per_device)
    local_node = lax.dynamic_slice_in_dim(strip_node, position * per_device, per_device)
    top_taper = 1.0 - jnp.arange(node_count, dtype=jnp.float32) / node_count
    vorticity = strip_fields[0]
    flow_x = strip_fields[1]
    flow_y = strip_fields[2]
    motion = jnp.zeros((per_device, 2 * substeps), jnp.float32)
    displacement = jnp.zeros((2 * substeps, node_count), jnp.float32)
    for coupled_step in range(COUPLED):
        vorticity, force_rows = strip_step(vorticity, flow_x, flow_y, motion, kernels, substeps)
        partial_drag = jnp.sum(force_rows[:, substeps:], axis=0)
        total_drag = lax.psum(partial_drag, ("group", "strip"))
        offset = total_drag / jnp.sqrt(jnp.float32(total_strips))
        beam_load = first_contract(
            lax.all_gather(force_rows, "strip", axis=0, tiled=True), node_hit
        )
        displacement = beam_solve(beam_load, pivot_inv[0], lower_block[0], upper_block[0])
        displacement = displacement.at[substeps:, :].add(offset[:, None] * top_taper[None, :])
        if coupled_step + 1 < COUPLED:
            every_owner = lax.all_gather(displacement[None], "strip", axis=0, tiled=True)
            chosen = jnp.take(every_owner, local_owner, axis=0)
            node_pick = jnp.broadcast_to(local_node[:, None, None], (per_device, 2 * substeps, 1))
            motion = jnp.take_along_axis(chosen, node_pick, axis=2)[:, :, 0]
    return (vorticity, displacement[None])


def solution(mesh):
    in_specs = (
        P(None, ("group", "strip"), None, None),
        P("group", None),
        P("group"),
        P("group", None),
        P(("group", "strip"), None, None, None),
        P(("group", "strip"), None, None, None),
        P(("group", "strip"), None, None, None),
    )
    out_specs = (P(("group", "strip"), None, None), P(("group", "strip"), None, None))
    return jax.shard_map(local, mesh=mesh, in_specs=in_specs, out_specs=out_specs, check_vma=False)
```

profile of v0, /device:TPU:0, one launch (start us, length us, event | category | flops | bytes accessed | tf_op | source)
XLA Modules:
  0.0 231.5 jit_solution(9136430588047142506)
XLA Ops:
  7.2 0.9 slice_bitcast_fusion
  8.5 0.8 copy-done
  12.4 0.7 multiply_reduce_fusion.32
  14.6 0.5 multiply_reduce_fusion.23
  15.9 42.0 %psum.14 = f32[8]{0:T(128)S(1)} all-reduce(f32[8]{0:T(128)S(1)} %reduce_sum.352), channel_id=1, replica_groups=mesh['group'=2,'strip'=16] {'group','strip'}, use_global_device_ids=true, to_apply=%region_20.21 | all-reduce | flops 8 | bytes 64 | tf_op jit(solution)/shard_map/psum | solution.py:114
  58.8 21.0 %all-gather = f32[16,2,16]{2,1,0:T(2,128)S(1)} all-gather(f32[1,2,16]{2,1,0:T(2,128)S(1)} %bitcast.564), channel_id=1, replica_groups=mesh['group'=2,'strip'=16] {'strip'}, dimensions={0}, use_global_device_ids=true | all-gather | bytes 2176 | tf_op jit(solution)/shard_map/all_gather | solution.py:117
  79.8 0.7 copy-done.6
  80.5 0.7 copy-done.5
  81.5 1.0 fusion.167
  82.5 1.1 convolution_subtract_fusion.27
  83.6 1.1 fusion.159
  84.7 1.1 convolution_subtract_fusion.26
  85.8 1.1 fusion.149
  86.9 1.1 convolution_subtract_fusion.25
  88.0 1.1 fusion.139
  89.0 1.1 convolution_subtract_fusion.24
  90.1 1.1 fusion.129
  91.2 1.1 convolution_subtract_fusion.23
  92.2 1.1 fusion.119
  93.3 1.1 convolution_subtract_fusion.22
  94.3 1.1 fusion.109
  95.4 1.1 convolution_subtract_fusion.21
  96.5 1.1 fusion.99
  99.3 0.3 convolution_subtract_fusion.16
  100.2 0.3 convolution_subtract_fusion.14
  100.9 0.6 copy-done.3
  102.2 33.8 %all-gather.4.cloned.1.call-done = f32[16,16,1024]{2,1,0:T(8,128)} async-done(((f32[1,16,1024]{2,1,0:T(8,128)}), f32[16,16,1024]{2,1,0:T(8,128)}) %all-gather.4.cloned.1.call-update) | async-done | bytes 1048592 | tf_op jit(solution)/shard_map/all_gather | solution.py:122
  136.0 1.8 gather_fusion
  137.8 0.8 gather_fusion.1
  142.2 1.1 multiply_reduce_fusion.7
  144.2 38.9 %psum.15 = f32[8]{0:T(128)S(1)} all-reduce(f32[8]{0:T(128)S(1)} %reduce_sum.369), channel_id=1, replica_groups=mesh['group'=2,'strip'=16] {'group','strip'}, use_global_device_ids=true, to_apply=%region_38.39 | all-reduce | flops 8 | bytes 64 | tf_op jit(solution)/shard_map/psum | solution.py:114
  183.9 20.6 %all-gather.1 = f32[16,2,16]{2,1,0:T(2,128)S(1)} all-gather(f32[1,2,16]{2,1,0:T(2,128)S(1)} %bitcast.565), channel_id=1, replica_groups=mesh['group'=2,'strip'=16] {'strip'}, dimensions={0}, use_global_device_ids=true | all-gather | bytes 2176 | tf_op jit(solution)/shard_map/all_gather | solution.py:117
  204.8 1.0 fusion.164
  205.8 1.1 convolution_subtract_fusion.13
  206.9 1.1 fusion.155
  208.0 1.1 convolution_subtract_fusion.12
  209.0 1.1 fusion.145
  210.1 1.1 convolution_subtract_fusion.11
  211.2 1.1 fusion.135
  212.2 1.1 convolution_subtract_fusion.10
  213.3 1.1 fusion.125
  214.3 1.1 convolution_subtract_fusion.9
  215.4 1.1 fusion.115
  216.5 1.1 convolution_subtract_fusion.8
  217.5 1.1 fusion.105
  218.6 1.1 convolution_subtract_fusion.7
  219.6 1.1 fusion.97
  224.1 0.6 copy-done.4
  (204 shorter events, 17.4 us)
Async XLA Ops:
  7.2 128.8 %all-gather.4.cloned.1.call-start = ((), (), s32[]{:S(2)}) async-start(), calls=%async_computation | async-start | bytes 1114112 | tf_op jit(solution)/shard_map/all_gather | solution.py:122
  8.3 1.0 copy-start
  79.8 0.7 copy-start.6
  79.8 0.7 copy-start.7
  80.5 0.7 copy-start.5
  84.7 12.9 %copy-start.2 = (f32[1,7,128,128]{3,2,1,0:T(8,128)S(1)}, f32[1,7,128,128]{3,2,1,0:T(8,128)}, u32[]{:S(2)}) copy-start(f32[1,7,128,128]{3,2,1,0:T(8,128)} %param.17) | copy-start | bytes 1376260
  85.8 12.0 %copy-start.1 = (f32[1,8,128,128]{3,2,1,0:T(8,128)S(1)}, f32[1,8,128,128]{3,2,1,0:T(8,128)}, u32[]{:S(2)}) copy-start(f32[1,8,128,128]{3,2,1,0:T(8,128)} %param.15) | copy-start | bytes 1572868
  100.9 0.6 copy-start.3
  224.1 0.6 copy-start.4
Sparse Core Ops, SparseCore 0:
  101.7 34.2 all-gather.3
where the time goes:
time: 233 us; the launch traced here: 232 us
  blocking collectives  123 us (53%)
  matrix products  38.5 us (17%)
  waiting for transfers between devices  33.8 us (15%)
  between operations  16.3 us (7%)
  local copies, waits for them, and re-layouts  14.4 us (6%)
  other arithmetic  5.94 us (3%)
    psum x2, blocking collectives, local(): total_drag = lax.psum(partial_drag, ('group', 'strip'))  80.9 us
    all_gather x2, blocking collectives, local(): lax.all_gather(force_rows, 'strip', axis=0, tiled=True)  41.6 us
    dot_general x58, matrix products, apply_block(): lax.dot_general(vectors, matrix, (((1,), (1,)), ((), ())), precision=EXAC...  38 us
    all_gather x1, waiting for transfers between devices, local(): lax.all_gather(displacement[None], 'strip', axis=0, tiled=True)  33.8 us
  transfers between devices with their start and end apart: 1, of which 1 were waited for; matrix products, arithmetic and copies ran while one was open for 0% of the time, Pallas kernels for 0%

commit v1 on v0

--- a/solution.py
+++ b/solution.py
@@ -82,47 +82,62 @@
 
 
 def local(strip_fields, strip_riser, strip_node, riser_owner, pivot_inv, lower_block, upper_block):
-    devices = lax.axis_size("strip")
     position = lax.axis_index("strip")
+    group_position = lax.axis_index("group")
+    group_count = lax.axis_size("group")
+    devices = lax.axis_size("strip") * group_count
     per_device = strip_fields.shape[1]
     grid_cells = strip_fields.shape[2]
     node_count = pivot_inv.shape[1] * pivot_inv.shape[2]
     riser_count = riser_owner.shape[1]
+    group_strips = strip_node.shape[0]
     substeps = NSUB
-    total_strips = per_device * devices * lax.axis_size("group")
+    total_strips = per_device * devices
     kernels = make_kernels(grid_cells)
     riser_match = (
         strip_riser[:, 0][:, None] == jnp.arange(riser_count, dtype=jnp.int32)[None, :]
     ).astype(jnp.int32)
     owner_index = jnp.sum(riser_match * riser_owner[0][None, :], axis=1)
-    owned_here = owner_index == position
-    node_hit = (
-        owned_here[:, None]
-        & (strip_node[:, None] == jnp.arange(node_count, dtype=jnp.int32)[None, :])
+    owned_here = (owner_index == position).astype(jnp.float32)
+    node_onehot = (
+        strip_node[:, None] == jnp.arange(node_count, dtype=jnp.int32)[None, :]
     ).astype(jnp.float32)
-    local_owner = lax.dynamic_slice_in_dim(owner_index, position * per_device, per_device)
     local_node = lax.dynamic_slice_in_dim(strip_node, position * per_device, per_device)
     top_taper = 1.0 - jnp.arange(node_count, dtype=jnp.float32) / node_count
+    local_taper = 1.0 - local_node.astype(jnp.float32) / node_count
+
+    unit_response = beam_solve(
+        node_onehot * owned_here[:, None], pivot_inv[0], lower_block[0], upper_block[0]
+    )
+    coupling = apply_block(node_onehot, unit_response) * owned_here[:, None]
+    coupling_out = jnp.where(
+        jnp.arange(group_count)[:, None, None] == group_position, coupling[None], 0.0
+    ).reshape(group_count * group_strips, group_strips)
+
     vorticity = strip_fields[0]
     flow_x = strip_fields[1]
     flow_y = strip_fields[2]
     motion = jnp.zeros((per_device, 2 * substeps), jnp.float32)
-    displacement = jnp.zeros((2 * substeps, node_count), jnp.float32)
     for coupled_step in range(COUPLED):
         vorticity, force_rows = strip_step(vorticity, flow_x, flow_y, motion, kernels, substeps)
-        partial_drag = jnp.sum(force_rows[:, substeps:], axis=0)
-        total_drag = lax.psum(partial_drag, ("group", "strip"))
-        offset = total_drag / jnp.sqrt(jnp.float32(total_strips))
-        beam_load = first_contract(
-            lax.all_gather(force_rows, "strip", axis=0, tiled=True), node_hit
-        )
-        displacement = beam_solve(beam_load, pivot_inv[0], lower_block[0], upper_block[0])
-        displacement = displacement.at[substeps:, :].add(offset[:, None] * top_taper[None, :])
+        sent = jnp.tile(force_rows, (devices, 1))
         if coupled_step + 1 < COUPLED:
-            every_owner = lax.all_gather(displacement[None], "strip", axis=0, tiled=True)
-            chosen = jnp.take(every_owner, local_owner, axis=0)
-            node_pick = jnp.broadcast_to(local_node[:, None, None], (per_device, 2 * substeps, 1))
-            motion = jnp.take_along_axis(chosen, node_pick, axis=2)[:, :, 0]
+            sent = jnp.concatenate([sent, coupling_out], axis=1)
+        received = lax.all_to_all(sent, ("group", "strip"), 0, 0, tiled=True)
+        every_force = received[:, : 2 * substeps]
+        offset = jnp.sum(every_force[:, substeps:], axis=0) / jnp.sqrt(jnp.float32(total_strips))
+        group_force = lax.dynamic_slice_in_dim(every_force, group_position * group_strips, group_strips)
+        if coupled_step + 1 < COUPLED:
+            my_coupling = jnp.sum(
+                received[:, 2 * substeps :].reshape(devices, per_device, group_strips), axis=0
+            )
+            motion = lax.dot_general(
+                my_coupling, group_force, (((1,), (0,)), ((), ())), precision=EXACT_DOT
+            )
+            motion = motion.at[:, substeps:].add(local_taper[:, None] * offset[None, :])
+        else:
+            displacement = first_contract(group_force * owned_here[:, None], unit_response)
+            displacement = displacement.at[substeps:, :].add(offset[:, None] * top_taper[None, :])
     return (vorticity, displacement[None])
 
 

time: 233 us -> 62.9 us (0.27)
  blocking collectives: 123 us -> 0 us
  matrix products: 38.5 us -> 6.89 us
  waiting for transfers between devices: 33.8 us -> 14.2 us
  between operations: 16.3 us -> 3.1 us
  starting transfers between devices: 0.04 us -> 9.86 us
  local copies, waits for them, and re-layouts: 14.4 us -> 21.4 us
    psum x2 -> x0, blocking collectives: 80.9 us -> none  [local(): total_drag = lax.psum(partial_drag, ('group', 'strip'))]
    all_gather x2 -> x0, blocking collectives: 41.6 us -> none  [local(): lax.all_gather(force_rows, 'strip', axis=0, tiled=True)]
    all_gather x1 -> x0, waiting for transfers between devices: 33.8 us -> none  [local(): lax.all_gather(displacement[None], 'strip', axis=0, tiled=True)]
    dot_general x58 -> x30, matrix products: 38 us -> 6.44 us  [apply_block(): lax.dot_general(vectors, matrix, (((1,), (1,)), ((), ())), precision=EXAC...]
    all_to_all x0 -> x2, waiting for transfers between devices: none -> 14.2 us  [local(): received = lax.all_to_all(sent, ('group', 'strip'), 0, 0, tiled=True)]
    all_to_all x0 -> x2, starting transfers between devices: none -> 9.86 us  [local(): received = lax.all_to_all(sent, ('group', 'strip'), 0, 0, tiled=True)]
    unnamed x34 -> x53, local copies, waits for them, and re-layouts: 3.65 us -> 12.5 us
    gather x4 -> x0, local copies, waits for them, and re-layouts: 2.75 us -> none  [the longest x1 1.78 us: local(): chosen = jnp.take(every_owner, local_owner, axis=0)]
  transfers between devices with their start and end apart: 1 -> 2, of which waited for: 1 -> 2; matrix products, arithmetic and copies ran while one was open for 0% -> 0% of each run, Pallas kernels for 0% -> 0%
where the time goes in v1:
time: 62.9 us; the launch traced here: 62.5 us
  local copies, waits for them, and re-layouts  21.4 us (34%)
  waiting for transfers between devices  14.2 us (23%)
  starting transfers between devices  9.86 us (16%)
  other arithmetic  7.09 us (11%)
  matrix products  6.89 us (11%)
  between operations  3.1 us (5%)
    all_to_all x2, waiting for transfers between devices, local(): received = lax.all_to_all(sent, ('group', 'strip'), 0, 0, tiled=True)  14.2 us
    unnamed x53, local copies, waits for them, and re-layouts  12.5 us
    all_to_all x2, starting transfers between devices, local(): received = lax.all_to_all(sent, ('group', 'strip'), 0, 0, tiled=True)  9.86 us
    dot_general x30, matrix products, apply_block(): lax.dot_general(vectors, matrix, (((1,), (1,)), ((), ())), precision=EXAC...  6.44 us
    another operation x34, local copies, waits for them, and re-layouts, strip_step(): return (vorticity, jnp.stack(lift_rows + drag_rows, axis=1))  3.17 us
    slice x32, local copies, waits for them, and re-layouts, strip_step(): right_cell = jnp.roll(vorticity, -1, axis=2)  2.98 us
    add x14, other arithmetic, strip_step(): vorticity = vorticity + TIME_STEP * tendency + COUPLING * forcing  2.5 us
    reduce_sum x2, other arithmetic, strip_step(): drag_rows.append(jnp.sum(vorticity * drag_kernel, axis=(1, 2)))  2.09 us
  transfers between devices with their start and end apart: 2, of which 2 were waited for; matrix products, arithmetic and copies ran while one was open for 0% of the time, Pallas kernels for 0%

profile of v1, /device:TPU:0, one launch (start us, length us, event | category | flops | bytes accessed | tf_op | source)
XLA Modules:
  0.0 62.5 jit_solution(1050595055360050635)
XLA Ops:
  0.6 0.9 %slice_bitcast_fusion = f32[2,128,128]{2,1,0:T(8,128)S(1)} fusion(f32[3,2,128,128]{3,2,1,0:T(8,128)} %param.11), kind=kLoop, calls=%fused_computation.225 | loop fusion | bytes 262144 | tf_op jit(solution)/shard_map/squeeze | solution.py:117
  1.9 0.8 %copy-done = f32[3,2,128,128]{3,2,1,0:T(8,128)S(1)} copy-done((f32[3,2,128,128]{3,2,1,0:T(8,128)S(1)}, f32[3,2,128,128]{3,2,1,0:T(8,128)}, u32[]{:S(2)}) %copy-start) | copy-done | bytes 393240
  5.8 0.7 %multiply_reduce_fusion.32 = (f32[]{:T(128)}, f32[]{:T(128)}) fusion(f32[128]{0:T(128)S(1)} %get-tuple-element.325, f32[128]{0:T(128)S(1)} %get-tuple-element.326, f32[128]{0:T(128)S(1)} %fusion.174), kind=kLoop, calls=%fused_computation.286 | loop fusion | flops 147454 | bytes 1544 | tf_op jit(solution)/shard_map/reduce_sum | solution.py:29
  8.0 1.0 %multiply_reduce_fusion.23 = (f32[2]{0:T(128)}, f32[2]{0:T(128)}, f32[2]{0:T(128)}, f32[2]{0:T(128)}, f32[2]{0:T(128)}, /*index=5*/f32[2]{0:T(128)}, f32[2]{0:T(...) fusion(f32[2,128,128]{2,1,0:T(8,128)S(1)} %fusion.3, ...), kind=kLoop, calls=%fused_computation.216 | loop fusion | flops 1736672 | bytes 2031744 | tf_op jit(solution)/shard_map/reduce_sum | solution.py:57
  9.0 0.7 %copy-done.20 = f32[2]{0:T(128)S(1)} copy-done((f32[2]{0:T(128)S(1)}, f32[2]{0:T(128)}, u32[]{:S(2)}) %copy-start.20) | copy-done | bytes 32
  9.8 0.6 copy-done.19
  10.5 0.6 copy-done.18
  11.2 0.7 %copy-done.17 = f32[2]{0:T(128)S(1)} copy-done((f32[2]{0:T(128)S(1)}, f32[2]{0:T(128)}, u32[]{:S(2)}) %copy-start.17) | copy-done | bytes 32
  11.9 0.7 %copy-done.16 = f32[2]{0:T(128)S(1)} copy-done((f32[2]{0:T(128)S(1)}, f32[2]{0:T(128)}, u32[]{:S(2)}) %copy-start.16) | copy-done | bytes 32
  12.7 0.7 %copy-done.15 = f32[2]{0:T(128)S(1)} copy-done((f32[2]{0:T(128)S(1)}, f32[2]{0:T(128)}, u32[]{:S(2)}) %copy-start.15) | copy-done | bytes 32
  13.5 0.6 copy-done.14
  14.2 0.6 copy-done.13
  14.8 0.7 %copy-done.12 = f32[2]{0:T(128)S(1)} copy-done((f32[2]{0:T(128)S(1)}, f32[2]{0:T(128)}, u32[]{:S(2)}) %copy-start.12) | copy-done | bytes 32
  15.6 0.7 %copy-done.11 = f32[2]{0:T(128)S(1)} copy-done((f32[2]{0:T(128)S(1)}, f32[2]{0:T(128)}, u32[]{:S(2)}) %copy-start.11) | copy-done | bytes 32
  16.4 0.7 %copy-done.10 = f32[2]{0:T(128)S(1)} copy-done((f32[2]{0:T(128)S(1)}, f32[2]{0:T(128)}, u32[]{:S(2)}) %copy-start.10) | copy-done | bytes 32
  17.1 0.7 %copy-done.9 = f32[2]{0:T(128)S(1)} copy-done((f32[2]{0:T(128)S(1)}, f32[2]{0:T(128)}, u32[]{:S(2)}) %copy-start.9) | copy-done | bytes 32
  17.9 0.6 copy-done.8
  18.6 0.6 copy-done.7
  19.3 0.6 %copy-done.6 = f32[2]{0:T(128)S(1)} copy-done((f32[2]{0:T(128)S(1)}, f32[2]{0:T(128)}, u32[]{:S(2)}) %copy-start.6) | copy-done | bytes 32
  20.1 0.7 %copy-done.21 = s32[1,4]{1,0:T(1,128)S(1)} copy-done((s32[1,4]{1,0:T(1,128)S(1)}, s32[1,4]{1,0:T(1,128)}, u32[]{:S(2)}) %copy-start.21) | copy-done | bytes 40
  20.9 0.6 %copy-done.5 = s32[32]{0:T(128)S(1)} copy-done((s32[32]{0:T(128)S(1)}, s32[32]{0:T(128)}, u32[]{:S(2)}) %copy-start.5) | copy-done | bytes 152
  22.0 0.2 fusion.117
  22.3 0.2 convolution_subtract_fusion.12
  22.5 0.2 fusion.112
  22.7 0.2 convolution_subtract_fusion.11
  23.2 0.2 convolution_subtract_fusion.10
  23.4 0.2 fusion.102
  23.6 0.2 convolution_subtract_fusion.9
  23.9 0.2 fusion.97
  24.1 0.2 convolution_subtract_fusion.8
  24.5 0.2 convolution_subtract_fusion.7
  25.4 0.2 convolution_subtract_fusion.5
  25.9 0.2 convolution_subtract_fusion.4
  26.3 0.2 convolution_subtract_fusion.3
  26.8 0.2 convolution_subtract_fusion.2
  27.2 0.2 convolution_subtract_fusion.1
  27.7 0.2 convolution_subtract_fusion
  28.2 0.3 convolution_multiply_fusion
  28.9 0.7 %pad_maximum_fusion.64 = f32[32,2,48]{2,1,0:T(2,128)} fusion(f32[32,2,32]{2,1,0:T(2,128)S(1)} %broadcast_select_fusion, f32[32,2,16]{2,1,0:T(2,128)S(1)} %tile.4), kind=kLoop, calls=%fused_computation.316 | loop fusion | flops 3072 | bytes 24576 | tf_op jit(solution)/shard_map/concatenate | solution.py:125
  29.7 7.3 %all-to-all-start = ((f32[32,2,48]{2,1,0:T(2,128)}), f32[32,2,48]{2,1,0:T(2,128)S(1)}, u32[]{:S(2)}, u32[]{:S(2)}) async-start(f32[32,2,48]{2,1,0:T(2,128)} %pad_maximum_fusion.64), calls=%async_computation | async-start | bytes 65536 | tf_op jit(solution)/shard_map/all_to_all | solution.py:126
  37.3 6.9 %all-to-all-done = f32[32,2,48]{2,1,0:T(2,128)S(1)} async-done(((f32[32,2,48]{2,1,0:T(2,128)}), f32[32,2,48]{2,1,0:T(2,128)S(1)}, u32[]{:S(2)}, u32[]{:S(2)}) %all-to-all-start) | async-done | bytes 12320 | tf_op jit(solution)/shard_map/all_to_all | solution.py:126
  45.0 0.2 slice_reduce_fusion.3
  48.2 1.1 %multiply_reduce_fusion.7 = (f32[2]{0:T(128)S(1)}, f32[2]{0:T(128)S(1)}, f32[2]{0:T(128)S(1)}, f32[2]{0:T(128)S(1)}, f32[2]{0:T(128)S(1)}, /*index=5*/f32[2]{0:T...) fusion(f32[2,128,128]{2,1,0:T(8,128)S(1)} %fusion.35, ...), kind=kLoop, calls=%fused_computation.199 | loop fusion | flops 1867744 | bytes 2097296 | tf_op jit(solution)/shard_map/reduce_sum | solution.py:57
  50.9 0.6 %tile.5 = f32[32,2,16]{2,1,0:T(2,128)} broadcast(f32[2,16]{1,0:T(2,128)S(1)} %stack.135), dimensions={1,2} | broadcast | bytes 4224 | tf_op jit(solution)/shard_map/tile | solution.py:123
  51.5 2.6 %all-to-all-start.1 = ((f32[32,2,16]{2,1,0:T(2,128)}), f32[32,2,16]{2,1,0:T(2,128)S(1)}, u32[]{:S(2)}, u32[]{:S(2)}) async-start(f32[32,2,16]{2,1,0:T(2,128)} %tile.5), calls=%async_computation.1 | async-start | bytes 65536 | tf_op jit(solution)/shard_map/all_to_all | solution.py:126
  54.1 7.2 %all-to-all-done.1 = f32[32,2,16]{2,1,0:T(2,128)S(1)} async-done(((f32[32,2,16]{2,1,0:T(2,128)}), f32[32,2,16]{2,1,0:T(2,128)S(1)}, u32[]{:S(2)}, u32[]{:S(2)}) %all-to-all-start.1) | async-done | bytes 4128 | tf_op jit(solution)/shard_map/all_to_all | solution.py:126
  61.4 0.3 fusion.161
  61.9 0.6 %copy-done.4 = f32[1,16,1024]{2,1,0:T(8,128)} copy-done((f32[1,16,1024]{2,1,0:T(8,128)}, f32[1,16,1024]{2,1,0:T(8,128)S(1)}, u32[]{:S(2)}) %copy-start.4) | copy-done | bytes 65560
  (189 shorter events, 13.7 us)
Async XLA Ops:
  1.8 1.0 %copy-start = (f32[3,2,128,128]{3,2,1,0:T(8,128)S(1)}, f32[3,2,128,128]{3,2,1,0:T(8,128)}, u32[]{:S(2)}) copy-start(f32[3,2,128,128]{3,2,1,0:T(8,128)} %param.11) | copy-start | bytes 1179652
  8.0 13.6 %copy-start.1 = (f32[1,8,128,128]{3,2,1,0:T(8,128)S(1)}, f32[1,8,128,128]{3,2,1,0:T(8,128)}, u32[]{:S(2)}) copy-start(f32[1,8,128,128]{3,2,1,0:T(8,128)} %param.15) | copy-start | bytes 1572868
  8.0 13.9 %copy-start.2 = (f32[1,7,128,128]{3,2,1,0:T(8,128)S(1)}, f32[1,7,128,128]{3,2,1,0:T(8,128)}, u32[]{:S(2)}) copy-start(f32[1,7,128,128]{3,2,1,0:T(8,128)} %param.16) | copy-start | bytes 1376260
  9.0 0.7 %copy-start.20 = (f32[2]{0:T(128)S(1)}, f32[2]{0:T(128)}, u32[]{:S(2)}) copy-start(f32[2]{0:T(128)} %get-tuple-element.155) | copy-start | bytes 28
  9.8 0.6 copy-start.19
  10.5 0.6 copy-start.18
  11.2 0.7 %copy-start.17 = (f32[2]{0:T(128)S(1)}, f32[2]{0:T(128)}, u32[]{:S(2)}) copy-start(f32[2]{0:T(128)} %get-tuple-element.166) | copy-start | bytes 28
  11.9 0.7 %copy-start.16 = (f32[2]{0:T(128)S(1)}, f32[2]{0:T(128)}, u32[]{:S(2)}) copy-start(f32[2]{0:T(128)} %get-tuple-element.159) | copy-start | bytes 28
  12.7 0.7 %copy-start.15 = (f32[2]{0:T(128)S(1)}, f32[2]{0:T(128)}, u32[]{:S(2)}) copy-start(f32[2]{0:T(128)} %get-tuple-element.164) | copy-start | bytes 28
  13.5 0.6 copy-start.14
  14.2 0.6 copy-start.13
  14.8 0.7 %copy-start.12 = (f32[2]{0:T(128)S(1)}, f32[2]{0:T(128)}, u32[]{:S(2)}) copy-start(f32[2]{0:T(128)} %get-tuple-element.154) | copy-start | bytes 28
  15.6 0.7 %copy-start.11 = (f32[2]{0:T(128)S(1)}, f32[2]{0:T(128)}, u32[]{:S(2)}) copy-start(f32[2]{0:T(128)} %get-tuple-element.169) | copy-start | bytes 28
  16.4 0.7 %copy-start.10 = (f32[2]{0:T(128)S(1)}, f32[2]{0:T(128)}, u32[]{:S(2)}) copy-start(f32[2]{0:T(128)} %get-tuple-element.156) | copy-start | bytes 28
  17.1 0.7 %copy-start.9 = (f32[2]{0:T(128)S(1)}, f32[2]{0:T(128)}, u32[]{:S(2)}) copy-start(f32[2]{0:T(128)} %get-tuple-element.167) | copy-start | bytes 28
  17.9 0.6 %copy-start.8 = (f32[2]{0:T(128)S(1)}, f32[2]{0:T(128)}, u32[]{:S(2)}) copy-start(f32[2]{0:T(128)} %get-tuple-element.158) | copy-start | bytes 28
  18.6 0.6 copy-start.7
  19.3 0.6 %copy-start.6 = (f32[2]{0:T(128)S(1)}, f32[2]{0:T(128)}, u32[]{:S(2)}) copy-start(f32[2]{0:T(128)} %get-tuple-element.160) | copy-start | bytes 28
  20.1 0.7 %copy-start.21 = (s32[1,4]{1,0:T(1,128)S(1)}, s32[1,4]{1,0:T(1,128)}, u32[]{:S(2)}) copy-start(s32[1,4]{1,0:T(1,128)} %param.14) | copy-start | bytes 52
  20.1 0.7 %copy-start.22 = (s32[32,1]{0,1:T(1,128)S(1)}, s32[32,1]{0,1:T(1,128)}, u32[]{:S(2)}) copy-start(s32[32,1]{0,1:T(1,128)} %param.12) | copy-start | bytes 388
  20.9 0.7 %copy-start.5 = (s32[32]{0:T(128)S(1)}, s32[32]{0:T(128)}, u32[]{:S(2)}) copy-start(s32[32]{0:T(128)} %param.13) | copy-start | bytes 388
  22.9 2.1 %copy-start.3 = (f32[1,7,128,128]{3,2,1,0:T(8,128)S(1)}, f32[1,7,128,128]{3,2,1,0:T(8,128)}, u32[]{:S(2)}) copy-start(f32[1,7,128,128]{3,2,1,0:T(8,128)} %param.17) | copy-start | bytes 1376260
  29.7 14.6 %all-to-all-start = ((f32[32,2,48]{2,1,0:T(2,128)}), f32[32,2,48]{2,1,0:T(2,128)S(1)}, u32[]{:S(2)}, u32[]{:S(2)}) async-start(f32[32,2,48]{2,1,0:T(2,128)} %pad_maximum_fusion.64), calls=%async_computation | async-start | bytes 65536 | tf_op jit(solution)/shard_map/all_to_all | solution.py:126
  51.5 9.8 %all-to-all-start.1 = ((f32[32,2,16]{2,1,0:T(2,128)}), f32[32,2,16]{2,1,0:T(2,128)S(1)}, u32[]{:S(2)}, u32[]{:S(2)}) async-start(f32[32,2,16]{2,1,0:T(2,128)} %tile.5), calls=%async_computation.1 | async-start | bytes 65536 | tf_op jit(solution)/shard_map/all_to_all | solution.py:126
  61.9 0.6 %copy-start.4 = (f32[1,16,1024]{2,1,0:T(8,128)}, f32[1,16,1024]{2,1,0:T(8,128)S(1)}, u32[]{:S(2)}) copy-start(f32[1,16,1024]{2,1,0:T(8,128)S(1)} %fusion.160) | copy-start | bytes 196612

commit v2 on v1

--- a/solution.py
+++ b/solution.py
@@ -30,32 +30,76 @@
     return (source_x, source_y, lift_kernel, drag_kernel)
 
 
-def strip_step(vorticity, flow_x, flow_y, motion, kernels, substeps):
+def advance(vorticity, flow_x, flow_y):
+    right_cell = jnp.roll(vorticity, -1, axis=2)
+    left_cell = jnp.roll(vorticity, 1, axis=2)
+    upper_cell = jnp.roll(vorticity, -1, axis=1)
+    lower_cell = jnp.roll(vorticity, 1, axis=1)
+    laplacian = right_cell + left_cell + upper_cell + lower_cell - 4.0 * vorticity
+    tendency = (
+        VISCOSITY * laplacian
+        - flow_x * (0.5 * (right_cell - left_cell))
+        - flow_y * (0.5 * (upper_cell - lower_cell))
+    )
+    return vorticity + TIME_STEP * tendency
+
+
+def kernel_sums(fields, lift_kernel, drag_kernel):
+    stacked = jnp.stack(fields, axis=0)
+    lift = jnp.sum(stacked * lift_kernel, axis=(2, 3))
+    drag = jnp.sum(stacked * drag_kernel, axis=(2, 3))
+    return lift, drag
+
+
+def free_run(vorticity, flow_x, flow_y, kernels, substeps):
+    _, _, lift_kernel, drag_kernel = kernels
+    fields = []
+    for substep in range(substeps):
+        vorticity = advance(vorticity, flow_x, flow_y)
+        fields.append(vorticity)
+    lift, drag = kernel_sums(fields, lift_kernel, drag_kernel)
+    return vorticity, jnp.concatenate([lift.T, drag.T], axis=1)
+
+
+def source_responses(flow_x, flow_y, kernels, substeps):
     source_x, source_y, lift_kernel, drag_kernel = kernels
+    shape = flow_x.shape
+    carried_x = [jnp.broadcast_to(source_x, shape)]
+    carried_y = [jnp.broadcast_to(source_y, shape)]
+    for _ in range(substeps - 1):
+        carried_x.append(advance(carried_x[-1], flow_x, flow_y))
+        carried_y.append(advance(carried_y[-1], flow_x, flow_y))
+    lift, drag = kernel_sums(carried_x + carried_y, lift_kernel, drag_kernel)
+    return carried_x, carried_y, lift, drag
+
+
+def forced_rows(free_rows, motion, response_lift, response_drag, substeps):
     halves = motion.reshape(motion.shape[0], 2, substeps)
     earlier = jnp.concatenate([jnp.zeros_like(halves[:, :, :1]), halves[:, :, :-1]], axis=2)
     velocity = halves - earlier
-    lift_rows = []
-    drag_rows = []
+    later = jnp.arange(substeps)[:, None] - jnp.arange(substeps)[None, :]
+    reach = jnp.clip(later, 0, substeps - 1)
+    mask = (later >= 0).astype(jnp.float32)
+    rows = []
+    for response in (response_lift, response_drag):
+        toeplitz_x = response[:substeps][reach] * mask[:, :, None]
+        toeplitz_y = response[substeps:][reach] * mask[:, :, None]
+        gain = jnp.sum(
+            toeplitz_x * velocity[:, 0, :].T[None, :, :] - toeplitz_y * velocity[:, 1, :].T[None, :, :],
+            axis=1,
+        )
+        rows.append(COUPLING * gain.T)
+    return free_rows + jnp.concatenate(rows, axis=1), velocity
+
+
+def forced_field(free_field, velocity, carried_x, carried_y, substeps):
+    field = free_field
     for substep in range(substeps):
-        right_cell = jnp.roll(vorticity, -1, axis=2)
-        left_cell = jnp.roll(vorticity, 1, axis=2)
-        upper_cell = jnp.roll(vorticity, -1, axis=1)
-        lower_cell = jnp.roll(vorticity, 1, axis=1)
-        laplacian = right_cell + left_cell + upper_cell + lower_cell - 4.0 * vorticity
-        tendency = (
-            VISCOSITY * laplacian
-            - flow_x * (0.5 * (right_cell - left_cell))
-            - flow_y * (0.5 * (upper_cell - lower_cell))
+        field = field + COUPLING * (
+            velocity[:, 0, substep][:, None, None] * carried_x[substeps - 1 - substep]
+            - velocity[:, 1, substep][:, None, None] * carried_y[substeps - 1 - substep]
         )
-        forcing = (
-            velocity[:, 0, substep][:, None, None] * source_x
-            - velocity[:, 1, substep][:, None, None] * source_y
-        )
-        vorticity = vorticity + TIME_STEP * tendency + COUPLING * forcing
-        lift_rows.append(jnp.sum(vorticity * lift_kernel, axis=(1, 2)))
-        drag_rows.append(jnp.sum(vorticity * drag_kernel, axis=(1, 2)))
-    return (vorticity, jnp.stack(lift_rows + drag_rows, axis=1))
+    return field
 
 
 def apply_block(vectors, matrix):
@@ -117,27 +161,24 @@
     vorticity = strip_fields[0]
     flow_x = strip_fields[1]
     flow_y = strip_fields[2]
-    motion = jnp.zeros((per_device, 2 * substeps), jnp.float32)
-    for coupled_step in range(COUPLED):
-        vorticity, force_rows = strip_step(vorticity, flow_x, flow_y, motion, kernels, substeps)
-        sent = jnp.tile(force_rows, (devices, 1))
-        if coupled_step + 1 < COUPLED:
-            sent = jnp.concatenate([sent, coupling_out], axis=1)
-        received = lax.all_to_all(sent, ("group", "strip"), 0, 0, tiled=True)
-        every_force = received[:, : 2 * substeps]
-        offset = jnp.sum(every_force[:, substeps:], axis=0) / jnp.sqrt(jnp.float32(total_strips))
-        group_force = lax.dynamic_slice_in_dim(every_force, group_position * group_strips, group_strips)
-        if coupled_step + 1 < COUPLED:
-            my_coupling = jnp.sum(
-                received[:, 2 * substeps :].reshape(devices, per_device, group_strips), axis=0
-            )
-            motion = lax.dot_general(
-                my_coupling, group_force, (((1,), (0,)), ((), ())), precision=EXACT_DOT
-            )
-            motion = motion.at[:, substeps:].add(local_taper[:, None] * offset[None, :])
-        else:
-            displacement = first_contract(group_force * owned_here[:, None], unit_response)
-            displacement = displacement.at[substeps:, :].add(offset[:, None] * top_taper[None, :])
+    vorticity, force_rows = free_run(vorticity, flow_x, flow_y, kernels, substeps)
+    sent = jnp.concatenate([jnp.tile(force_rows, (devices, 1)), coupling_out], axis=1)
+    received = lax.all_to_all(sent, ("group", "strip"), 0, 0, tiled=True)
+    free_field, free_rows = free_run(vorticity, flow_x, flow_y, kernels, substeps)
+    carried_x, carried_y, response_lift, response_drag = source_responses(flow_x, flow_y, kernels, substeps)
+    every_force = received[:, : 2 * substeps]
+    offset = jnp.sum(every_force[:, substeps:], axis=0) / jnp.sqrt(jnp.float32(total_strips))
+    group_force = lax.dynamic_slice_in_dim(every_force, group_position * group_strips, group_strips)
+    my_coupling = jnp.sum(received[:, 2 * substeps :].reshape(devices, per_device, group_strips), axis=0)
+    motion = lax.dot_general(my_coupling, group_force, (((1,), (0,)), ((), ())), precision=EXACT_DOT)
+    motion = motion.at[:, substeps:].add(local_taper[:, None] * offset[None, :])
+    force_rows, velocity = forced_rows(free_rows, motion, response_lift, response_drag, substeps)
+    received = lax.all_to_all(jnp.tile(force_rows, (devices, 1)), ("group", "strip"), 0, 0, tiled=True)
+    vorticity = forced_field(free_field, velocity, carried_x, carried_y, substeps)
+    offset = jnp.sum(received[:, substeps:], axis=0) / jnp.sqrt(jnp.float32(total_strips))
+    group_force = lax.dynamic_slice_in_dim(received, group_position * group_strips, group_strips)
+    displacement = first_contract(group_force * owned_here[:, None], unit_response)
+    displacement = displacement.at[substeps:, :].add(offset[:, None] * top_taper[None, :])
     return (vorticity, displacement[None])
 
 

time: 62.9 us -> 208 us (3.31)
  local copies, waits for them, and re-layouts: 21.4 us -> 122 us
  other arithmetic: 7.09 us -> 46.3 us
  waiting for transfers between devices: 14.2 us -> 3.95 us
  matrix products: 6.89 us -> 15.7 us
  starting transfers between devices: 9.86 us -> 13.2 us
  between operations: 3.1 us -> 5.5 us
    concatenate x0 -> x86, local copies, waits for them, and re-layouts: none -> 67.5 us  [the longest x40 32.1 us: advance(): right_cell = jnp.roll(vorticity, -1, axis=2)]
    slice x65 -> x48, local copies, waits for them, and re-layouts: 3.61 us -> 31 us  [the longest x20 15.2 us: advance(): right_cell = jnp.roll(vorticity, -1, axis=2)]
    unnamed x0 -> x20, other arithmetic: none -> 23.7 us
    all_to_all x2 -> x1, waiting for transfers between devices: 14.2 us -> 0.01 us  [local(): received = lax.all_to_all(sent, ('group', 'strip'), 0, 0, tiled=True)]
    dot_general x30, matrix products: 6.44 us -> 14.5 us  [apply_block(): lax.dot_general(vectors, matrix, (((1,), (1,)), ((), ())), precision=EXAC...]
    all_to_all x0 -> x1, starting transfers between devices: none -> 5.76 us  [local(): lax.all_to_all(jnp.tile(force_rows, (devices, 1)), ('group', 'strip'), 0,...]
    add x14 -> x28, other arithmetic: 2.5 us -> 8.24 us  [the longest x26 5.05 us: advance(): return vorticity + TIME_STEP * tendency]
    all_to_all x0 -> x1, waiting for transfers between devices: none -> 3.95 us  [local(): lax.all_to_all(jnp.tile(force_rows, (devices, 1)), ('group', 'strip'), 0,...]
  transfers between devices with their start and end apart: 2 -> 2, of which waited for: 2 -> 1; matrix products, arithmetic and copies ran while one was open for 0% -> 12% of each run, Pallas kernels for 0% -> 0%
where the time goes in v2:
time: 208 us; the launch traced here: 207 us
  local copies, waits for them, and re-layouts  122 us (59%)
  other arithmetic  46.3 us (22%)
  matrix products  15.7 us (8%)
  starting transfers between devices  13.2 us (6%)
  between operations  5.5 us (3%)
  waiting for transfers between devices  3.95 us (2%)
    concatenate x40, local copies, waits for them, and re-layouts, advance(): right_cell = jnp.roll(vorticity, -1, axis=2)  32.1 us
    concatenate x40, local copies, waits for them, and re-layouts, advance(): upper_cell = jnp.roll(vorticity, -1, axis=1)  28.1 us
    unnamed x20, other arithmetic  23.7 us
    slice x20, local copies, waits for them, and re-layouts, advance(): right_cell = jnp.roll(vorticity, -1, axis=2)  15.2 us
    dot_general x30, matrix products, apply_block(): lax.dot_general(vectors, matrix, (((1,), (1,)), ((), ())), precision=EXAC...  14.5 us
    unnamed x422, local copies, waits for them, and re-layouts  13.7 us
    slice x18, local copies, waits for them, and re-layouts, advance(): upper_cell = jnp.roll(vorticity, -1, axis=1)  10.8 us
    all_to_all x1, starting transfers between devices, local(): received = lax.all_to_all(sent, ('group', 'strip'), 0, 0, tiled=True)  7.43 us
  transfers between devices with their start and end apart: 2, of which 1 were waited for; matrix products, arithmetic and copies ran while one was open for 12% of the time, Pallas kernels for 0%

profile of v2, /device:TPU:0, one launch (start us, length us, event | category | flops | bytes accessed | tf_op | source)
XLA Modules:
  0.0 207.1 jit_solution(17588667558150031168)
XLA Ops:
  33.6 1.1 multiply_add_fusion.40
  54.3 0.9 fusion.152
  56.5 1.1 convolution_subtract_fusion.13
  57.8 1.1 convolution_subtract_fusion.12
  59.0 1.1 convolution_subtract_fusion.11
  60.3 1.1 convolution_subtract_fusion.10
  61.6 1.1 convolution_subtract_fusion.9
  62.9 1.1 convolution_subtract_fusion.8
  64.2 1.1 convolution_subtract_fusion.7
  65.5 1.1 convolution_subtract_fusion.6
  66.8 1.1 convolution_subtract_fusion.5
  70.4 0.9 convolution_multiply_fusion
  74.1 1.4 copy.2460
  76.7 5.3 %constant_dynamic-update-slice_fusion.21 = (f32[8,2,128,128]{3,2,1,0:T(8,128)S(1)}, f32[1,2,128,128]{3,2,1,0:T(8,128)}, f32[1,2,128,128]{3,2,1,0:T(8,128)}, f32[...) fusion(f32[3,2,128,128]{3,2,1,0:T(8,128)S(1)} %copy-done, ...), kind=kLoop, calls=%fused_computation.406 | loop fusion | flops 5832703 | bytes 6553600
  84.7 1.6 constant_dynamic-update-slice_fusion.6
  86.2 1.6 constant_dynamic-update-slice_fusion.5
  87.8 1.6 constant_dynamic-update-slice_fusion.4
  89.4 1.6 constant_dynamic-update-slice_fusion.3
  91.1 1.6 constant_dynamic-update-slice_fusion.2
  92.6 1.6 constant_dynamic-update-slice_fusion.1
  94.2 1.6 constant_dynamic-update-slice_fusion
  96.7 1.5 constant_dynamic-update-slice_fusion.20
  98.3 1.5 constant_dynamic-update-slice_fusion.19
  101.9 1.0 multiply_reduce_fusion.5
  104.6 7.4 %all-to-all-start = ((f32[32,2,48]{2,1,0:T(2,128)}), f32[32,2,48]{2,1,0:T(2,128)}, u32[]{:S(2)}, u32[]{:S(2)}) async-start(f32[32,2,48]{2,1,0:T(2,128)} %pad_maximum_fusion.234), calls=%async_computation | async-start | bytes 65536 | tf_op jit(solution)/shard_map/all_to_all | solution.py:166
  130.1 0.9 slice_bitcast_fusion.70
  137.9 1.4 broadcast_multiply_fusion
  140.1 0.9 slice_bitcast_fusion.226
  154.0 0.9 slice_bitcast_fusion.102
  155.5 0.9 slice_bitcast_fusion.106
  157.3 1.5 copy.2560
  158.7 1.6 copy.2558
  160.9 1.6 copy.2566
  162.5 1.6 copy.2564
  164.0 1.6 copy.2562
  165.6 1.4 copy.2561
  167.0 1.5 copy.2559
  168.6 1.3 pad_maximum_fusion.184
  169.9 2.1 %constant_dynamic-update-slice_fusion.33 = (f32[16,2,128,128]{3,2,1,0:T(8,128)}, f32[1,2,128,128]{3,2,1,0:T(8,128)S(1)}) fusion(f32[16,2,128,128]{3,2,1,0:T(8,128)} %get-tuple-element.105, f32[1,2,127,128]{3,2,1,0:T(8,128)} %copy.2566, f32[1,2,1,128]{3,2,1,0:T(1,128)} %bitcast.864, f32[1,2,1,128]{3,2,1,0:T(1,128)} %bitcast.863, ...), kind=kLoop, calls=%fused_computation.418 | loop fusion | flops 1245184 | bytes 1838080
  172.2 1.6 constant_dynamic-update-slice_fusion.32
  174.0 1.6 constant_dynamic-update-slice_fusion.31
  180.5 1.0 constant_dynamic-update-slice_fusion.26
  182.6 1.6 constant_dynamic-update-slice_fusion.24
  186.0 0.9 add_dynamic-update-slice_fusion
  187.1 2.1 %multiply_reduce_fusion.1 = (f32[16,2]{1,0:T(8,128)S(1)}, f32[16,2]{1,0:T(8,128)S(1)}) fusion(f32[16,2,128,128]{3,2,1,0:T(8,128)} %add_dynamic-update-slice_fusion, f32[128,128]{1,0:T(8,128)S(1)} %copy-done.11, f32[128,128]{1,0:T(8,128)S(1)} %copy-done.9), kind=kLoop, calls=%fused_computation.5 | loop fusion | flops 2097088 | bytes 2228480 | tf_op jit(solution)/shard_map/reduce_sum | solution.py:49
  192.9 5.8 %all-to-all-start.1 = ((f32[32,2,16]{2,1,0:T(2,128)}), f32[32,2,16]{2,1,0:T(2,128)S(1)}, u32[]{:S(2)}, u32[]{:S(2)}) async-start(f32[32,2,16]{2,1,0:T(2,128)} %tile.5), calls=%async_computation.1 | async-start | bytes 65536 | tf_op jit(solution)/shard_map/all_to_all | solution.py:176
  198.9 3.1 %fusion.45 = f32[2,128,128]{2,1,0:T(8,128)} fusion(f32[2,128,128]{2,0,1:T(2,128)} %get-tuple-element.560, f32[2,128,128]{2,0,1:T(2,128)} %get-tuple-element.78, f32[2,128,128]{2,1,0:T(8,128)S(1)} %multiply_add_fusion.21, f32[2,128,128]{2,1,0:T(8,128)S(1)} %copy_add_fusion, f32[2,128,128]{2,1,0:T(8,128)S(1)} %multiply_add_fusion.20, ...), kind=kLoop, calls=%fused_computation.306 | loop fusion | flops 3768320 | bytes 4325480 | tf_op jit(solution)/shard_map/add | solution.py:98
  202.0 4.0 %all-to-all-done.1 = f32[32,2,16]{2,1,0:T(2,128)S(1)} async-done(((f32[32,2,16]{2,1,0:T(2,128)}), f32[32,2,16]{2,1,0:T(2,128)S(1)}, u32[]{:S(2)}, u32[]{:S(2)}) %all-to-all-start.1) | async-done | bytes 4128 | tf_op jit(solution)/shard_map/all_to_all | solution.py:176
  (690 shorter events, 119.4 us)
Async XLA Ops:
  1.5 111.5 %copy-start.12 = (f32[127,128]{1,0:T(8,128)}, f32[127,128]{1,0:T(8,128)S(1)}, u32[]{:S(2)}) copy-start(f32[127,128]{1,0:T(8,128)S(1)} %get-tuple-element.557) | copy-start | bytes 195076
  1.5 111.6 %copy-start.16 = (f32[127,128]{1,0:T(8,128)}, f32[127,128]{1,0:T(8,128)S(1)}, u32[]{:S(2)}) copy-start(f32[127,128]{1,0:T(8,128)S(1)} %get-tuple-element.556) | copy-start | bytes 195076
  2.2 110.6 %copy-start.14 = (f32[128,127]{1,0:T(8,128)}, f32[128,127]{1,0:T(8,128)S(1)}, u32[]{:S(2)}) copy-start(f32[128,127]{1,0:T(8,128)S(1)} %get-tuple-element.559) | copy-start | bytes 195076
  2.2 110.7 %copy-start.18 = (f32[128,127]{1,0:T(8,128)}, f32[128,127]{1,0:T(8,128)S(1)}, u32[]{:S(2)}) copy-start(f32[128,127]{1,0:T(8,128)S(1)} %get-tuple-element.558) | copy-start | bytes 195076
  55.2 16.9 %copy-start.123 = (f32[1,2,127,128]{3,1,2,0:T(2,128)S(1)}, f32[1,2,127,128]{3,1,2,0:T(2,128)}, u32[]{:S(2)}) copy-start(f32[1,2,127,128]{3,1,2,0:T(2,128)} %get-tuple-element.430) | copy-start | bytes 390148
  56.0 16.8 %copy-start.122 = (f32[1,2,127,128]{3,1,2,0:T(2,128)S(1)}, f32[1,2,127,128]{3,1,2,0:T(2,128)}, u32[]{:S(2)}) copy-start(f32[1,2,127,128]{3,1,2,0:T(2,128)} %get-tuple-element.429) | copy-start | bytes 390148
  56.0 17.4 %copy-start.49 = (f32[1,2,128,127]{3,1,2,0:T(2,128)S(1)}, f32[1,2,128,127]{3,1,2,0:T(2,128)}, u32[]{:S(2)}) copy-start(f32[1,2,128,127]{3,1,2,0:T(2,128)} %get-tuple-element.426) | copy-start | bytes 390148
  56.0 12.0 %copy-start.124 = (f32[1,7,128,128]{3,2,1,0:T(8,128)S(1)}, f32[1,7,128,128]{3,2,1,0:T(8,128)}, u32[]{:S(2)}) copy-start(f32[1,7,128,128]{3,2,1,0:T(8,128)} %param.17) | copy-start | bytes 1376260
  56.2 14.3 %copy-start.139 = (f32[32]{0:T(128)}, f32[32]{0:T(128)S(1)}, u32[]{:S(2)}) copy-start(f32[32]{0:T(128)S(1)} %compare_convert_fusion) | copy-start | bytes 388
  70.4 6.2 %copy-start.6 = (f32[32,1024]{1,0:T(8,128)}, f32[32,1024]{1,0:T(8,128)S(1)}, u32[]{:S(2)}) copy-start(f32[32,1024]{1,0:T(8,128)S(1)} %constant_dynamic-update-slice_fusion.8) | copy-start | bytes 393220
  76.6 6.0 %copy-start.186 = (f32[128]{0:T(128)S(1)}, f32[128]{0:T(128)}, u32[]{:S(2)}) copy-start(f32[128]{0:T(128)} %get-tuple-element.588) | copy-start | bytes 1540
  82.0 14.6 %copy-start.20 = (f32[1,2,128,128]{3,2,1,0:T(8,128)S(1)}, f32[1,2,128,128]{3,2,1,0:T(8,128)}, u32[]{:S(2)}) copy-start(f32[1,2,128,128]{3,2,1,0:T(8,128)} %get-tuple-element.93) | copy-start | bytes 393220
  89.4 10.4 %copy-start.74 = (f32[1,2,127,128]{3,2,1,0:T(8,128)S(1)}, f32[1,2,127,128]{3,2,1,0:T(8,128)}, u32[]{:S(2)}) copy-start(f32[1,2,127,128]{3,2,1,0:T(8,128)} %get-tuple-element.370) | copy-start | bytes 390148
  89.4 10.4 %copy-start.75 = (f32[1,2,127,128]{3,2,1,0:T(8,128)S(1)}, f32[1,2,127,128]{3,2,1,0:T(8,128)}, u32[]{:S(2)}) copy-start(f32[1,2,127,128]{3,2,1,0:T(8,128)} %get-tuple-element.371) | copy-start | bytes 390148
  89.4 10.5 %copy-start.76 = (f32[1,2,128,127]{3,2,1,0:T(8,128)S(1)}, f32[1,2,128,127]{3,2,1,0:T(8,128)}, u32[]{:S(2)}) copy-start(f32[1,2,128,127]{3,2,1,0:T(8,128)} %get-tuple-element.362) | copy-start | bytes 390148
  89.4 10.5 %copy-start.77 = (f32[1,2,128,127]{3,2,1,0:T(8,128)S(1)}, f32[1,2,128,127]{3,2,1,0:T(8,128)}, u32[]{:S(2)}) copy-start(f32[1,2,128,127]{3,2,1,0:T(8,128)} %get-tuple-element.363) | copy-start | bytes 390148
  89.4 10.5 %copy-start.78 = (f32[1,2,128,1]{3,2,1,0:T(8,128)S(1)}, f32[1,2,128,1]{3,2,1,0:T(8,128)}, u32[]{:S(2)}) copy-start(f32[1,2,128,1]{3,2,1,0:T(8,128)} %get-tuple-element.366) | copy-start | bytes 3076
  89.4 10.5 %copy-start.79 = (f32[1,2,128,1]{3,2,1,0:T(8,128)S(1)}, f32[1,2,128,1]{3,2,1,0:T(8,128)}, u32[]{:S(2)}) copy-start(f32[1,2,128,1]{3,2,1,0:T(8,128)} %get-tuple-element.367) | copy-start | bytes 3076
  89.4 10.5 %copy-start.171 = (f32[1,2,1,128]{3,2,1,0:T(1,128)S(1)}, f32[1,2,1,128]{3,2,1,0:T(1,128)}, u32[]{:S(2)}) copy-start(f32[1,2,1,128]{3,2,1,0:T(1,128)} %get-tuple-element.374) | copy-start | bytes 3076
  89.4 10.5 %copy-start.172 = (f32[1,2,1,128]{3,2,1,0:T(1,128)S(1)}, f32[1,2,1,128]{3,2,1,0:T(1,128)}, u32[]{:S(2)}) copy-start(f32[1,2,1,128]{3,2,1,0:T(1,128)} %get-tuple-element.375) | copy-start | bytes 3076
  101.6 11.3 %copy-start.137 = (f32[128]{0:T(128)S(1)}, f32[128]{0:T(128)}, u32[]{:S(2)}) copy-start(f32[128]{0:T(128)} %get-tuple-element.34) | copy-start | bytes 1540
  101.6 11.4 %copy-start.193 = (f32[128]{0:T(128)S(1)}, f32[128]{0:T(128)}, u32[]{:S(2)}) copy-start(f32[128]{0:T(128)} %get-tuple-element.555) | copy-start | bytes 1540
  101.6 11.4 %copy-start.195 = (f32[128]{0:T(128)S(1)}, f32[128]{0:T(128)}, u32[]{:S(2)}) copy-start(f32[128]{0:T(128)} %get-tuple-element.554) | copy-start | bytes 1540
  104.6 28.7 %all-to-all-start = ((f32[32,2,48]{2,1,0:T(2,128)}), f32[32,2,48]{2,1,0:T(2,128)}, u32[]{:S(2)}, u32[]{:S(2)}) async-start(f32[32,2,48]{2,1,0:T(2,128)} %pad_maximum_fusion.234), calls=%async_computation | async-start | bytes 65536 | tf_op jit(solution)/shard_map/all_to_all | solution.py:166
  128.5 8.8 %copy-start.200 = (f32[128]{0:T(128)S(1)}, f32[128]{0:T(128)}, u32[]{:S(2)}) copy-start(f32[128]{0:T(128)} %copy-done.199) | copy-start | bytes 1540
  128.5 8.8 %copy-start.198 = (f32[128]{0:T(128)S(1)}, f32[128]{0:T(128)}, u32[]{:S(2)}) copy-start(f32[128]{0:T(128)} %copy-done.197) | copy-start | bytes 1540
  128.5 8.9 %copy-start.144 = (f32[128]{0:T(128)S(1)}, f32[128]{0:T(128)}, u32[]{:S(2)}) copy-start(f32[128]{0:T(128)} %copy-done.143) | copy-start | bytes 1540
  128.5 9.1 %copy-start.142 = (f32[128]{0:T(128)S(1)}, f32[128]{0:T(128)}, u32[]{:S(2)}) copy-start(f32[128]{0:T(128)} %copy-done.141) | copy-start | bytes 1540
  165.6 8.2 %copy-start.179 = (f32[1,2,1,128]{3,2,1,0:T(1,128)S(1)}, f32[1,2,1,128]{3,2,1,0:T(1,128)}, u32[]{:S(2)}) copy-start(f32[1,2,1,128]{3,2,1,0:T(1,128)} %get-tuple-element.265) | copy-start | bytes 3076
  186.9 11.8 %copy-start.21 = (f32[2,127,128]{2,1,0:T(8,128)S(1)}, f32[2,127,128]{2,1,0:T(8,128)}, u32[]{:S(2)}) copy-start(f32[2,127,128]{2,1,0:T(8,128)} %get-tuple-element.301) | copy-start | bytes 390148
  186.9 11.8 %copy-start.22 = (f32[2,127,128]{2,1,0:T(8,128)S(1)}, f32[2,127,128]{2,1,0:T(8,128)}, u32[]{:S(2)}) copy-start(f32[2,127,128]{2,1,0:T(8,128)} %get-tuple-element.304) | copy-start | bytes 390148
  186.9 11.8 %copy-start.23 = (f32[2,128,127]{2,1,0:T(8,128)S(1)}, f32[2,128,127]{2,1,0:T(8,128)}, u32[]{:S(2)}) copy-start(f32[2,128,127]{2,1,0:T(8,128)} %get-tuple-element.293) | copy-start | bytes 390148
  186.9 11.8 %copy-start.24 = (f32[2,128,127]{2,1,0:T(8,128)S(1)}, f32[2,128,127]{2,1,0:T(8,128)}, u32[]{:S(2)}) copy-start(f32[2,128,127]{2,1,0:T(8,128)} %get-tuple-element.296) | copy-start | bytes 390148
  187.0 11.8 %copy-start.129 = (f32[2,1,128]{2,1,0:T(1,128)S(1)}, f32[2,1,128]{2,1,0:T(1,128)}, u32[]{:S(2)}) copy-start(f32[2,1,128]{2,1,0:T(1,128)} %copy-done.128) | copy-start | bytes 3076
  187.0 11.8 %copy-start.131 = (f32[2,1,128]{2,1,0:T(1,128)S(1)}, f32[2,1,128]{2,1,0:T(1,128)}, u32[]{:S(2)}) copy-start(f32[2,1,128]{2,1,0:T(1,128)} %copy-done.130) | copy-start | bytes 3076
  187.0 11.8 %copy-start.147 = (f32[2,1,128]{2,1,0:T(1,128)S(1)}, f32[2,1,128]{2,1,0:T(1,128)}, u32[]{:S(2)}) copy-start(f32[2,1,128]{2,1,0:T(1,128)} %get-tuple-element.305) | copy-start | bytes 3076
  187.0 11.8 %copy-start.148 = (f32[2,1,128]{2,1,0:T(1,128)S(1)}, f32[2,1,128]{2,1,0:T(1,128)}, u32[]{:S(2)}) copy-start(f32[2,1,128]{2,1,0:T(1,128)} %get-tuple-element.308) | copy-start | bytes 3076
  187.0 11.8 %copy-start.149 = (f32[2,1,128]{2,1,0:T(1,128)S(1)}, f32[2,1,128]{2,1,0:T(1,128)}, u32[]{:S(2)}) copy-start(f32[2,1,128]{2,1,0:T(1,128)} %get-tuple-element.123) | copy-start | bytes 3076
  187.0 11.8 %copy-start.150 = (f32[2,1,128]{2,1,0:T(1,128)S(1)}, f32[2,1,128]{2,1,0:T(1,128)}, u32[]{:S(2)}) copy-start(f32[2,1,128]{2,1,0:T(1,128)} %get-tuple-element.124) | copy-start | bytes 3076
  187.0 11.8 %copy-start.155 = (f32[2,1,128]{2,1,0:T(1,128)S(1)}, f32[2,1,128]{2,1,0:T(1,128)}, u32[]{:S(2)}) copy-start(f32[2,1,128]{2,1,0:T(1,128)} %get-tuple-element.219) | copy-start | bytes 3076
  187.0 11.8 %copy-start.156 = (f32[2,1,128]{2,1,0:T(1,128)S(1)}, f32[2,1,128]{2,1,0:T(1,128)}, u32[]{:S(2)}) copy-start(f32[2,1,128]{2,1,0:T(1,128)} %get-tuple-element.220) | copy-start | bytes 3076
  187.0 11.8 %copy-start.187 = (f32[2]{0:T(128)S(1)}, f32[2]{0:T(128)}, u32[]{:S(2)}) copy-start(f32[2]{0:T(128)} %get-tuple-element.40) | copy-start | bytes 28
  187.0 11.8 %copy-start.188 = (f32[2]{0:T(128)S(1)}, f32[2]{0:T(128)}, u32[]{:S(2)}) copy-start(f32[2]{0:T(128)} %get-tuple-element.43) | copy-start | bytes 28
  187.1 11.8 %copy-start.189 = (f32[2]{0:T(128)S(1)}, f32[2]{0:T(128)}, u32[]{:S(2)}) copy-start(f32[2]{0:T(128)} %get-tuple-element.45) | copy-start | bytes 28
  187.1 11.8 %copy-start.190 = (f32[2]{0:T(128)S(1)}, f32[2]{0:T(128)}, u32[]{:S(2)}) copy-start(f32[2]{0:T(128)} %get-tuple-element.46) | copy-start | bytes 28
  192.9 13.0 %all-to-all-start.1 = ((f32[32,2,16]{2,1,0:T(2,128)}), f32[32,2,16]{2,1,0:T(2,128)S(1)}, u32[]{:S(2)}, u32[]{:S(2)}) async-start(f32[32,2,16]{2,1,0:T(2,128)} %tile.5), calls=%async_computation.1 | async-start | bytes 65536 | tf_op jit(solution)/shard_map/all_to_all | solution.py:176
  198.9 7.1 %copy-start.7 = (f32[32,1024]{1,0:T(8,128)S(1)}, f32[32,1024]{1,0:T(8,128)}, u32[]{:S(2)}) copy-start(f32[32,1024]{1,0:T(8,128)} %copy-done.6) | copy-start | bytes 393220
  198.9 7.1 %copy-start.140 = (f32[32]{0:T(128)S(1)}, f32[32]{0:T(128)}, u32[]{:S(2)}) copy-start(f32[32]{0:T(128)} %copy-done.139) | copy-start | bytes 388
  (157 other events, 514.1 us)

commit v3 on v1

--- a/solution.py
+++ b/solution.py
@@ -2,6 +2,8 @@
 import jax.numpy as jnp
 from jax import lax
 from jax.sharding import PartitionSpec as P
+from jax.experimental import pallas as pl
+from jax.experimental.pallas import tpu as pltpu
 
 NSUB = 8
 COUPLED = 2
@@ -56,6 +58,69 @@
         lift_rows.append(jnp.sum(vorticity * lift_kernel, axis=(1, 2)))
         drag_rows.append(jnp.sum(vorticity * drag_kernel, axis=(1, 2)))
     return (vorticity, jnp.stack(lift_rows + drag_rows, axis=1))
+
+
+def stencil_kernel(velocity_ref, vorticity_ref, flow_x_ref, flow_y_ref, source_x_ref, source_y_ref, lift_ref, drag_ref, out_ref, rows_ref, *, substeps):
+    strip = pl.program_id(0)
+    vorticity = vorticity_ref[0, 0]
+    flow_x = flow_x_ref[0, 0]
+    flow_y = flow_y_ref[0, 0]
+    rows_across, cols_across = vorticity.shape
+    lane = lax.broadcasted_iota(jnp.int32, (1, 2 * substeps), 1)
+    row = jnp.zeros((1, 2 * substeps), jnp.float32)
+    for substep in range(substeps):
+        right_cell = pltpu.roll(vorticity, cols_across - 1, 1)
+        left_cell = pltpu.roll(vorticity, 1, 1)
+        upper_cell = pltpu.roll(vorticity, rows_across - 1, 0)
+        lower_cell = pltpu.roll(vorticity, 1, 0)
+        laplacian = right_cell + left_cell + upper_cell + lower_cell - 4.0 * vorticity
+        tendency = (
+            VISCOSITY * laplacian
+            - flow_x * (0.5 * (right_cell - left_cell))
+            - flow_y * (0.5 * (upper_cell - lower_cell))
+        )
+        forcing = (
+            velocity_ref[strip, substep] * source_x_ref[...]
+            - velocity_ref[strip, substeps + substep] * source_y_ref[...]
+        )
+        vorticity = vorticity + TIME_STEP * tendency + COUPLING * forcing
+        lift = jnp.sum(jnp.sum(vorticity * lift_ref[...], axis=0, keepdims=True), axis=1, keepdims=True)
+        drag = jnp.sum(jnp.sum(vorticity * drag_ref[...], axis=0, keepdims=True), axis=1, keepdims=True)
+        row = row + jnp.where(lane == substep, lift, 0.0) + jnp.where(lane == substeps + substep, drag, 0.0)
+    out_ref[0] = vorticity
+    rows_ref[0] = row
+
+
+def strip_step_kernel(strip_fields, vorticity, motion, kernels, substeps):
+    source_x, source_y, lift_kernel, drag_kernel = kernels
+    strips, cells_y, cells_x = strip_fields.shape[1:]
+    halves = motion.reshape(strips, 2, substeps)
+    earlier = jnp.concatenate([jnp.zeros_like(halves[:, :, :1]), halves[:, :, :-1]], axis=2)
+    velocity = (halves - earlier).reshape(strips, 2 * substeps)
+    plane = pl.BlockSpec((cells_y, cells_x), lambda s: (0, 0))
+
+    def field(index):
+        return pl.BlockSpec((1, 1, cells_y, cells_x), lambda s: (index, s, 0, 0))
+
+    new_vorticity, rows = pl.pallas_call(
+        lambda *refs: stencil_kernel(*refs, substeps=substeps),
+        grid=(strips,),
+        in_specs=[
+            pl.BlockSpec(memory_space=pltpu.SMEM),
+            field(0), field(1), field(2),
+            plane, plane, plane, plane,
+        ],
+        out_specs=[
+            pl.BlockSpec((1, cells_y, cells_x), lambda s: (s, 0, 0)),
+            pl.BlockSpec((1, 1, 2 * substeps), lambda s: (s, 0, 0)),
+        ],
+        out_shape=[
+            jax.ShapeDtypeStruct((strips, cells_y, cells_x), jnp.float32),
+            jax.ShapeDtypeStruct((strips, 1, 2 * substeps), jnp.float32),
+        ],
+        name="strip_stencil",
+    )(velocity, vorticity, strip_fields, strip_fields, source_x, source_y, lift_kernel, drag_kernel)
+    return new_vorticity, rows[:, 0, :]
 
 
 def apply_block(vectors, matrix):
@@ -114,12 +179,10 @@
         jnp.arange(group_count)[:, None, None] == group_position, coupling[None], 0.0
     ).reshape(group_count * group_strips, group_strips)
 
-    vorticity = strip_fields[0]
-    flow_x = strip_fields[1]
-    flow_y = strip_fields[2]
+    vorticity = strip_fields
     motion = jnp.zeros((per_device, 2 * substeps), jnp.float32)
     for coupled_step in range(COUPLED):
-        vorticity, force_rows = strip_step(vorticity, flow_x, flow_y, motion, kernels, substeps)
+        vorticity, force_rows = strip_step_kernel(strip_fields, vorticity, motion, kernels, substeps)
         sent = jnp.tile(force_rows, (devices, 1))
         if coupled_step + 1 < COUPLED:
             sent = jnp.concatenate([sent, coupling_out], axis=1)
@@ -135,6 +198,7 @@
                 my_coupling, group_force, (((1,), (0,)), ((), ())), precision=EXACT_DOT
             )
             motion = motion.at[:, substeps:].add(local_taper[:, None] * offset[None, :])
+            vorticity = vorticity[None]
         else:
             displacement = first_contract(group_force * owned_here[:, None], unit_response)
             displacement = displacement.at[substeps:, :].add(offset[:, None] * top_taper[None, :])

time: 62.9 us -> 58.7 us (0.933)
  local copies, waits for them, and re-layouts: 21.4 us -> 5.11 us
  matrix products: 6.89 us -> 14.3 us
  Pallas kernels: 0 us -> 6.42 us
  other arithmetic: 7.09 us -> 5.16 us
    unnamed x53 -> x19, local copies, waits for them, and re-layouts: 12.5 us -> 2.71 us
    dot_general x30, matrix products: 6.44 us -> 13.9 us  [apply_block(): lax.dot_general(vectors, matrix, (((1,), (1,)), ((), ())), precision=EXAC...]
    pallas_call x0 -> x2, Pallas kernels: none -> 6.42 us  [strip_step_kernel(): pl.pallas_call(lambda *refs: stencil_kernel(*refs, substeps=substeps), gr...]
    slice x65 -> x0, local copies, waits for them, and re-layouts: 3.61 us -> none  [the longest x32 2.98 us: strip_step(): right_cell = jnp.roll(vorticity, -1, axis=2)]
    another operation x34 -> x0, local copies, waits for them, and re-layouts: 3.17 us -> none  [strip_step(): return (vorticity, jnp.stack(lift_rows + drag_rows, axis=1))]
    add x14 -> x0, other arithmetic: 2.5 us -> none  [strip_step(): vorticity = vorticity + TIME_STEP * tendency + COUPLING * forcing]
    reduce_sum x2 -> x0, other arithmetic: 2.09 us -> none  [strip_step(): drag_rows.append(jnp.sum(vorticity * drag_kernel, axis=(1, 2)))]
    reshape x1 -> x3, local copies, waits for them, and re-layouts: 0.08 us -> 1.33 us  [the longest x2 1.25 us: strip_step_kernel(): velocity = (halves - earlier).reshape(strips, 2 * substeps)]
where the time goes in v3:
time: 58.7 us; the launch traced here: 57.9 us
  waiting for transfers between devices  14.4 us (25%)
  matrix products  14.3 us (24%)
  starting transfers between devices  9.86 us (17%)
  Pallas kernels  6.42 us (11%)
  other arithmetic  5.16 us (9%)
  local copies, waits for them, and re-layouts  5.11 us (9%)
  between operations  2.63 us (4%)
    all_to_all x2, waiting for transfers between devices, local(): received = lax.all_to_all(sent, ('group', 'strip'), 0, 0, tiled=True)  14.4 us
    dot_general x30, matrix products, apply_block(): lax.dot_general(vectors, matrix, (((1,), (1,)), ((), ())), precision=EXAC...  13.9 us
    all_to_all x2, starting transfers between devices, local(): received = lax.all_to_all(sent, ('group', 'strip'), 0, 0, tiled=True)  9.86 us
    pallas_call x2, Pallas kernels, strip_step_kernel(): pl.pallas_call(lambda *refs: stencil_kernel(*refs, substeps=substeps), gr...  6.42 us
    unnamed x19, local copies, waits for them, and re-layouts  2.71 us
    reshape x2, local copies, waits for them, and re-layouts, strip_step_kernel(): velocity = (halves - earlier).reshape(strips, 2 * substeps)  1.25 us
  transfers between devices with their start and end apart: 2, of which 2 were waited for; matrix products, arithmetic and copies ran while one was open for 0% of the time, Pallas kernels for 0%

profile of v3, /device:TPU:0, one launch (start us, length us, event | category | flops | bytes accessed | tf_op | source)
XLA Modules:
  0.0 57.9 jit_solution(5739782752038007865)
XLA Ops:
  0.7 0.8 %select_reduce_fusion = s32[32]{0:T(128)S(1)} fusion(s32[4]{0:T(128)} %bitcast.172, s32[32]{0:T(128)} %bitcast.173), kind=kLoop, calls=%fused_computation.132 | loop fusion | flops 352 | bytes 272 | tf_op jit(solution)/shard_map/reduce_sum | solution.py:165
  1.5 0.7 %compare_select_fusion = f32[32,8,128]{2,0,1:T(8,128)S(1)} fusion(f32[32]{0:T(128)S(1)} %compare_convert_fusion, s32[8,128]{1,0:T(8,128)S(1)} %multiply_add_fusion, s32[32]{0:T(128)} %param.13), kind=kLoop, calls=%fused_computation.17 | loop fusion | flops 65536 | bytes 135424 | tf_op jit(solution)/shard_map/mul | solution.py:175
  2.2 1.0 %fusion.41 = f32[32,128]{1,0:T(8,128)S(1)} fusion(f32[1,8,128,128]{3,2,1,0:T(8,128)} %param.15, f32[32,8,128]{2,0,1:T(8,128)S(1)} %compare_select_fusion), kind=kOutput, calls=%fused_computation.59 | convolution fusion | flops 6291456 | bytes 98304 | tf_op jit(solution)/shard_map/dot_general | solution.py:127
  3.3 1.1 %convolution_subtract_fusion.13 = f32[32,128]{1,0:T(8,128)S(1)} fusion(f32[32,128]{1,0:T(8,128)S(1)} %fusion.41, f32[1,7,128,128]{3,2,1,0:T(8,128)} %param.16, f32[32,8,128]{2,0,1:T(8,128)S(1)} %compare_select_fusion), kind=kOutput, calls=%fused_computation.15 | convolution fusion | flops 6295552 | bytes 114688 | tf_op jit(solution)/shard_map/dot_general | solution.py:127
  4.4 1.0 %fusion.37 = f32[32,128]{1,0:T(8,128)S(1)} fusion(f32[32,128]{1,0:T(8,128)S(1)} %convolution_subtract_fusion.13, f32[1,8,128,128]{3,2,1,0:T(8,128)} %param.15), kind=kOutput, calls=%fused_computation.55 | convolution fusion | flops 6291456 | bytes 98304 | tf_op jit(solution)/shard_map/dot_general | solution.py:127
  5.4 1.1 %convolution_subtract_fusion.12 = f32[32,128]{1,0:T(8,128)S(1)} fusion(f32[32,128]{1,0:T(8,128)S(1)} %fusion.37, f32[1,7,128,128]{3,2,1,0:T(8,128)} %param.16, f32[32,8,128]{2,0,1:T(8,128)S(1)} %compare_select_fusion), kind=kOutput, calls=%fused_computation.14 | convolution fusion | flops 6295552 | bytes 114688 | tf_op jit(solution)/shard_map/dot_general | solution.py:127
  6.7 1.1 %convolution_subtract_fusion.11 = f32[32,128]{1,0:T(8,128)S(1)} fusion(f32[32,128]{1,0:T(8,128)S(1)} %fusion.32, f32[1,7,128,128]{3,2,1,0:T(8,128)} %param.16, f32[32,8,128]{2,0,1:T(8,128)S(1)} %compare_select_fusion), kind=kOutput, calls=%fused_computation.13 | convolution fusion | flops 6295552 | bytes 114688 | tf_op jit(solution)/shard_map/dot_general | solution.py:127
  8.0 1.1 %convolution_subtract_fusion.10 = f32[32,128]{1,0:T(8,128)S(1)} fusion(f32[32,128]{1,0:T(8,128)S(1)} %fusion.27, f32[1,7,128,128]{3,2,1,0:T(8,128)} %param.16, f32[32,8,128]{2,0,1:T(8,128)S(1)} %compare_select_fusion), kind=kOutput, calls=%fused_computation.12 | convolution fusion | flops 6295552 | bytes 114688 | tf_op jit(solution)/shard_map/dot_general | solution.py:127
  9.1 0.2 fusion.22
  9.3 1.1 %convolution_subtract_fusion.9 = f32[32,128]{1,0:T(8,128)S(1)} fusion(f32[32,128]{1,0:T(8,128)S(1)} %fusion.22, f32[1,7,128,128]{3,2,1,0:T(8,128)} %param.16, f32[32,8,128]{2,0,1:T(8,128)S(1)} %compare_select_fusion), kind=kOutput, calls=%fused_computation.11 | convolution fusion | flops 6295552 | bytes 114688 | tf_op jit(solution)/shard_map/dot_general | solution.py:127
  10.4 0.2 fusion.17
  10.6 1.1 %convolution_subtract_fusion.8 = f32[32,128]{1,0:T(8,128)S(1)} fusion(f32[32,128]{1,0:T(8,128)S(1)} %fusion.17, f32[1,7,128,128]{3,2,1,0:T(8,128)} %param.16, f32[32,8,128]{2,0,1:T(8,128)S(1)} %compare_select_fusion), kind=kOutput, calls=%fused_computation.10 | convolution fusion | flops 6295552 | bytes 114688 | tf_op jit(solution)/shard_map/dot_general | solution.py:127
  11.7 0.2 fusion.12
  11.9 1.1 %convolution_subtract_fusion.7 = f32[32,128]{1,0:T(8,128)S(1)} fusion(f32[32,128]{1,0:T(8,128)S(1)} %fusion.12, f32[1,7,128,128]{3,2,1,0:T(8,128)} %param.16, f32[32,8,128]{2,0,1:T(8,128)S(1)} %compare_select_fusion), kind=kOutput, calls=%fused_computation.9 | convolution fusion | flops 6295552 | bytes 114688 | tf_op jit(solution)/shard_map/dot_general | solution.py:127
  13.0 0.2 fusion.7
  13.4 0.2 fusion.10
  13.6 0.2 convolution_subtract_fusion.5
  13.8 0.2 fusion.15
  14.1 0.2 convolution_subtract_fusion.4
  14.3 0.2 fusion.20
  14.5 0.2 convolution_subtract_fusion.3
  14.7 0.2 fusion.25
  15.0 0.2 convolution_subtract_fusion.2
  15.2 0.2 fusion.30
  15.4 0.2 convolution_subtract_fusion.1
  15.6 0.2 fusion.35
  15.9 0.2 convolution_subtract_fusion
  16.1 0.2 convolution_dynamic-update-slice_fusion
  16.4 0.6 %copy-done.3 = s32[32]{0:T(128)S(1)} copy-done((s32[32]{0:T(128)S(1)}, s32[32]{0:T(128)}, u32[]{:S(2)}) %copy-start.3) | copy-done | bytes 152
  17.1 0.3 convolution_multiply_fusion
  17.5 0.7 %multiply_reduce_fusion = (f32[]{:T(128)}, f32[]{:T(128)}) fusion(f32[128]{0:T(128)S(1)} %get-tuple-element.42, f32[128]{0:T(128)S(1)} %get-tuple-element.43, f32[128]{0:T(128)S(1)} %fusion.94), kind=kLoop, calls=%fused_computation.77 | loop fusion | flops 147454 | bytes 1544 | tf_op jit(solution)/shard_map/reduce_sum | solution.py:31
  19.7 0.7 %fusion.62 = (f32[128,128]{1,0:T(8,128)}, f32[128,128]{1,0:T(8,128)}) fusion(f32[]{:T(128)S(6)} %sqrt.7, f32[128]{0:T(128)S(1)} %get-tuple-element.42, f32[128]{0:T(128)S(1)} %get-tuple-element.43, f32[]{:T(128)S(6)} %sqrt.6, f32[128]{0:T(128)S(1)} %fusion.94), kind=kLoop, calls=%fused_computation.83 | loop fusion | flops 114688 | bytes 132616 | tf_op jit(solution)/shard_map/div | solution.py:31
  20.5 0.7 %fusion.63 = (f32[128,128]{1,0:T(8,128)}, f32[128,128]{1,0:T(8,128)}) fusion(f32[128]{0:T(128)S(1)} %get-tuple-element.41, f32[128]{0:T(128)S(1)} %get-tuple-element.40), kind=kLoop, calls=%fused_computation.85 | loop fusion | flops 81920 | bytes 132096 | tf_op jit(solution)/shard_map/mul | solution.py:24
  21.2 0.6 reshape.217.refs_0_
  21.8 3.2 %strip_stencil.2 = (f32[2,128,128]{2,1,0:T(8,128)}, f32[2,1,16]{2,1,0:T(1,128)}) custom-call(f32[2,16]{1,0:T(2,128)} %reshape.217.refs_0_, f32[3,2,128,128]{3,2,1,0:T(8,128)} %refs_3_.3, f32[3,2,128,128]{3,2,1,0:T(8,128)} %refs_3_.3, f32[3,2,128,128]{3,2,1,0:T(8,128)} %refs_3_.3, f32[128,128]{1,0:T(8,128)} %get-tuple-element.37.refs_4_, ...), custom_call_target="tpu_custom_call" | custom-call | tf_op jit(solution)/shard_map/strip_stencil/pallas_call | solution.py:105
  25.0 0.7 %copy-done.5 = f32[2,1,16]{2,1,0:T(1,128)S(1)} copy-done((f32[2,1,16]{2,1,0:T(1,128)S(1)}, f32[2,1,16]{2,1,0:T(1,128)}, u32[]{:S(2)}) %copy-start.5) | copy-done | bytes 152
  25.7 0.7 %pad_maximum_fusion = f32[32,2,48]{2,1,0:T(2,128)} fusion(f32[32,2,32]{2,1,0:T(2,128)S(1)} %broadcast_select_fusion, f32[32,2,16]{2,1,0:T(2,128)S(1)} %tile.17), kind=kLoop, calls=%fused_computation.106 | loop fusion | flops 3072 | bytes 24576 | tf_op jit(solution)/shard_map/concatenate | solution.py:188
  26.4 7.3 %all-to-all-start = ((f32[32,2,48]{2,1,0:T(2,128)}), f32[32,2,48]{2,1,0:T(2,128)S(1)}, u32[]{:S(2)}, u32[]{:S(2)}) async-start(f32[32,2,48]{2,1,0:T(2,128)} %pad_maximum_fusion), calls=%async_computation | async-start | bytes 65536 | tf_op jit(solution)/shard_map/all_to_all | solution.py:189
  33.8 7.2 %all-to-all-done = f32[32,2,48]{2,1,0:T(2,128)S(1)} async-done(((f32[32,2,48]{2,1,0:T(2,128)}), f32[32,2,48]{2,1,0:T(2,128)S(1)}, u32[]{:S(2)}, u32[]{:S(2)}) %all-to-all-start) | async-done | bytes 12320 | tf_op jit(solution)/shard_map/all_to_all | solution.py:189
  41.4 0.2 scatter-add.6
  41.7 0.7 %reshape.220.refs_0_ = f32[2,16]{1,0:T(2,128)} reshape(f32[2,2,8]{2,1,0:T(2,128)S(1)} %pad_subtract_fusion) | data formatting | bytes 256 | tf_op jit(solution)/shard_map/reshape | solution.py:99
  42.4 3.2 %strip_stencil.3 = (f32[2,128,128]{2,1,0:T(8,128)}, f32[2,1,16]{2,1,0:T(1,128)}) custom-call(f32[2,16]{1,0:T(2,128)} %reshape.220.refs_0_, f32[1,2,128,128]{3,2,1,0:T(8,128)} %bitcast.168, f32[3,2,128,128]{3,2,1,0:T(8,128)} %refs_3_.3, f32[3,2,128,128]{3,2,1,0:T(8,128)} %refs_3_.3, f32[128,128]{1,0:T(8,128)} %get-tuple-element.37.refs_4_, ...), custom_call_target="tpu_custom_call" | custom-call | tf_op jit(solution)/shard_map/strip_stencil/pallas_call | solution.py:105
  45.6 0.7 %copy-done.4 = f32[2,1,16]{2,1,0:T(1,128)S(1)} copy-done((f32[2,1,16]{2,1,0:T(1,128)S(1)}, f32[2,1,16]{2,1,0:T(1,128)}, u32[]{:S(2)}) %copy-start.4) | copy-done | bytes 152
  46.3 0.6 %tile.19 = f32[32,2,16]{2,1,0:T(2,128)} broadcast(f32[2,16]{1,0:T(2,128)S(1)} %bitcast.170), dimensions={1,2} | broadcast | bytes 4224 | tf_op jit(solution)/shard_map/tile | solution.py:186
  46.9 2.6 %all-to-all-start.1 = ((f32[32,2,16]{2,1,0:T(2,128)}), f32[32,2,16]{2,1,0:T(2,128)S(1)}, u32[]{:S(2)}, u32[]{:S(2)}) async-start(f32[32,2,16]{2,1,0:T(2,128)} %tile.19), calls=%async_computation.1 | async-start | bytes 65536 | tf_op jit(solution)/shard_map/all_to_all | solution.py:189
  49.5 7.2 %all-to-all-done.1 = f32[32,2,16]{2,1,0:T(2,128)S(1)} async-done(((f32[32,2,16]{2,1,0:T(2,128)}), f32[32,2,16]{2,1,0:T(2,128)S(1)}, u32[]{:S(2)}, u32[]{:S(2)}) %all-to-all-start.1) | async-done | bytes 4128 | tf_op jit(solution)/shard_map/all_to_all | solution.py:189
  56.8 0.3 fusion.81
  57.3 0.6 %copy-done.2 = f32[1,16,1024]{2,1,0:T(8,128)} copy-done((f32[1,16,1024]{2,1,0:T(8,128)}, f32[1,16,1024]{2,1,0:T(8,128)S(1)}, u32[]{:S(2)}) %copy-start.2) | copy-done | bytes 65560
  (43 shorter events, 1.8 us)
Async XLA Ops:
  0.6 5.9 %copy-start = (f32[1,8,128,128]{3,2,1,0:T(8,128)S(1)}, f32[1,8,128,128]{3,2,1,0:T(8,128)}, u32[]{:S(2)}) copy-start(f32[1,8,128,128]{3,2,1,0:T(8,128)} %param.15) | copy-start | bytes 1572868
  7.8 5.4 %copy-start.1 = (f32[1,7,128,128]{3,2,1,0:T(8,128)S(1)}, f32[1,7,128,128]{3,2,1,0:T(8,128)}, u32[]{:S(2)}) copy-start(f32[1,7,128,128]{3,2,1,0:T(8,128)} %param.17) | copy-start | bytes 1376260
  16.4 0.7 %copy-start.3 = (s32[32]{0:T(128)S(1)}, s32[32]{0:T(128)}, u32[]{:S(2)}) copy-start(s32[32]{0:T(128)} %param.13) | copy-start | bytes 388
  25.0 0.7 %copy-start.5 = (f32[2,1,16]{2,1,0:T(1,128)S(1)}, f32[2,1,16]{2,1,0:T(1,128)}, u32[]{:S(2)}) copy-start(f32[2,1,16]{2,1,0:T(1,128)} %get-tuple-element.30) | copy-start | bytes 388
  26.4 14.6 %all-to-all-start = ((f32[32,2,48]{2,1,0:T(2,128)}), f32[32,2,48]{2,1,0:T(2,128)S(1)}, u32[]{:S(2)}, u32[]{:S(2)}) async-start(f32[32,2,48]{2,1,0:T(2,128)} %pad_maximum_fusion), calls=%async_computation | async-start | bytes 65536 | tf_op jit(solution)/shard_map/all_to_all | solution.py:189
  45.6 0.7 %copy-start.4 = (f32[2,1,16]{2,1,0:T(1,128)S(1)}, f32[2,1,16]{2,1,0:T(1,128)}, u32[]{:S(2)}) copy-start(f32[2,1,16]{2,1,0:T(1,128)} %get-tuple-element.33) | copy-start | bytes 388
  46.9 9.8 %all-to-all-start.1 = ((f32[32,2,16]{2,1,0:T(2,128)}), f32[32,2,16]{2,1,0:T(2,128)S(1)}, u32[]{:S(2)}, u32[]{:S(2)}) async-start(f32[32,2,16]{2,1,0:T(2,128)} %tile.19), calls=%async_computation.1 | async-start | bytes 65536 | tf_op jit(solution)/shard_map/all_to_all | solution.py:189
  57.3 0.6 %copy-start.2 = (f32[1,16,1024]{2,1,0:T(8,128)}, f32[1,16,1024]{2,1,0:T(8,128)S(1)}, u32[]{:S(2)}) copy-start(f32[1,16,1024]{2,1,0:T(8,128)S(1)} %fusion.80) | copy-start | bytes 196612

commit v4 on v3

--- a/solution.py
+++ b/solution.py
@@ -144,6 +144,39 @@
         remainder = carried[block_index] - apply_block(solved[0], upper_block[block_index])
         solved.insert(0, apply_block(remainder, pivot_inv[block_index]))
     return jnp.concatenate(solved, axis=1)
+
+
+def solve_kernel(load_ref, pivot_ref, lower_ref, upper_ref, out_ref):
+    block_count = pivot_ref.shape[1]
+    block_size = pivot_ref.shape[2]
+
+    def apply(vectors, matrix):
+        return lax.dot_general(
+            vectors, matrix, (((1,), (1,)), ((), ())),
+            precision=EXACT_DOT, preferred_element_type=jnp.float32,
+        )
+
+    carried = [load_ref[:, 0:block_size]]
+    for block_index in range(1, block_count):
+        pivoted = apply(carried[-1], pivot_ref[0, block_index - 1])
+        carried.append(
+            load_ref[:, block_index * block_size:(block_index + 1) * block_size]
+            - apply(pivoted, lower_ref[0, block_index - 1])
+        )
+    solved = apply(carried[-1], pivot_ref[0, block_count - 1])
+    out_ref[:, (block_count - 1) * block_size:] = solved
+    for block_index in range(block_count - 2, -1, -1):
+        remainder = carried[block_index] - apply(solved, upper_ref[0, block_index])
+        solved = apply(remainder, pivot_ref[0, block_index])
+        out_ref[:, block_index * block_size:(block_index + 1) * block_size] = solved
+
+
+def beam_solve_kernel(beam_load, pivot_inv, lower_block, upper_block):
+    return pl.pallas_call(
+        solve_kernel,
+        out_shape=jax.ShapeDtypeStruct(beam_load.shape, jnp.float32),
+        name="beam_solve",
+    )(beam_load, pivot_inv, lower_block, upper_block)
 
 
 def local(strip_fields, strip_riser, strip_node, riser_owner, pivot_inv, lower_block, upper_block):
@@ -171,8 +204,8 @@
     top_taper = 1.0 - jnp.arange(node_count, dtype=jnp.float32) / node_count
     local_taper = 1.0 - local_node.astype(jnp.float32) / node_count
 
-    unit_response = beam_solve(
-        node_onehot * owned_here[:, None], pivot_inv[0], lower_block[0], upper_block[0]
+    unit_response = beam_solve_kernel(
+        node_onehot * owned_here[:, None], pivot_inv, lower_block, upper_block
     )
     coupling = apply_block(node_onehot, unit_response) * owned_here[:, None]
     coupling_out = jnp.where(

time: 58.7 us -> 55.2 us (0.940)
  matrix products: 14.3 us -> 1.61 us
  Pallas kernels: 6.42 us -> 16.7 us
  other arithmetic: 5.16 us -> 4.42 us
    dot_general x30 -> x1, matrix products: 13.9 us -> 1.16 us  [apply_block(): lax.dot_general(vectors, matrix, (((1,), (1,)), ((), ())), precision=EXAC...]
    pallas_call x0 -> x1, Pallas kernels: none -> 10.3 us  [beam_solve_kernel(): pl.pallas_call(solve_kernel, out_shape=jax.ShapeDtypeStruct(beam_load.sha...]
    reduce_sum x1, other arithmetic: 0.8 us -> 0.08 us  [local(): owner_index = jnp.sum(riser_match * riser_owner[0][None, :], axis=1)]
    unnamed x19 -> x15, local copies, waits for them, and re-layouts: 2.71 us -> 3.28 us
where the time goes in v4:
time: 55.2 us; the launch traced here: 54.9 us
  Pallas kernels  16.7 us (30%)
  waiting for transfers between devices  14.4 us (26%)
  starting transfers between devices  9.86 us (18%)
  local copies, waits for them, and re-layouts  5.68 us (10%)
  other arithmetic  4.42 us (8%)
  between operations  2.15 us (4%)
  matrix products  1.61 us (3%)
    all_to_all x2, waiting for transfers between devices, local(): received = lax.all_to_all(sent, ('group', 'strip'), 0, 0, tiled=True)  14.4 us
    pallas_call x1, Pallas kernels, beam_solve_kernel(): pl.pallas_call(solve_kernel, out_shape=jax.ShapeDtypeStruct(beam_load.sha...  10.3 us
    all_to_all x2, starting transfers between devices, local(): received = lax.all_to_all(sent, ('group', 'strip'), 0, 0, tiled=True)  9.86 us
    pallas_call x2, Pallas kernels, strip_step_kernel(): pl.pallas_call(lambda *refs: stencil_kernel(*refs, substeps=substeps), gr...  6.45 us
    unnamed x15, local copies, waits for them, and re-layouts  3.28 us
    reshape x2, local copies, waits for them, and re-layouts, strip_step_kernel(): velocity = (halves - earlier).reshape(strips, 2 * substeps)  1.25 us
    dot_general x1, matrix products, apply_block(): lax.dot_general(vectors, matrix, (((1,), (1,)), ((), ())), precision=EXAC...  1.16 us
  transfers between devices with their start and end apart: 2, of which 2 were waited for; matrix products, arithmetic and copies ran while one was open for 0% of the time, Pallas kernels for 0%

profile of v4, /device:TPU:0, one launch (start us, length us, event | category | flops | bytes accessed | tf_op | source)
XLA Modules:
  0.0 54.9 jit_solution(16387348478263140848)
XLA Ops:
  0.7 0.0 copy-start.5
  0.7 0.0 copy-start.6
  0.7 0.6 %copy-done.5 = s32[1,4]{1,0:T(1,128)S(1)} copy-done((s32[1,4]{1,0:T(1,128)S(1)}, s32[1,4]{1,0:T(1,128)}, u32[]{:S(2)}) %copy-start.5) | copy-done | bytes 40
  1.3 0.0 copy-done.6
  1.3 0.1 select_reduce_fusion
  1.4 0.0 copy-start.2
  1.4 0.6 %copy-done.2 = s32[32]{0:T(128)S(1)} copy-done((s32[32]{0:T(128)S(1)}, s32[32]{0:T(128)}, u32[]{:S(2)}) %copy-start.2) | copy-done | bytes 152
  2.1 0.7 %fusion.load_ref = f32[32,1024]{1,0:T(8,128)} fusion(f32[32]{0:T(128)S(1)} %compare_convert_fusion, s32[32]{0:T(128)S(1)} %copy-done.2), kind=kLoop, calls=%fused_computation.2 | loop fusion | flops 65536 | bytes 131328 | tf_op jit(solution)/shard_map/mul | solution.py:208
  2.8 10.3 %beam_solve.1 = f32[32,1024]{1,0:T(8,128)} custom-call(f32[32,1024]{1,0:T(8,128)} %fusion.load_ref, f32[1,8,128,128]{3,2,1,0:T(8,128)} %pivot_ref.1, f32[1,7,128,128]{3,2,1,0:T(8,128)} %lower_ref.1, f32[1,7,128,128]{3,2,1,0:T(8,128)} %upper_ref.1), custom_call_target="tpu_custom_call" | custom-call | tf_op jit(solution)/shard_map/beam_solve/pallas_call | solution.py:175
  13.1 1.2 %convolution_multiply_fusion = f32[32,32]{1,0:T(8,128)S(1)} fusion(f32[32,1024]{1,0:T(8,128)} %beam_solve.1, s32[32]{0:T(128)S(1)} %copy-done.2, f32[32]{0:T(128)S(1)} %compare_convert_fusion), kind=kOutput, calls=%fused_computation | convolution fusion | flops 12616704 | bytes 135424 | tf_op jit(solution)/shard_map/dot_general | solution.py:127
  14.3 0.1 broadcast_in_dim.50
  14.4 0.1 broadcast_in_dim.51
  14.4 0.7 %multiply_reduce_fusion = (f32[]{:T(128)}, f32[]{:T(128)}) fusion(f32[128]{0:T(128)S(1)} %get-tuple-element.42, f32[128]{0:T(128)S(1)} %get-tuple-element.43, f32[128]{0:T(128)S(1)} %fusion.23), kind=kLoop, calls=%fused_computation.4 | loop fusion | flops 147454 | bytes 1544 | tf_op jit(solution)/shard_map/reduce_sum | solution.py:31
  16.5 0.1 broadcast_select_fusion
  16.6 0.7 %fusion.6 = (f32[128,128]{1,0:T(8,128)}, f32[128,128]{1,0:T(8,128)}) fusion(f32[128]{0:T(128)S(1)} %get-tuple-element.41, f32[128]{0:T(128)S(1)} %get-tuple-element.40), kind=kLoop, calls=%fused_computation.12 | loop fusion | flops 81920 | bytes 132096 | tf_op jit(solution)/shard_map/mul | solution.py:24
  17.4 0.7 %fusion.5 = (f32[128,128]{1,0:T(8,128)}, f32[128,128]{1,0:T(8,128)}) fusion(f32[]{:T(128)S(6)} %sqrt.7, f32[128]{0:T(128)S(1)} %get-tuple-element.42, f32[128]{0:T(128)S(1)} %get-tuple-element.43, f32[]{:T(128)S(6)} %sqrt.6, f32[128]{0:T(128)S(1)} %fusion.23), kind=kLoop, calls=%fused_computation.10 | loop fusion | flops 114688 | bytes 132616 | tf_op jit(solution)/shard_map/div | solution.py:31
  18.1 0.6 %reshape.154.refs_0_ = f32[2,16]{1,0:T(2,128)} broadcast(f32[]{:T(128)} %constant.91.clone.1), dimensions={} | broadcast | bytes 132 | tf_op jit(solution)/shard_map/reshape | solution.py:99
  18.7 3.2 %strip_stencil.2 = (f32[2,128,128]{2,1,0:T(8,128)}, f32[2,1,16]{2,1,0:T(1,128)}) custom-call(f32[2,16]{1,0:T(2,128)} %reshape.154.refs_0_, f32[3,2,128,128]{3,2,1,0:T(8,128)} %refs_3_.3, f32[3,2,128,128]{3,2,1,0:T(8,128)} %refs_3_.3, f32[3,2,128,128]{3,2,1,0:T(8,128)} %refs_3_.3, f32[128,128]{1,0:T(8,128)} %get-tuple-element.37.refs_4_, ...), custom_call_target="tpu_custom_call" | custom-call | tf_op jit(solution)/shard_map/strip_stencil/pallas_call | solution.py:105
  21.9 0.0 copy-start.4
  21.9 0.7 %copy-done.4 = f32[2,1,16]{2,1,0:T(1,128)S(1)} copy-done((f32[2,1,16]{2,1,0:T(1,128)S(1)}, f32[2,1,16]{2,1,0:T(1,128)}, u32[]{:S(2)}) %copy-start.4) | copy-done | bytes 152
  22.6 0.7 %pad_maximum_fusion = f32[32,2,48]{2,1,0:T(2,128)} fusion(f32[32,2,32]{2,1,0:T(2,128)S(1)} %broadcast_select_fusion, f32[32,2,16]{2,1,0:T(2,128)S(1)} %tile.17), kind=kLoop, calls=%fused_computation.19 | loop fusion | flops 3072 | bytes 24576 | tf_op jit(solution)/shard_map/concatenate | solution.py:221
  23.3 7.3 %all-to-all-start = ((f32[32,2,48]{2,1,0:T(2,128)}), f32[32,2,48]{2,1,0:T(2,128)S(1)}, u32[]{:S(2)}, u32[]{:S(2)}) async-start(f32[32,2,48]{2,1,0:T(2,128)} %pad_maximum_fusion), calls=%async_computation | async-start | bytes 65536 | tf_op jit(solution)/shard_map/all_to_all | solution.py:222
  30.6 0.1 multiply_subtract_fusion.1
  30.7 7.2 %all-to-all-done = f32[32,2,48]{2,1,0:T(2,128)S(1)} async-done(((f32[32,2,48]{2,1,0:T(2,128)}), f32[32,2,48]{2,1,0:T(2,128)S(1)}, u32[]{:S(2)}, u32[]{:S(2)}) %all-to-all-start) | async-done | bytes 12320 | tf_op jit(solution)/shard_map/all_to_all | solution.py:222
  37.9 0.1 slice.61
  37.9 0.1 slice_reduce_fusion.1
  38.1 0.1 fusion.13
  38.2 0.1 multiply_add_fusion
  38.3 0.2 scatter-add.6
  38.5 0.1 reshape.156
  38.6 0.1 pad_subtract_fusion
  38.6 0.7 %reshape.157.refs_0_ = f32[2,16]{1,0:T(2,128)} reshape(f32[2,2,8]{2,1,0:T(2,128)S(1)} %pad_subtract_fusion) | data formatting | bytes 256 | tf_op jit(solution)/shard_map/reshape | solution.py:99
  39.3 0.0 copy-start
  39.3 3.3 %strip_stencil.3 = (f32[2,128,128]{2,1,0:T(8,128)}, f32[2,1,16]{2,1,0:T(1,128)}) custom-call(f32[2,16]{1,0:T(2,128)} %reshape.157.refs_0_, f32[1,2,128,128]{3,2,1,0:T(8,128)} %bitcast.27, f32[3,2,128,128]{3,2,1,0:T(8,128)} %refs_3_.3, f32[3,2,128,128]{3,2,1,0:T(8,128)} %refs_3_.3, f32[128,128]{1,0:T(8,128)} %get-tuple-element.37.refs_4_, ...), custom_call_target="tpu_custom_call" | custom-call | tf_op jit(solution)/shard_map/strip_stencil/pallas_call | solution.py:105
  42.6 0.0 copy-start.3
  42.6 0.7 %copy-done.3 = f32[2,1,16]{2,1,0:T(1,128)S(1)} copy-done((f32[2,1,16]{2,1,0:T(1,128)S(1)}, f32[2,1,16]{2,1,0:T(1,128)}, u32[]{:S(2)}) %copy-start.3) | copy-done | bytes 152
  43.2 0.6 %tile.19 = f32[32,2,16]{2,1,0:T(2,128)} broadcast(f32[2,16]{1,0:T(2,128)S(1)} %bitcast.29), dimensions={1,2} | broadcast | bytes 4224 | tf_op jit(solution)/shard_map/tile | solution.py:219
  43.9 2.6 %all-to-all-start.1 = ((f32[32,2,16]{2,1,0:T(2,128)}), f32[32,2,16]{2,1,0:T(2,128)S(1)}, u32[]{:S(2)}, u32[]{:S(2)}) async-start(f32[32,2,16]{2,1,0:T(2,128)} %tile.19), calls=%async_computation.1 | async-start | bytes 65536 | tf_op jit(solution)/shard_map/all_to_all | solution.py:222
  46.5 7.2 %all-to-all-done.1 = f32[32,2,16]{2,1,0:T(2,128)S(1)} async-done(((f32[32,2,16]{2,1,0:T(2,128)}), f32[32,2,16]{2,1,0:T(2,128)S(1)}, u32[]{:S(2)}, u32[]{:S(2)}) %all-to-all-start.1) | async-done | bytes 4128 | tf_op jit(solution)/shard_map/all_to_all | solution.py:222
  53.7 0.0 copy-done
  53.7 0.3 fusion.10
  54.0 0.1 slice_reduce_fusion
  54.1 0.1 fusion.9
  54.2 0.0 copy-start.1
  54.2 0.6 %copy-done.1 = f32[1,16,1024]{2,1,0:T(8,128)} copy-done((f32[1,16,1024]{2,1,0:T(8,128)}, f32[1,16,1024]{2,1,0:T(8,128)S(1)}, u32[]{:S(2)}) %copy-start.1) | copy-done | bytes 65560
  (12 shorter events, 0.1 us)
Async XLA Ops:
  0.7 0.7 %copy-start.5 = (s32[1,4]{1,0:T(1,128)S(1)}, s32[1,4]{1,0:T(1,128)}, u32[]{:S(2)}) copy-start(s32[1,4]{1,0:T(1,128)} %param.14) | copy-start | bytes 52
  0.7 0.7 %copy-start.6 = (s32[32,1]{0,1:T(1,128)S(1)}, s32[32,1]{0,1:T(1,128)}, u32[]{:S(2)}) copy-start(s32[32,1]{0,1:T(1,128)} %param.12) | copy-start | bytes 388
  1.4 0.7 %copy-start.2 = (s32[32]{0:T(128)S(1)}, s32[32]{0:T(128)}, u32[]{:S(2)}) copy-start(s32[32]{0:T(128)} %param.13) | copy-start | bytes 388
  21.9 0.7 %copy-start.4 = (f32[2,1,16]{2,1,0:T(1,128)S(1)}, f32[2,1,16]{2,1,0:T(1,128)}, u32[]{:S(2)}) copy-start(f32[2,1,16]{2,1,0:T(1,128)} %get-tuple-element.30) | copy-start | bytes 388
  23.3 14.6 %all-to-all-start = ((f32[32,2,48]{2,1,0:T(2,128)}), f32[32,2,48]{2,1,0:T(2,128)S(1)}, u32[]{:S(2)}, u32[]{:S(2)}) async-start(f32[32,2,48]{2,1,0:T(2,128)} %pad_maximum_fusion), calls=%async_computation | async-start | bytes 65536 | tf_op jit(solution)/shard_map/all_to_all | solution.py:222
  39.3 14.4 %copy-start = (f32[32,1024]{1,0:T(8,128)S(1)}, f32[32,1024]{1,0:T(8,128)}, u32[]{:S(2)}) copy-start(f32[32,1024]{1,0:T(8,128)} %beam_solve.1) | copy-start | bytes 393220
  42.6 0.7 %copy-start.3 = (f32[2,1,16]{2,1,0:T(1,128)S(1)}, f32[2,1,16]{2,1,0:T(1,128)}, u32[]{:S(2)}) copy-start(f32[2,1,16]{2,1,0:T(1,128)} %get-tuple-element.33) | copy-start | bytes 388
  43.9 9.8 %all-to-all-start.1 = ((f32[32,2,16]{2,1,0:T(2,128)}), f32[32,2,16]{2,1,0:T(2,128)S(1)}, u32[]{:S(2)}, u32[]{:S(2)}) async-start(f32[32,2,16]{2,1,0:T(2,128)} %tile.19), calls=%async_computation.1 | async-start | bytes 65536 | tf_op jit(solution)/shard_map/all_to_all | solution.py:222
  54.2 0.6 %copy-start.1 = (f32[1,16,1024]{2,1,0:T(8,128)}, f32[1,16,1024]{2,1,0:T(8,128)S(1)}, u32[]{:S(2)}) copy-start(f32[1,16,1024]{2,1,0:T(8,128)S(1)} %fusion.9) | copy-start | bytes 196612

commit v5 on v3

--- a/solution.py
+++ b/solution.py
@@ -144,6 +144,36 @@
         remainder = carried[block_index] - apply_block(solved[0], upper_block[block_index])
         solved.insert(0, apply_block(remainder, pivot_inv[block_index]))
     return jnp.concatenate(solved, axis=1)
+
+
+def solve_kernel(load_ref, pivot_ref, lower_ref, upper_ref, out_ref):
+    block_count = pivot_ref.shape[1]
+    block_size = pivot_ref.shape[2]
+
+    def apply(matrix, vectors):
+        return jnp.dot(matrix, vectors, precision=EXACT_DOT, preferred_element_type=jnp.float32)
+
+    carried = [load_ref[0:block_size, :]]
+    for block_index in range(1, block_count):
+        pivoted = apply(pivot_ref[0, block_index - 1], carried[-1])
+        carried.append(
+            load_ref[block_index * block_size:(block_index + 1) * block_size, :]
+            - apply(lower_ref[0, block_index - 1], pivoted)
+        )
+    solved = apply(pivot_ref[0, block_count - 1], carried[-1])
+    out_ref[(block_count - 1) * block_size:, :] = solved
+    for block_index in range(block_count - 2, -1, -1):
+        remainder = carried[block_index] - apply(upper_ref[0, block_index], solved)
+        solved = apply(pivot_ref[0, block_index], remainder)
+        out_ref[block_index * block_size:(block_index + 1) * block_size, :] = solved
+
+
+def beam_solve_kernel(load_t, pivot_inv, lower_block, upper_block):
+    return pl.pallas_call(
+        solve_kernel,
+        out_shape=jax.ShapeDtypeStruct(load_t.shape, jnp.float32),
+        name="beam_solve",
+    )(load_t, pivot_inv, lower_block, upper_block)
 
 
 def local(strip_fields, strip_riser, strip_node, riser_owner, pivot_inv, lower_block, upper_block):
@@ -171,10 +201,10 @@
     top_taper = 1.0 - jnp.arange(node_count, dtype=jnp.float32) / node_count
     local_taper = 1.0 - local_node.astype(jnp.float32) / node_count
 
-    unit_response = beam_solve(
-        node_onehot * owned_here[:, None], pivot_inv[0], lower_block[0], upper_block[0]
+    unit_response = beam_solve_kernel(
+        node_onehot.T * owned_here[None, :], pivot_inv, lower_block, upper_block
     )
-    coupling = apply_block(node_onehot, unit_response) * owned_here[:, None]
+    coupling = jnp.dot(node_onehot, unit_response, precision=EXACT_DOT) * owned_here[:, None]
     coupling_out = jnp.where(
         jnp.arange(group_count)[:, None, None] == group_position, coupling[None], 0.0
     ).reshape(group_count * group_strips, group_strips)
@@ -200,7 +230,9 @@
             motion = motion.at[:, substeps:].add(local_taper[:, None] * offset[None, :])
             vorticity = vorticity[None]
         else:
-            displacement = first_contract(group_force * owned_here[:, None], unit_response)
+            displacement = lax.dot_general(
+                group_force * owned_here[:, None], unit_response, (((0,), (1,)), ((), ())), precision=EXACT_DOT
+            )
             displacement = displacement.at[substeps:, :].add(offset[:, None] * top_taper[None, :])
     return (vorticity, displacement[None])
 

time: 58.7 us -> 54.2 us (0.923)
  matrix products: 14.3 us -> 2.09 us
  Pallas kernels: 6.42 us -> 15.1 us
    dot_general x31 -> x2, matrix products: 14.2 us -> 1.96 us  [the longest x1 1.36 us: local(): jnp.dot(node_onehot, unit_response, precision=EXACT_DOT)]
    pallas_call x0 -> x1, Pallas kernels: none -> 8.58 us  [beam_solve_kernel(): pl.pallas_call(solve_kernel, out_shape=jax.ShapeDtypeStruct(load_t.shape,...]
    reduce_sum x1, other arithmetic: 0.8 us -> 0.08 us  [local(): owner_index = jnp.sum(riser_match * riser_owner[0][None, :], axis=1)]
    unnamed x19 -> x15, local copies, waits for them, and re-layouts: 2.71 us -> 3.26 us
where the time goes in v5:
time: 54.2 us; the launch traced here: 53.8 us
  Pallas kernels  15.1 us (28%)
  waiting for transfers between devices  14.4 us (27%)
  starting transfers between devices  9.86 us (18%)
  local copies, waits for them, and re-layouts  5.64 us (10%)
  other arithmetic  4.59 us (8%)
  between operations  2.15 us (4%)
  matrix products  2.09 us (4%)
    all_to_all x2, waiting for transfers between devices, local(): received = lax.all_to_all(sent, ('group', 'strip'), 0, 0, tiled=True)  14.4 us
    all_to_all x2, starting transfers between devices, local(): received = lax.all_to_all(sent, ('group', 'strip'), 0, 0, tiled=True)  9.86 us
    pallas_call x1, Pallas kernels, beam_solve_kernel(): pl.pallas_call(solve_kernel, out_shape=jax.ShapeDtypeStruct(load_t.shape,...  8.58 us
    pallas_call x2, Pallas kernels, strip_step_kernel(): pl.pallas_call(lambda *refs: stencil_kernel(*refs, substeps=substeps), gr...  6.48 us
    unnamed x15, local copies, waits for them, and re-layouts  3.26 us
    dot_general x1, matrix products, local(): jnp.dot(node_onehot, unit_response, precision=EXACT_DOT)  1.36 us
    reshape x2, local copies, waits for them, and re-layouts, strip_step_kernel(): velocity = (halves - earlier).reshape(strips, 2 * substeps)  1.23 us
  transfers between devices with their start and end apart: 2, of which 2 were waited for; matrix products, arithmetic and copies ran while one was open for 0% of the time, Pallas kernels for 0%

profile of v5, /device:TPU:0, one launch (start us, length us, event | category | flops | bytes accessed | tf_op | source)
XLA Modules:
  0.0 53.8 jit_solution(13953163822158920927)
XLA Ops:
  0.7 0.0 copy-start.5
  0.7 0.0 copy-start.6
  0.7 0.6 %copy-done.5 = s32[1,4]{1,0:T(1,128)S(1)} copy-done((s32[1,4]{1,0:T(1,128)S(1)}, s32[1,4]{1,0:T(1,128)}, u32[]{:S(2)}) %copy-start.5) | copy-done | bytes 40
  1.3 0.0 copy-done.6
  1.3 0.1 select_reduce_fusion
  1.4 0.0 copy-start.2
  1.4 0.6 %copy-done.2 = s32[32]{0:T(128)S(1)} copy-done((s32[32]{0:T(128)S(1)}, s32[32]{0:T(128)}, u32[]{:S(2)}) %copy-start.2) | copy-done | bytes 152
  2.1 0.9 %fusion.load_ref = f32[1024,32]{1,0:T(8,128)} fusion(f32[32]{0:T(128)S(1)} %compare_convert_fusion, s32[32]{0:T(128)S(1)} %copy-done.2), kind=kLoop, calls=%fused_computation.2 | loop fusion | flops 65536 | bytes 131328 | tf_op jit(solution)/shard_map/mul | solution.py:205
  3.0 8.6 %beam_solve.1 = f32[1024,32]{1,0:T(8,128)} custom-call(f32[1024,32]{1,0:T(8,128)} %fusion.load_ref, f32[1,8,128,128]{3,2,1,0:T(8,128)} %pivot_ref.1, f32[1,7,128,128]{3,2,1,0:T(8,128)} %lower_ref.1, f32[1,7,128,128]{3,2,1,0:T(8,128)} %upper_ref.1), custom_call_target="tpu_custom_call" | custom-call | tf_op jit(solution)/shard_map/beam_solve/pallas_call | solution.py:172
  11.5 1.4 %convolution_multiply_fusion = f32[32,32]{1,0:T(8,128)S(1)} fusion(f32[1024,32]{1,0:T(8,128)} %beam_solve.1, s32[32]{0:T(128)S(1)} %copy-done.2, f32[32]{0:T(128)S(1)} %compare_convert_fusion), kind=kOutput, calls=%fused_computation | convolution fusion | flops 12616704 | bytes 135424 | tf_op jit(solution)/shard_map/dot_general | solution.py:207
  12.9 0.1 broadcast_in_dim.50
  13.0 0.1 broadcast_in_dim.51
  13.1 0.7 %multiply_reduce_fusion = (f32[]{:T(128)}, f32[]{:T(128)}) fusion(f32[128]{0:T(128)S(1)} %get-tuple-element.42, f32[128]{0:T(128)S(1)} %get-tuple-element.43, f32[128]{0:T(128)S(1)} %fusion.23), kind=kLoop, calls=%fused_computation.5 | loop fusion | flops 147454 | bytes 1544 | tf_op jit(solution)/shard_map/reduce_sum | solution.py:31
  15.2 0.1 broadcast_select_fusion
  15.3 0.7 %fusion.6 = (f32[128,128]{1,0:T(8,128)}, f32[128,128]{1,0:T(8,128)}) fusion(f32[128]{0:T(128)S(1)} %get-tuple-element.41, f32[128]{0:T(128)S(1)} %get-tuple-element.40), kind=kLoop, calls=%fused_computation.13 | loop fusion | flops 81920 | bytes 132096 | tf_op jit(solution)/shard_map/mul | solution.py:24
  16.0 0.8 %fusion.5 = (f32[128,128]{1,0:T(8,128)}, f32[128,128]{1,0:T(8,128)}) fusion(f32[]{:T(128)S(6)} %sqrt.7, f32[128]{0:T(128)S(1)} %get-tuple-element.42, f32[128]{0:T(128)S(1)} %get-tuple-element.43, f32[]{:T(128)S(6)} %sqrt.6, f32[128]{0:T(128)S(1)} %fusion.23), kind=kLoop, calls=%fused_computation.11 | loop fusion | flops 114688 | bytes 132616 | tf_op jit(solution)/shard_map/div | solution.py:31
  16.8 0.6 %reshape.158.refs_0_ = f32[2,16]{1,0:T(2,128)} broadcast(f32[]{:T(128)} %constant.91.clone.1), dimensions={} | broadcast | bytes 132 | tf_op jit(solution)/shard_map/reshape | solution.py:99
  17.3 3.2 %strip_stencil.2 = (f32[2,128,128]{2,1,0:T(8,128)}, f32[2,1,16]{2,1,0:T(1,128)}) custom-call(f32[2,16]{1,0:T(2,128)} %reshape.158.refs_0_, f32[3,2,128,128]{3,2,1,0:T(8,128)} %refs_3_.3, f32[3,2,128,128]{3,2,1,0:T(8,128)} %refs_3_.3, f32[3,2,128,128]{3,2,1,0:T(8,128)} %refs_3_.3, f32[128,128]{1,0:T(8,128)} %get-tuple-element.37.refs_4_, ...), custom_call_target="tpu_custom_call" | custom-call | tf_op jit(solution)/shard_map/strip_stencil/pallas_call | solution.py:105
  20.5 0.0 copy-start.4
  20.5 0.7 %copy-done.4 = f32[2,1,16]{2,1,0:T(1,128)S(1)} copy-done((f32[2,1,16]{2,1,0:T(1,128)S(1)}, f32[2,1,16]{2,1,0:T(1,128)}, u32[]{:S(2)}) %copy-start.4) | copy-done | bytes 152
  21.2 0.7 %pad_maximum_fusion = f32[32,2,48]{2,1,0:T(2,128)} fusion(f32[32,2,32]{2,1,0:T(2,128)S(1)} %broadcast_select_fusion, f32[32,2,16]{2,1,0:T(2,128)S(1)} %tile.17), kind=kLoop, calls=%fused_computation.20 | loop fusion | flops 3072 | bytes 24576 | tf_op jit(solution)/shard_map/concatenate | solution.py:218
  21.9 7.3 %all-to-all-start = ((f32[32,2,48]{2,1,0:T(2,128)}), f32[32,2,48]{2,1,0:T(2,128)S(1)}, u32[]{:S(2)}, u32[]{:S(2)}) async-start(f32[32,2,48]{2,1,0:T(2,128)} %pad_maximum_fusion), calls=%async_computation | async-start | bytes 65536 | tf_op jit(solution)/shard_map/all_to_all | solution.py:219
  29.2 0.1 multiply_subtract_fusion.1
  29.3 7.2 %all-to-all-done = f32[32,2,48]{2,1,0:T(2,128)S(1)} async-done(((f32[32,2,48]{2,1,0:T(2,128)}), f32[32,2,48]{2,1,0:T(2,128)S(1)}, u32[]{:S(2)}, u32[]{:S(2)}) %all-to-all-start) | async-done | bytes 12320 | tf_op jit(solution)/shard_map/all_to_all | solution.py:219
  36.5 0.1 slice.61
  36.6 0.1 slice_reduce_fusion.1
  36.7 0.1 fusion.13
  36.8 0.1 multiply_add_fusion
  36.9 0.2 scatter-add.6
  37.1 0.1 reshape.160
  37.2 0.1 pad_subtract_fusion
  37.3 0.7 %reshape.161.refs_0_ = f32[2,16]{1,0:T(2,128)} reshape(f32[2,2,8]{2,1,0:T(2,128)S(1)} %pad_subtract_fusion) | data formatting | bytes 256 | tf_op jit(solution)/shard_map/reshape | solution.py:99
  37.9 0.0 copy-start
  37.9 3.3 %strip_stencil.3 = (f32[2,128,128]{2,1,0:T(8,128)}, f32[2,1,16]{2,1,0:T(1,128)}) custom-call(f32[2,16]{1,0:T(2,128)} %reshape.161.refs_0_, f32[1,2,128,128]{3,2,1,0:T(8,128)} %bitcast.27, f32[3,2,128,128]{3,2,1,0:T(8,128)} %refs_3_.3, f32[3,2,128,128]{3,2,1,0:T(8,128)} %refs_3_.3, f32[128,128]{1,0:T(8,128)} %get-tuple-element.37.refs_4_, ...), custom_call_target="tpu_custom_call" | custom-call | tf_op jit(solution)/shard_map/strip_stencil/pallas_call | solution.py:105
  41.2 0.0 copy-start.3
  41.2 0.7 %copy-done.3 = f32[2,1,16]{2,1,0:T(1,128)S(1)} copy-done((f32[2,1,16]{2,1,0:T(1,128)S(1)}, f32[2,1,16]{2,1,0:T(1,128)}, u32[]{:S(2)}) %copy-start.3) | copy-done | bytes 152
  41.9 0.6 %tile.19 = f32[32,2,16]{2,1,0:T(2,128)} broadcast(f32[2,16]{1,0:T(2,128)S(1)} %bitcast.29), dimensions={1,2} | broadcast | bytes 4224 | tf_op jit(solution)/shard_map/tile | solution.py:216
  42.5 2.6 %all-to-all-start.1 = ((f32[32,2,16]{2,1,0:T(2,128)}), f32[32,2,16]{2,1,0:T(2,128)S(1)}, u32[]{:S(2)}, u32[]{:S(2)}) async-start(f32[32,2,16]{2,1,0:T(2,128)} %tile.19), calls=%async_computation.1 | async-start | bytes 65536 | tf_op jit(solution)/shard_map/all_to_all | solution.py:219
  45.1 7.2 %all-to-all-done.1 = f32[32,2,16]{2,1,0:T(2,128)S(1)} async-done(((f32[32,2,16]{2,1,0:T(2,128)}), f32[32,2,16]{2,1,0:T(2,128)S(1)}, u32[]{:S(2)}, u32[]{:S(2)}) %all-to-all-start.1) | async-done | bytes 4128 | tf_op jit(solution)/shard_map/all_to_all | solution.py:219
  52.3 0.0 copy-done
  52.3 0.6 %fusion.10 = f32[16,1024]{1,0:T(8,128)S(1)} fusion(f32[1024,32]{1,0:T(8,128)S(1)} %copy-done, f32[64,16]{1,0:T(8,128)S(1)} %bitcast.23, s32[]{:T(128)S(6)} %select_n.14, f32[32]{0:T(128)S(1)} %compare_convert_fusion), kind=kOutput, calls=%fused_computation.22 | convolution fusion | flops 6291968 | bytes 606724 | tf_op jit(solution)/shard_map/dot_general | solution.py:233
  52.9 0.1 slice_reduce_fusion
  53.1 0.1 fusion.9
  53.2 0.0 copy-start.1
  53.2 0.6 %copy-done.1 = f32[1,16,1024]{2,1,0:T(8,128)} copy-done((f32[1,16,1024]{2,1,0:T(8,128)}, f32[1,16,1024]{2,1,0:T(8,128)S(1)}, u32[]{:S(2)}) %copy-start.1) | copy-done | bytes 65560
  (12 shorter events, 0.1 us)
Async XLA Ops:
  0.7 0.7 %copy-start.5 = (s32[1,4]{1,0:T(1,128)S(1)}, s32[1,4]{1,0:T(1,128)}, u32[]{:S(2)}) copy-start(s32[1,4]{1,0:T(1,128)} %param.14) | copy-start | bytes 52
  0.7 0.7 %copy-start.6 = (s32[32,1]{0,1:T(1,128)S(1)}, s32[32,1]{0,1:T(1,128)}, u32[]{:S(2)}) copy-start(s32[32,1]{0,1:T(1,128)} %param.12) | copy-start | bytes 388
  1.4 0.7 %copy-start.2 = (s32[32]{0:T(128)S(1)}, s32[32]{0:T(128)}, u32[]{:S(2)}) copy-start(s32[32]{0:T(128)} %param.13) | copy-start | bytes 388
  20.5 0.7 %copy-start.4 = (f32[2,1,16]{2,1,0:T(1,128)S(1)}, f32[2,1,16]{2,1,0:T(1,128)}, u32[]{:S(2)}) copy-start(f32[2,1,16]{2,1,0:T(1,128)} %get-tuple-element.30) | copy-start | bytes 388
  21.9 14.6 %all-to-all-start = ((f32[32,2,48]{2,1,0:T(2,128)}), f32[32,2,48]{2,1,0:T(2,128)S(1)}, u32[]{:S(2)}, u32[]{:S(2)}) async-start(f32[32,2,48]{2,1,0:T(2,128)} %pad_maximum_fusion), calls=%async_computation | async-start | bytes 65536 | tf_op jit(solution)/shard_map/all_to_all | solution.py:219
  37.9 14.4 %copy-start = (f32[1024,32]{1,0:T(8,128)S(1)}, f32[1024,32]{1,0:T(8,128)}, u32[]{:S(2)}) copy-start(f32[1024,32]{1,0:T(8,128)} %beam_solve.1) | copy-start | bytes 393220
  41.2 0.7 %copy-start.3 = (f32[2,1,16]{2,1,0:T(1,128)S(1)}, f32[2,1,16]{2,1,0:T(1,128)}, u32[]{:S(2)}) copy-start(f32[2,1,16]{2,1,0:T(1,128)} %get-tuple-element.33) | copy-start | bytes 388
  42.5 9.8 %all-to-all-start.1 = ((f32[32,2,16]{2,1,0:T(2,128)}), f32[32,2,16]{2,1,0:T(2,128)S(1)}, u32[]{:S(2)}, u32[]{:S(2)}) async-start(f32[32,2,16]{2,1,0:T(2,128)} %tile.19), calls=%async_computation.1 | async-start | bytes 65536 | tf_op jit(solution)/shard_map/all_to_all | solution.py:219
  53.2 0.6 %copy-start.1 = (f32[1,16,1024]{2,1,0:T(8,128)}, f32[1,16,1024]{2,1,0:T(8,128)S(1)}, u32[]{:S(2)}) copy-start(f32[1,16,1024]{2,1,0:T(8,128)S(1)} %fusion.9) | copy-start | bytes 196612

commit v6 on v5

--- a/solution.py
+++ b/solution.py
@@ -151,7 +151,7 @@
     block_size = pivot_ref.shape[2]
 
     def apply(matrix, vectors):
-        return jnp.dot(matrix, vectors, precision=EXACT_DOT, preferred_element_type=jnp.float32)
+        return jnp.dot(matrix, vectors, precision=lax.Precision.HIGH, preferred_element_type=jnp.float32)
 
     carried = [load_ref[0:block_size, :]]
     for block_index in range(1, block_count):

time: 54.2 us -> 52.8 us (0.974)
  Pallas kernels: 15.1 us -> 13.6 us
    pallas_call x1, Pallas kernels: 8.58 us -> 7.13 us  [beam_solve_kernel(): pl.pallas_call(solve_kernel, out_shape=jax.ShapeDtypeStruct(load_t.shape,...]
where the time goes in v6:
time: 52.8 us; the launch traced here: 52.3 us
  waiting for transfers between devices  14.4 us (27%)
  Pallas kernels  13.6 us (26%)
  starting transfers between devices  9.87 us (19%)
  local copies, waits for them, and re-layouts  5.64 us (11%)
  other arithmetic  4.59 us (9%)
  between operations  2.15 us (4%)
  matrix products  2.09 us (4%)
    all_to_all x2, waiting for transfers between devices, local(): received = lax.all_to_all(sent, ('group', 'strip'), 0, 0, tiled=True)  14.4 us
    all_to_all x2, starting transfers between devices, local(): received = lax.all_to_all(sent, ('group', 'strip'), 0, 0, tiled=True)  9.87 us
    pallas_call x1, Pallas kernels, beam_solve_kernel(): pl.pallas_call(solve_kernel, out_shape=jax.ShapeDtypeStruct(load_t.shape,...  7.13 us
    pallas_call x2, Pallas kernels, strip_step_kernel(): pl.pallas_call(lambda *refs: stencil_kernel(*refs, substeps=substeps), gr...  6.48 us
    unnamed x15, local copies, waits for them, and re-layouts  3.26 us
    dot_general x1, matrix products, local(): jnp.dot(node_onehot, unit_response, precision=EXACT_DOT)  1.36 us
    reshape x2, local copies, waits for them, and re-layouts, strip_step_kernel(): velocity = (halves - earlier).reshape(strips, 2 * substeps)  1.23 us
  transfers between devices with their start and end apart: 2, of which 2 were waited for; matrix products, arithmetic and copies ran while one was open for 0% of the time, Pallas kernels for 0%

profile of v6, /device:TPU:0, one launch (start us, length us, event | category | flops | bytes accessed | tf_op | source)
XLA Modules:
  0.0 52.3 jit_solution(17650333007432364559)
XLA Ops:
  0.7 0.0 copy-start.5
  0.7 0.0 copy-start.6
  0.7 0.6 %copy-done.5 = s32[1,4]{1,0:T(1,128)S(1)} copy-done((s32[1,4]{1,0:T(1,128)S(1)}, s32[1,4]{1,0:T(1,128)}, u32[]{:S(2)}) %copy-start.5) | copy-done | bytes 40
  1.3 0.0 copy-done.6
  1.3 0.1 select_reduce_fusion
  1.4 0.0 copy-start.2
  1.4 0.6 %copy-done.2 = s32[32]{0:T(128)S(1)} copy-done((s32[32]{0:T(128)S(1)}, s32[32]{0:T(128)}, u32[]{:S(2)}) %copy-start.2) | copy-done | bytes 152
  2.1 0.9 %fusion.load_ref = f32[1024,32]{1,0:T(8,128)} fusion(f32[32]{0:T(128)S(1)} %compare_convert_fusion, s32[32]{0:T(128)S(1)} %copy-done.2), kind=kLoop, calls=%fused_computation.2 | loop fusion | flops 65536 | bytes 131328 | tf_op jit(solution)/shard_map/mul | solution.py:205
  3.0 7.1 %beam_solve.1 = f32[1024,32]{1,0:T(8,128)} custom-call(f32[1024,32]{1,0:T(8,128)} %fusion.load_ref, f32[1,8,128,128]{3,2,1,0:T(8,128)} %pivot_ref.1, f32[1,7,128,128]{3,2,1,0:T(8,128)} %lower_ref.1, f32[1,7,128,128]{3,2,1,0:T(8,128)} %upper_ref.1), custom_call_target="tpu_custom_call" | custom-call | tf_op jit(solution)/shard_map/beam_solve/pallas_call | solution.py:172
  10.1 1.4 %convolution_multiply_fusion = f32[32,32]{1,0:T(8,128)S(1)} fusion(f32[1024,32]{1,0:T(8,128)} %beam_solve.1, s32[32]{0:T(128)S(1)} %copy-done.2, f32[32]{0:T(128)S(1)} %compare_convert_fusion), kind=kOutput, calls=%fused_computation | convolution fusion | flops 12616704 | bytes 135424 | tf_op jit(solution)/shard_map/dot_general | solution.py:207
  11.5 0.1 broadcast_in_dim.50
  11.5 0.1 broadcast_in_dim.51
  11.6 0.7 %multiply_reduce_fusion = (f32[]{:T(128)}, f32[]{:T(128)}) fusion(f32[128]{0:T(128)S(1)} %get-tuple-element.42, f32[128]{0:T(128)S(1)} %get-tuple-element.43, f32[128]{0:T(128)S(1)} %fusion.23), kind=kLoop, calls=%fused_computation.5 | loop fusion | flops 147454 | bytes 1544 | tf_op jit(solution)/shard_map/reduce_sum | solution.py:31
  13.7 0.1 broadcast_select_fusion
  13.8 0.7 %fusion.6 = (f32[128,128]{1,0:T(8,128)}, f32[128,128]{1,0:T(8,128)}) fusion(f32[128]{0:T(128)S(1)} %get-tuple-element.41, f32[128]{0:T(128)S(1)} %get-tuple-element.40), kind=kLoop, calls=%fused_computation.13 | loop fusion | flops 81920 | bytes 132096 | tf_op jit(solution)/shard_map/mul | solution.py:24
  14.6 0.8 %fusion.5 = (f32[128,128]{1,0:T(8,128)}, f32[128,128]{1,0:T(8,128)}) fusion(f32[]{:T(128)S(6)} %sqrt.7, f32[128]{0:T(128)S(1)} %get-tuple-element.42, f32[128]{0:T(128)S(1)} %get-tuple-element.43, f32[]{:T(128)S(6)} %sqrt.6, f32[128]{0:T(128)S(1)} %fusion.23), kind=kLoop, calls=%fused_computation.11 | loop fusion | flops 114688 | bytes 132616 | tf_op jit(solution)/shard_map/div | solution.py:31
  15.3 0.6 %reshape.158.refs_0_ = f32[2,16]{1,0:T(2,128)} broadcast(f32[]{:T(128)} %constant.91.clone.1), dimensions={} | broadcast | bytes 132 | tf_op jit(solution)/shard_map/reshape | solution.py:99
  15.9 3.2 %strip_stencil.2 = (f32[2,128,128]{2,1,0:T(8,128)}, f32[2,1,16]{2,1,0:T(1,128)}) custom-call(f32[2,16]{1,0:T(2,128)} %reshape.158.refs_0_, f32[3,2,128,128]{3,2,1,0:T(8,128)} %refs_3_.3, f32[3,2,128,128]{3,2,1,0:T(8,128)} %refs_3_.3, f32[3,2,128,128]{3,2,1,0:T(8,128)} %refs_3_.3, f32[128,128]{1,0:T(8,128)} %get-tuple-element.37.refs_4_, ...), custom_call_target="tpu_custom_call" | custom-call | tf_op jit(solution)/shard_map/strip_stencil/pallas_call | solution.py:105
  19.1 0.0 copy-start.4
  19.1 0.7 %copy-done.4 = f32[2,1,16]{2,1,0:T(1,128)S(1)} copy-done((f32[2,1,16]{2,1,0:T(1,128)S(1)}, f32[2,1,16]{2,1,0:T(1,128)}, u32[]{:S(2)}) %copy-start.4) | copy-done | bytes 152
  19.8 0.7 %pad_maximum_fusion = f32[32,2,48]{2,1,0:T(2,128)} fusion(f32[32,2,32]{2,1,0:T(2,128)S(1)} %broadcast_select_fusion, f32[32,2,16]{2,1,0:T(2,128)S(1)} %tile.17), kind=kLoop, calls=%fused_computation.20 | loop fusion | flops 3072 | bytes 24576 | tf_op jit(solution)/shard_map/concatenate | solution.py:218
  20.5 7.3 %all-to-all-start = ((f32[32,2,48]{2,1,0:T(2,128)}), f32[32,2,48]{2,1,0:T(2,128)S(1)}, u32[]{:S(2)}, u32[]{:S(2)}) async-start(f32[32,2,48]{2,1,0:T(2,128)} %pad_maximum_fusion), calls=%async_computation | async-start | bytes 65536 | tf_op jit(solution)/shard_map/all_to_all | solution.py:219
  27.8 0.1 multiply_subtract_fusion.1
  27.9 7.2 %all-to-all-done = f32[32,2,48]{2,1,0:T(2,128)S(1)} async-done(((f32[32,2,48]{2,1,0:T(2,128)}), f32[32,2,48]{2,1,0:T(2,128)S(1)}, u32[]{:S(2)}, u32[]{:S(2)}) %all-to-all-start) | async-done | bytes 12320 | tf_op jit(solution)/shard_map/all_to_all | solution.py:219
  35.0 0.1 slice.61
  35.1 0.1 slice_reduce_fusion.1
  35.3 0.1 fusion.13
  35.4 0.1 multiply_add_fusion
  35.5 0.2 scatter-add.6
  35.7 0.1 reshape.160
  35.7 0.1 pad_subtract_fusion
  35.8 0.7 %reshape.161.refs_0_ = f32[2,16]{1,0:T(2,128)} reshape(f32[2,2,8]{2,1,0:T(2,128)S(1)} %pad_subtract_fusion) | data formatting | bytes 256 | tf_op jit(solution)/shard_map/reshape | solution.py:99
  36.5 0.0 copy-start
  36.5 3.3 %strip_stencil.3 = (f32[2,128,128]{2,1,0:T(8,128)}, f32[2,1,16]{2,1,0:T(1,128)}) custom-call(f32[2,16]{1,0:T(2,128)} %reshape.161.refs_0_, f32[1,2,128,128]{3,2,1,0:T(8,128)} %bitcast.27, f32[3,2,128,128]{3,2,1,0:T(8,128)} %refs_3_.3, f32[3,2,128,128]{3,2,1,0:T(8,128)} %refs_3_.3, f32[128,128]{1,0:T(8,128)} %get-tuple-element.37.refs_4_, ...), custom_call_target="tpu_custom_call" | custom-call | tf_op jit(solution)/shard_map/strip_stencil/pallas_call | solution.py:105
  39.8 0.0 copy-start.3
  39.8 0.7 %copy-done.3 = f32[2,1,16]{2,1,0:T(1,128)S(1)} copy-done((f32[2,1,16]{2,1,0:T(1,128)S(1)}, f32[2,1,16]{2,1,0:T(1,128)}, u32[]{:S(2)}) %copy-start.3) | copy-done | bytes 152
  40.4 0.6 %tile.19 = f32[32,2,16]{2,1,0:T(2,128)} broadcast(f32[2,16]{1,0:T(2,128)S(1)} %bitcast.29), dimensions={1,2} | broadcast | bytes 4224 | tf_op jit(solution)/shard_map/tile | solution.py:216
  41.1 2.6 %all-to-all-start.1 = ((f32[32,2,16]{2,1,0:T(2,128)}), f32[32,2,16]{2,1,0:T(2,128)S(1)}, u32[]{:S(2)}, u32[]{:S(2)}) async-start(f32[32,2,16]{2,1,0:T(2,128)} %tile.19), calls=%async_computation.1 | async-start | bytes 65536 | tf_op jit(solution)/shard_map/all_to_all | solution.py:219
  43.6 7.2 %all-to-all-done.1 = f32[32,2,16]{2,1,0:T(2,128)S(1)} async-done(((f32[32,2,16]{2,1,0:T(2,128)}), f32[32,2,16]{2,1,0:T(2,128)S(1)}, u32[]{:S(2)}, u32[]{:S(2)}) %all-to-all-start.1) | async-done | bytes 4128 | tf_op jit(solution)/shard_map/all_to_all | solution.py:219
  50.9 0.0 copy-done
  50.9 0.6 %fusion.10 = f32[16,1024]{1,0:T(8,128)S(1)} fusion(f32[1024,32]{1,0:T(8,128)S(1)} %copy-done, f32[64,16]{1,0:T(8,128)S(1)} %bitcast.23, s32[]{:T(128)S(6)} %select_n.14, f32[32]{0:T(128)S(1)} %compare_convert_fusion), kind=kOutput, calls=%fused_computation.22 | convolution fusion | flops 6291968 | bytes 606724 | tf_op jit(solution)/shard_map/dot_general | solution.py:233
  51.5 0.1 slice_reduce_fusion
  51.6 0.1 fusion.9
  51.7 0.0 copy-start.1
  51.7 0.6 %copy-done.1 = f32[1,16,1024]{2,1,0:T(8,128)} copy-done((f32[1,16,1024]{2,1,0:T(8,128)}, f32[1,16,1024]{2,1,0:T(8,128)S(1)}, u32[]{:S(2)}) %copy-start.1) | copy-done | bytes 65560
  (12 shorter events, 0.1 us)
Async XLA Ops:
  0.7 0.7 %copy-start.5 = (s32[1,4]{1,0:T(1,128)S(1)}, s32[1,4]{1,0:T(1,128)}, u32[]{:S(2)}) copy-start(s32[1,4]{1,0:T(1,128)} %param.14) | copy-start | bytes 52
  0.7 0.7 %copy-start.6 = (s32[32,1]{0,1:T(1,128)S(1)}, s32[32,1]{0,1:T(1,128)}, u32[]{:S(2)}) copy-start(s32[32,1]{0,1:T(1,128)} %param.12) | copy-start | bytes 388
  1.4 0.7 %copy-start.2 = (s32[32]{0:T(128)S(1)}, s32[32]{0:T(128)}, u32[]{:S(2)}) copy-start(s32[32]{0:T(128)} %param.13) | copy-start | bytes 388
  19.1 0.7 %copy-start.4 = (f32[2,1,16]{2,1,0:T(1,128)S(1)}, f32[2,1,16]{2,1,0:T(1,128)}, u32[]{:S(2)}) copy-start(f32[2,1,16]{2,1,0:T(1,128)} %get-tuple-element.30) | copy-start | bytes 388
  20.5 14.6 %all-to-all-start = ((f32[32,2,48]{2,1,0:T(2,128)}), f32[32,2,48]{2,1,0:T(2,128)S(1)}, u32[]{:S(2)}, u32[]{:S(2)}) async-start(f32[32,2,48]{2,1,0:T(2,128)} %pad_maximum_fusion), calls=%async_computation | async-start | bytes 65536 | tf_op jit(solution)/shard_map/all_to_all | solution.py:219
  36.5 14.4 %copy-start = (f32[1024,32]{1,0:T(8,128)S(1)}, f32[1024,32]{1,0:T(8,128)}, u32[]{:S(2)}) copy-start(f32[1024,32]{1,0:T(8,128)} %beam_solve.1) | copy-start | bytes 393220
  39.8 0.7 %copy-start.3 = (f32[2,1,16]{2,1,0:T(1,128)S(1)}, f32[2,1,16]{2,1,0:T(1,128)}, u32[]{:S(2)}) copy-start(f32[2,1,16]{2,1,0:T(1,128)} %get-tuple-element.33) | copy-start | bytes 388
  41.1 9.8 %all-to-all-start.1 = ((f32[32,2,16]{2,1,0:T(2,128)}), f32[32,2,16]{2,1,0:T(2,128)S(1)}, u32[]{:S(2)}, u32[]{:S(2)}) async-start(f32[32,2,16]{2,1,0:T(2,128)} %tile.19), calls=%async_computation.1 | async-start | bytes 65536 | tf_op jit(solution)/shard_map/all_to_all | solution.py:219
  51.7 0.6 %copy-start.1 = (f32[1,16,1024]{2,1,0:T(8,128)}, f32[1,16,1024]{2,1,0:T(8,128)S(1)}, u32[]{:S(2)}) copy-start(f32[1,16,1024]{2,1,0:T(8,128)S(1)} %fusion.9) | copy-start | bytes 196612

commit v7 on v6

--- a/solution.py
+++ b/solution.py
@@ -60,11 +60,7 @@
     return (vorticity, jnp.stack(lift_rows + drag_rows, axis=1))
 
 
-def stencil_kernel(velocity_ref, vorticity_ref, flow_x_ref, flow_y_ref, source_x_ref, source_y_ref, lift_ref, drag_ref, out_ref, rows_ref, *, substeps):
-    strip = pl.program_id(0)
-    vorticity = vorticity_ref[0, 0]
-    flow_x = flow_x_ref[0, 0]
-    flow_y = flow_y_ref[0, 0]
+def run_substeps(vorticity, flow_x, flow_y, forcing_of, lift_kernel, drag_kernel, substeps):
     rows_across, cols_across = vorticity.shape
     lane = lax.broadcasted_iota(jnp.int32, (1, 2 * substeps), 1)
     row = jnp.zeros((1, 2 * substeps), jnp.float32)
@@ -79,14 +75,29 @@
             - flow_x * (0.5 * (right_cell - left_cell))
             - flow_y * (0.5 * (upper_cell - lower_cell))
         )
-        forcing = (
+        if forcing_of is None:
+            vorticity = vorticity + TIME_STEP * tendency
+        else:
+            vorticity = vorticity + TIME_STEP * tendency + COUPLING * forcing_of(substep)
+        lift = jnp.sum(jnp.sum(vorticity * lift_kernel, axis=0, keepdims=True), axis=1, keepdims=True)
+        drag = jnp.sum(jnp.sum(vorticity * drag_kernel, axis=0, keepdims=True), axis=1, keepdims=True)
+        row = row + jnp.where(lane == substep, lift, 0.0) + jnp.where(lane == substeps + substep, drag, 0.0)
+    return vorticity, row
+
+
+def stencil_kernel(velocity_ref, vorticity_ref, flow_x_ref, flow_y_ref, source_x_ref, source_y_ref, lift_ref, drag_ref, out_ref, rows_ref, *, substeps):
+    strip = pl.program_id(0)
+
+    def forcing_of(substep):
+        return (
             velocity_ref[strip, substep] * source_x_ref[...]
             - velocity_ref[strip, substeps + substep] * source_y_ref[...]
         )
-        vorticity = vorticity + TIME_STEP * tendency + COUPLING * forcing
-        lift = jnp.sum(jnp.sum(vorticity * lift_ref[...], axis=0, keepdims=True), axis=1, keepdims=True)
-        drag = jnp.sum(jnp.sum(vorticity * drag_ref[...], axis=0, keepdims=True), axis=1, keepdims=True)
-        row = row + jnp.where(lane == substep, lift, 0.0) + jnp.where(lane == substeps + substep, drag, 0.0)
+
+    vorticity, row = run_substeps(
+        vorticity_ref[0, 0], flow_x_ref[0, 0], flow_y_ref[0, 0], forcing_of,
+        lift_ref[...], drag_ref[...], substeps,
+    )
     out_ref[0] = vorticity
     rows_ref[0] = row
 
@@ -146,34 +157,64 @@
     return jnp.concatenate(solved, axis=1)
 
 
-def solve_kernel(load_ref, pivot_ref, lower_ref, upper_ref, out_ref):
+def start_kernel(node_col_ref, node_row_ref, owned_col_ref, owned_row_ref, pivot_ref, lower_ref, upper_ref,
+                 fields_ref, lift_ref, drag_ref, response_ref, coupling_ref, vorticity_ref, rows_ref, *, substeps):
     block_count = pivot_ref.shape[1]
     block_size = pivot_ref.shape[2]
+    node_count = block_count * block_size
+    strips = node_col_ref.shape[0]
 
     def apply(matrix, vectors):
         return jnp.dot(matrix, vectors, precision=lax.Precision.HIGH, preferred_element_type=jnp.float32)
 
-    carried = [load_ref[0:block_size, :]]
+    def unit_load(block_index):
+        node = block_index * block_size + lax.broadcasted_iota(jnp.int32, (block_size, strips), 0)
+        return (node == node_row_ref[...]).astype(jnp.float32) * owned_row_ref[...]
+
+    carried = [unit_load(0)]
     for block_index in range(1, block_count):
         pivoted = apply(pivot_ref[0, block_index - 1], carried[-1])
-        carried.append(
-            load_ref[block_index * block_size:(block_index + 1) * block_size, :]
-            - apply(lower_ref[0, block_index - 1], pivoted)
-        )
+        carried.append(unit_load(block_index) - apply(lower_ref[0, block_index - 1], pivoted))
     solved = apply(pivot_ref[0, block_count - 1], carried[-1])
-    out_ref[(block_count - 1) * block_size:, :] = solved
+    response_ref[(block_count - 1) * block_size:, :] = solved
     for block_index in range(block_count - 2, -1, -1):
         remainder = carried[block_index] - apply(upper_ref[0, block_index], solved)
         solved = apply(pivot_ref[0, block_index], remainder)
-        out_ref[block_index * block_size:(block_index + 1) * block_size, :] = solved
-
-
-def beam_solve_kernel(load_t, pivot_inv, lower_block, upper_block):
+        response_ref[block_index * block_size:(block_index + 1) * block_size, :] = solved
+
+    for strip in range(fields_ref.shape[1]):
+        vorticity, row = run_substeps(
+            fields_ref[0, strip], fields_ref[1, strip], fields_ref[2, strip], None,
+            lift_ref[...], drag_ref[...], substeps,
+        )
+        vorticity_ref[strip] = vorticity
+        rows_ref[strip:strip + 1, :] = row
+
+    node_onehot = (
+        node_col_ref[...] == lax.broadcasted_iota(jnp.int32, (strips, node_count), 1)
+    ).astype(jnp.float32)
+    coupling = jnp.dot(node_onehot, response_ref[...], precision=EXACT_DOT, preferred_element_type=jnp.float32)
+    coupling_ref[...] = coupling * owned_col_ref[...]
+
+
+def start_step(strip_node, owned_here, pivot_inv, lower_block, upper_block, strip_fields, kernels, substeps):
+    _, _, lift_kernel, drag_kernel = kernels
+    strips = strip_node.shape[0]
+    node_count = pivot_inv.shape[1] * pivot_inv.shape[2]
+    _, per_device, cells_y, cells_x = strip_fields.shape
     return pl.pallas_call(
-        solve_kernel,
-        out_shape=jax.ShapeDtypeStruct(load_t.shape, jnp.float32),
-        name="beam_solve",
-    )(load_t, pivot_inv, lower_block, upper_block)
+        lambda *refs: start_kernel(*refs, substeps=substeps),
+        out_shape=[
+            jax.ShapeDtypeStruct((node_count, strips), jnp.float32),
+            jax.ShapeDtypeStruct((strips, strips), jnp.float32),
+            jax.ShapeDtypeStruct((per_device, cells_y, cells_x), jnp.float32),
+            jax.ShapeDtypeStruct((per_device, 2 * substeps), jnp.float32),
+        ],
+        name="start_step",
+    )(
+        strip_node[:, None], strip_node[None, :], owned_here[:, None], owned_here[None, :],
+        pivot_inv, lower_block, upper_block, strip_fields, lift_kernel, drag_kernel,
+    )
 
 
 def local(strip_fields, strip_riser, strip_node, riser_owner, pivot_inv, lower_block, upper_block):
@@ -201,10 +242,9 @@
     top_taper = 1.0 - jnp.arange(node_count, dtype=jnp.float32) / node_count
     local_taper = 1.0 - local_node.astype(jnp.float32) / node_count
 
-    unit_response = beam_solve_kernel(
-        node_onehot.T * owned_here[None, :], pivot_inv, lower_block, upper_block
-    )
-    coupling = jnp.dot(node_onehot, unit_response, precision=EXACT_DOT) * owned_here[:, None]
+    unit_response, coupling, first_vorticity, first_rows = start_step(
+        strip_node, owned_here, pivot_inv, lower_block, upper_block, strip_fields, kernels, substeps
+    )
     coupling_out = jnp.where(
         jnp.arange(group_count)[:, None, None] == group_position, coupling[None], 0.0
     ).reshape(group_count * group_strips, group_strips)
@@ -212,7 +252,10 @@
     vorticity = strip_fields
     motion = jnp.zeros((per_device, 2 * substeps), jnp.float32)
     for coupled_step in range(COUPLED):
-        vorticity, force_rows = strip_step_kernel(strip_fields, vorticity, motion, kernels, substeps)
+        if coupled_step == 0:
+            vorticity, force_rows = first_vorticity[None], first_rows
+        else:
+            vorticity, force_rows = strip_step_kernel(strip_fields, vorticity, motion, kernels, substeps)
         sent = jnp.tile(force_rows, (devices, 1))
         if coupled_step + 1 < COUPLED:
             sent = jnp.concatenate([sent, coupling_out], axis=1)
@@ -228,7 +271,6 @@
                 my_coupling, group_force, (((1,), (0,)), ((), ())), precision=EXACT_DOT
             )
             motion = motion.at[:, substeps:].add(local_taper[:, None] * offset[None, :])
-            vorticity = vorticity[None]
         else:
             displacement = lax.dot_general(
                 group_force * owned_here[:, None], unit_response, (((0,), (1,)), ((), ())), precision=EXACT_DOT

time: 52.8 us -> 48.9 us (0.926)
  Pallas kernels: 13.6 us -> 10.7 us
  local copies, waits for them, and re-layouts: 5.64 us -> 7.22 us
  matrix products: 2.09 us -> 0.74 us
  waiting for transfers between devices: 14.4 us -> 13.6 us
    pallas_call x2 -> x1, Pallas kernels: 6.48 us -> 3.25 us  [strip_step_kernel(): pl.pallas_call(lambda *refs: stencil_kernel(*refs, substeps=substeps), gr...]
    dot_general x1 -> x0, matrix products: 1.36 us -> none  [local(): jnp.dot(node_onehot, unit_response, precision=EXACT_DOT)]
    mul x1 -> x0, other arithmetic: 0.86 us -> none  [local(): node_onehot.T * owned_here[None, :]]
    all_to_all x2, waiting for transfers between devices: 14.4 us -> 13.6 us  [local(): received = lax.all_to_all(sent, ('group', 'strip'), 0, 0, tiled=True)]
    broadcast_in_dim x3, local copies, waits for them, and re-layouts: 0.16 us -> 0.88 us  [local(): jnp.where(jnp.arange(group_count)[:, None, None] == group_position, coupl...]
    broadcast_in_dim x0 -> x1, local copies, waits for them, and re-layouts: none -> 0.69 us  [start_step(): strip_node[:, None]]
    convert_element_type x0 -> x1, local copies, waits for them, and re-layouts: none -> 0.68 us  [local(): owned_here = (owner_index == position).astype(jnp.float32)]
    reshape x2 -> x1, local copies, waits for them, and re-layouts: 1.23 us -> 0.67 us  [strip_step_kernel(): velocity = (halves - earlier).reshape(strips, 2 * substeps)]
  transfers between devices with their start and end apart: 2 -> 2, of which waited for: 2 -> 2; matrix products, arithmetic and copies ran while one was open for 0% -> 2% of each run, Pallas kernels for 0% -> 0%
where the time goes in v7:
time: 48.9 us; the launch traced here: 48.5 us
  waiting for transfers between devices  13.6 us (28%)
  Pallas kernels  10.7 us (22%)
  starting transfers between devices  9.86 us (20%)
  local copies, waits for them, and re-layouts  7.22 us (15%)
  other arithmetic  4.17 us (9%)
  between operations  2.15 us (4%)
  matrix products  0.74 us (2%)
    all_to_all x2, waiting for transfers between devices, local(): received = lax.all_to_all(sent, ('group', 'strip'), 0, 0, tiled=True)  13.6 us
    all_to_all x2, starting transfers between devices, local(): received = lax.all_to_all(sent, ('group', 'strip'), 0, 0, tiled=True)  9.86 us
    pallas_call x1, Pallas kernels, start_step(): pl.pallas_call(lambda *refs: start_kernel(*refs, substeps=substeps), out_...  7.47 us
    unnamed x17, local copies, waits for them, and re-layouts  3.3 us
    pallas_call x1, Pallas kernels, strip_step_kernel(): pl.pallas_call(lambda *refs: stencil_kernel(*refs, substeps=substeps), gr...  3.25 us
  transfers between devices with their start and end apart: 2, of which 2 were waited for; matrix products, arithmetic and copies ran while one was open for 2% of the time, Pallas kernels for 0%

profile of v7, /device:TPU:0, one launch (start us, length us, event | category | flops | bytes accessed | tf_op | source)
XLA Modules:
  0.0 48.5 jit_solution(1103214532363671144)
XLA Ops:
  0.7 0.0 copy-start.6
  0.7 0.0 copy-start.7
  0.7 0.6 %copy-done.6 = s32[1,4]{1,0:T(1,128)S(1)} copy-done((s32[1,4]{1,0:T(1,128)S(1)}, s32[1,4]{1,0:T(1,128)}, u32[]{:S(2)}) %copy-start.6) | copy-done | bytes 40
  1.3 0.0 copy-done.7
  1.3 0.1 select_reduce_fusion
  1.4 0.5 fusion.24.refs_3_
  1.9 0.7 %multiply_reduce_fusion = (f32[]{:T(128)}, f32[]{:T(128)}) fusion(f32[128]{0:T(128)S(1)} %get-tuple-element.44, f32[128]{0:T(128)S(1)} %get-tuple-element.45, f32[128]{0:T(128)S(1)} %fusion.21), kind=kLoop, calls=%fused_computation.3 | loop fusion | flops 147454 | bytes 1544 | tf_op jit(solution)/shard_map/reduce_sum | solution.py:31
  4.0 0.7 %copy.18.refs_2_ = f32[32,1]{1,0:T(8,128)} copy(f32[32,1]{0,1:T(1,128)S(1)} %fusion.25) | data formatting | bytes 256 | tf_op jit(solution)/shard_map/convert_element_type | solution.py:237
  4.7 0.0 copy-start.2
  4.7 0.7 %copy-done.2 = s32[32]{0:T(128)S(1)} copy-done((s32[32]{0:T(128)S(1)}, s32[32]{0:T(128)}, u32[]{:S(2)}) %copy-start.2) | copy-done | bytes 152
  5.3 0.7 %copy.17.refs_0_ = s32[32,1]{1,0:T(8,128)} copy(s32[32,1]{0,1:T(1,128)S(1)} %bitcast.34) | data formatting | bytes 256 | tf_op jit(solution)/shard_map/broadcast_in_dim | solution.py:215
  6.0 0.1 broadcast_in_dim.56
  6.1 0.1 broadcast_in_dim.57
  6.2 0.7 %fusion.5 = (f32[128,128]{1,0:T(8,128)}, f32[128,128]{1,0:T(8,128)}) fusion(f32[]{:T(128)S(6)} %sqrt.7, f32[128]{0:T(128)S(1)} %get-tuple-element.44, f32[128]{0:T(128)S(1)} %get-tuple-element.45, f32[]{:T(128)S(6)} %sqrt.6, f32[128]{0:T(128)S(1)} %fusion.21), kind=kLoop, calls=%fused_computation.9 | loop fusion | flops 114688 | bytes 132616 | tf_op jit(solution)/shard_map/div | solution.py:31
  6.9 7.5 %start_step.1 = (f32[1024,32]{1,0:T(8,128)}, f32[32,32]{1,0:T(8,128)}, f32[2,128,128]{2,1,0:T(8,128)}, f32[2,16]{1,0:T(2,128)}) custom-call(s32[32,1]{1,0:T(8,128)} %copy.17.refs_0_, s32[1,32]{1,0:T(1,128)} %bitcast.33, f32[32,1]{1,0:T(8,128)} %copy.18.refs_2_, f32[1,32]{1,0:T(1,128)} %fusion.24.refs_3_, f32[1,8,128,128]{3,2,1,0:T(8,128)} %refs_4_.1, ...), custom_call_target="tpu_custom_call" | custom-call | tf_op jit(solution)/shard_map/start_step/pallas_call | solution.py:205
  14.4 0.7 %broadcast_in_dim.59 = f32[2,32,32]{2,1,0:T(8,128)S(1)} broadcast(f32[32,32]{1,0:T(8,128)} %get-tuple-element.33), dimensions={1,2} | broadcast | bytes 12288 | tf_op jit(solution)/shard_map/jit(_where)/broadcast_in_dim | solution.py:248
  15.1 0.1 broadcast_select_fusion
  15.2 0.0 copy-start.4
  15.3 0.7 %copy-done.4 = f32[2,16]{1,0:T(2,128)S(1)} copy-done((f32[2,16]{1,0:T(2,128)S(1)}, f32[2,16]{1,0:T(2,128)}, u32[]{:S(2)}) %copy-start.4) | copy-done | bytes 152
  15.9 0.7 %pad_maximum_fusion = f32[32,2,48]{2,1,0:T(2,128)} fusion(f32[32,2,32]{2,1,0:T(2,128)S(1)} %broadcast_select_fusion, f32[32,2,16]{2,1,0:T(2,128)S(1)} %tile.6), kind=kLoop, calls=%fused_computation.15 | loop fusion | flops 3072 | bytes 24576 | tf_op jit(solution)/shard_map/concatenate | solution.py:261
  16.6 7.3 %all-to-all-start = ((f32[32,2,48]{2,1,0:T(2,128)}), f32[32,2,48]{2,1,0:T(2,128)S(1)}, u32[]{:S(2)}, u32[]{:S(2)}) async-start(f32[32,2,48]{2,1,0:T(2,128)} %pad_maximum_fusion), calls=%async_computation | async-start | bytes 65536 | tf_op jit(solution)/shard_map/all_to_all | solution.py:262
  24.0 0.0 copy-start.3
  24.0 0.7 %fusion = (f32[128,128]{1,0:T(8,128)}, f32[128,128]{1,0:T(8,128)}) fusion(f32[128]{0:T(128)S(1)} %get-tuple-element.47, f32[128]{0:T(128)S(1)} %get-tuple-element.46), kind=kLoop, calls=%fused_computation.1 | loop fusion | flops 81920 | bytes 132096 | tf_op jit(solution)/shard_map/mul | solution.py:24
  24.7 0.0 copy-done.3
  24.7 0.1 multiply_subtract_fusion.1
  24.8 6.4 %all-to-all-done = f32[32,2,48]{2,1,0:T(2,128)S(1)} async-done(((f32[32,2,48]{2,1,0:T(2,128)}), f32[32,2,48]{2,1,0:T(2,128)S(1)}, u32[]{:S(2)}, u32[]{:S(2)}) %all-to-all-start) | async-done | bytes 12320 | tf_op jit(solution)/shard_map/all_to_all | solution.py:262
  31.2 0.1 slice.61
  31.3 0.1 slice_reduce_fusion.1
  31.4 0.1 fusion.11
  31.6 0.1 multiply_add_fusion
  31.6 0.2 scatter-add.6
  31.8 0.1 reshape.175
  31.9 0.1 pad_subtract_fusion
  32.0 0.7 %reshape.176.refs_0_ = f32[2,16]{1,0:T(2,128)} reshape(f32[2,2,8]{2,1,0:T(2,128)S(1)} %pad_subtract_fusion) | data formatting | bytes 256 | tf_op jit(solution)/shard_map/reshape | solution.py:110
  32.7 0.0 copy-start
  32.7 3.3 %strip_stencil.1 = (f32[2,128,128]{2,1,0:T(8,128)}, f32[2,1,16]{2,1,0:T(1,128)}) custom-call(f32[2,16]{1,0:T(2,128)} %reshape.176.refs_0_, f32[1,2,128,128]{3,2,1,0:T(8,128)} %bitcast.31, f32[3,2,128,128]{3,2,1,0:T(8,128)} %refs_3_.1, f32[3,2,128,128]{3,2,1,0:T(8,128)} %refs_3_.1, f32[128,128]{1,0:T(8,128)} %get-tuple-element.41.refs_4_, ...), custom_call_target="tpu_custom_call" | custom-call | tf_op jit(solution)/shard_map/strip_stencil/pallas_call | solution.py:116
  35.9 0.0 copy-start.5
  35.9 0.7 %copy-done.5 = f32[2,1,16]{2,1,0:T(1,128)S(1)} copy-done((f32[2,1,16]{2,1,0:T(1,128)S(1)}, f32[2,1,16]{2,1,0:T(1,128)}, u32[]{:S(2)}) %copy-start.5) | copy-done | bytes 152
  36.6 0.6 %tile.8 = f32[32,2,16]{2,1,0:T(2,128)} broadcast(f32[2,16]{1,0:T(2,128)S(1)} %bitcast.35), dimensions={1,2} | broadcast | bytes 4224 | tf_op jit(solution)/shard_map/tile | solution.py:259
  37.2 2.6 %all-to-all-start.1 = ((f32[32,2,16]{2,1,0:T(2,128)}), f32[32,2,16]{2,1,0:T(2,128)S(1)}, u32[]{:S(2)}, u32[]{:S(2)}) async-start(f32[32,2,16]{2,1,0:T(2,128)} %tile.8), calls=%async_computation.1 | async-start | bytes 65536 | tf_op jit(solution)/shard_map/all_to_all | solution.py:262
  39.8 7.2 %all-to-all-done.1 = f32[32,2,16]{2,1,0:T(2,128)S(1)} async-done(((f32[32,2,16]{2,1,0:T(2,128)}), f32[32,2,16]{2,1,0:T(2,128)S(1)}, u32[]{:S(2)}, u32[]{:S(2)}) %all-to-all-start.1) | async-done | bytes 4128 | tf_op jit(solution)/shard_map/all_to_all | solution.py:262
  47.0 0.1 slice_reduce_fusion
  47.1 0.0 copy-done
  47.1 0.6 %fusion.8 = f32[16,1024]{1,0:T(8,128)S(1)} fusion(f32[1024,32]{1,0:T(8,128)S(1)} %copy-done, f32[64,16]{1,0:T(8,128)S(1)} %bitcast.28, s32[]{:T(128)S(6)} %select_n.14, f32[32]{0:T(128)S(1)} %compare_convert_fusion), kind=kOutput, calls=%fused_computation.17 | convolution fusion | flops 6291968 | bytes 606724 | tf_op jit(solution)/shard_map/dot_general | solution.py:275
  47.8 0.1 fusion.7
  47.9 0.0 copy-start.1
  47.9 0.6 %copy-done.1 = f32[1,16,1024]{2,1,0:T(8,128)} copy-done((f32[1,16,1024]{2,1,0:T(8,128)}, f32[1,16,1024]{2,1,0:T(8,128)S(1)}, u32[]{:S(2)}) %copy-start.1) | copy-done | bytes 65560
  (12 shorter events, 0.1 us)
Async XLA Ops:
  0.7 0.7 %copy-start.6 = (s32[1,4]{1,0:T(1,128)S(1)}, s32[1,4]{1,0:T(1,128)}, u32[]{:S(2)}) copy-start(s32[1,4]{1,0:T(1,128)} %param.14) | copy-start | bytes 52
  0.7 0.7 %copy-start.7 = (s32[32,1]{0,1:T(1,128)S(1)}, s32[32,1]{0,1:T(1,128)}, u32[]{:S(2)}) copy-start(s32[32,1]{0,1:T(1,128)} %param.12) | copy-start | bytes 388
  4.7 0.7 %copy-start.2 = (s32[32]{0:T(128)S(1)}, s32[32]{0:T(128)}, u32[]{:S(2)}) copy-start(s32[32]{0:T(128)} %param.13) | copy-start | bytes 388
  15.2 0.7 %copy-start.4 = (f32[2,16]{1,0:T(2,128)S(1)}, f32[2,16]{1,0:T(2,128)}, u32[]{:S(2)}) copy-start(f32[2,16]{1,0:T(2,128)} %get-tuple-element.32) | copy-start | bytes 388
  16.6 14.6 %all-to-all-start = ((f32[32,2,48]{2,1,0:T(2,128)}), f32[32,2,48]{2,1,0:T(2,128)S(1)}, u32[]{:S(2)}, u32[]{:S(2)}) async-start(f32[32,2,48]{2,1,0:T(2,128)} %pad_maximum_fusion), calls=%async_computation | async-start | bytes 65536 | tf_op jit(solution)/shard_map/all_to_all | solution.py:262
  24.0 0.7 %copy-start.3 = (s32[32]{0:T(128)S(1)}, s32[32]{0:T(128)}, u32[]{:S(2)}) copy-start(s32[32]{0:T(128)} %param.13) | copy-start | bytes 388
  32.7 14.5 %copy-start = (f32[1024,32]{1,0:T(8,128)S(1)}, f32[1024,32]{1,0:T(8,128)}, u32[]{:S(2)}) copy-start(f32[1024,32]{1,0:T(8,128)} %get-tuple-element.37) | copy-start | bytes 393220
  35.9 0.7 %copy-start.5 = (f32[2,1,16]{2,1,0:T(1,128)S(1)}, f32[2,1,16]{2,1,0:T(1,128)}, u32[]{:S(2)}) copy-start(f32[2,1,16]{2,1,0:T(1,128)} %get-tuple-element.36) | copy-start | bytes 388
  37.2 9.8 %all-to-all-start.1 = ((f32[32,2,16]{2,1,0:T(2,128)}), f32[32,2,16]{2,1,0:T(2,128)S(1)}, u32[]{:S(2)}, u32[]{:S(2)}) async-start(f32[32,2,16]{2,1,0:T(2,128)} %tile.8), calls=%async_computation.1 | async-start | bytes 65536 | tf_op jit(solution)/shard_map/all_to_all | solution.py:262
  47.9 0.6 %copy-start.1 = (f32[1,16,1024]{2,1,0:T(8,128)}, f32[1,16,1024]{2,1,0:T(8,128)S(1)}, u32[]{:S(2)}) copy-start(f32[1,16,1024]{2,1,0:T(8,128)S(1)} %fusion.7) | copy-start | bytes 196612

commit v8 on v7

--- a/solution.py
+++ b/solution.py
@@ -60,6 +60,28 @@
     return (vorticity, jnp.stack(lift_rows + drag_rows, axis=1))
 
 
+def kernel_planes(cells):
+    centre_x = lax.broadcasted_iota(jnp.int32, (cells, cells), 1).astype(jnp.float32) - cells / 2.0 + 0.5
+    centre_y = lax.broadcasted_iota(jnp.int32, (cells, cells), 0).astype(jnp.float32) - cells / 2.0 + 0.5
+    near_x = centre_x / (cells / 16.0)
+    near_y = centre_y / (cells / 16.0)
+    bell_near = jnp.exp(-(near_x * near_x + near_y * near_y) / 2.0)
+    source_x = -near_x * bell_near
+    source_y = -near_y * bell_near
+    wide_x = centre_x / (cells / 8.0)
+    wide_y = centre_y / (cells / 8.0)
+    bell_wide = jnp.exp(-(wide_x * wide_x + wide_y * wide_y) / 2.0)
+    lift_kernel = -wide_x * bell_wide
+    drag_kernel = wide_y * bell_wide
+
+    def total(plane):
+        return jnp.sum(jnp.sum(plane, axis=0, keepdims=True), axis=1, keepdims=True)
+
+    lift_kernel = lift_kernel / jnp.sqrt(total(lift_kernel * lift_kernel))
+    drag_kernel = drag_kernel / jnp.sqrt(total(drag_kernel * drag_kernel))
+    return (source_x, source_y, lift_kernel, drag_kernel)
+
+
 def run_substeps(vorticity, flow_x, flow_y, forcing_of, lift_kernel, drag_kernel, substeps):
     rows_across, cols_across = vorticity.shape
     lane = lax.broadcasted_iota(jnp.int32, (1, 2 * substeps), 1)
@@ -85,31 +107,29 @@
     return vorticity, row
 
 
-def stencil_kernel(velocity_ref, vorticity_ref, flow_x_ref, flow_y_ref, source_x_ref, source_y_ref, lift_ref, drag_ref, out_ref, rows_ref, *, substeps):
+def stencil_kernel(velocity_ref, vorticity_ref, flow_x_ref, flow_y_ref, out_ref, rows_ref, *, substeps):
     strip = pl.program_id(0)
+    source_x, source_y, lift_kernel, drag_kernel = kernel_planes(vorticity_ref.shape[-1])
 
     def forcing_of(substep):
         return (
-            velocity_ref[strip, substep] * source_x_ref[...]
-            - velocity_ref[strip, substeps + substep] * source_y_ref[...]
+            velocity_ref[strip, substep] * source_x
+            - velocity_ref[strip, substeps + substep] * source_y
         )
 
     vorticity, row = run_substeps(
         vorticity_ref[0, 0], flow_x_ref[0, 0], flow_y_ref[0, 0], forcing_of,
-        lift_ref[...], drag_ref[...], substeps,
+        lift_kernel, drag_kernel, substeps,
     )
     out_ref[0] = vorticity
     rows_ref[0] = row
 
 
 def strip_step_kernel(strip_fields, vorticity, motion, kernels, substeps):
-    source_x, source_y, lift_kernel, drag_kernel = kernels
     strips, cells_y, cells_x = strip_fields.shape[1:]
     halves = motion.reshape(strips, 2, substeps)
     earlier = jnp.concatenate([jnp.zeros_like(halves[:, :, :1]), halves[:, :, :-1]], axis=2)
     velocity = (halves - earlier).reshape(strips, 2 * substeps)
-    plane = pl.BlockSpec((cells_y, cells_x), lambda s: (0, 0))
-
     def field(index):
         return pl.BlockSpec((1, 1, cells_y, cells_x), lambda s: (index, s, 0, 0))
 
@@ -119,7 +139,6 @@
         in_specs=[
             pl.BlockSpec(memory_space=pltpu.SMEM),
             field(0), field(1), field(2),
-            plane, plane, plane, plane,
         ],
         out_specs=[
             pl.BlockSpec((1, cells_y, cells_x), lambda s: (s, 0, 0)),
@@ -130,7 +149,7 @@
             jax.ShapeDtypeStruct((strips, 1, 2 * substeps), jnp.float32),
         ],
         name="strip_stencil",
-    )(velocity, vorticity, strip_fields, strip_fields, source_x, source_y, lift_kernel, drag_kernel)
+    )(velocity, vorticity, strip_fields, strip_fields)
     return new_vorticity, rows[:, 0, :]
 
 
@@ -157,19 +176,32 @@
     return jnp.concatenate(solved, axis=1)
 
 
-def start_kernel(node_col_ref, node_row_ref, owned_col_ref, owned_row_ref, pivot_ref, lower_ref, upper_ref,
-                 fields_ref, lift_ref, drag_ref, response_ref, coupling_ref, vorticity_ref, rows_ref, *, substeps):
+def start_kernel(owner_ref, riser_ref, node_ref, spread_ref, pivot_ref, lower_ref, upper_ref, fields_ref,
+                 response_ref, vorticity_ref, sent_ref, *, substeps):
     block_count = pivot_ref.shape[1]
     block_size = pivot_ref.shape[2]
     node_count = block_count * block_size
-    strips = node_col_ref.shape[0]
+    strips = node_ref.shape[1]
+    per_device = fields_ref.shape[1]
+    position = lax.axis_index("strip")
+    group_position = lax.axis_index("group")
+
+    riser = riser_ref[...]
+    owner = jnp.zeros(riser.shape, jnp.int32)
+    for riser_index in range(owner_ref.shape[1]):
+        owner = jnp.where(riser == riser_index, owner_ref[0, riser_index], owner)
+    owned_col = (owner == position).astype(jnp.float32)
+    diagonal = lax.broadcasted_iota(jnp.int32, (strips, strips), 0) == lax.broadcasted_iota(jnp.int32, (strips, strips), 1)
+    owned_row = jnp.sum(jnp.where(diagonal, owned_col, 0.0), axis=0, keepdims=True)
+    node_row = node_ref[...]
+    node_col = jnp.sum(jnp.where(diagonal, node_row.astype(jnp.float32), 0.0), axis=1, keepdims=True)
 
     def apply(matrix, vectors):
         return jnp.dot(matrix, vectors, precision=lax.Precision.HIGH, preferred_element_type=jnp.float32)
 
     def unit_load(block_index):
         node = block_index * block_size + lax.broadcasted_iota(jnp.int32, (block_size, strips), 0)
-        return (node == node_row_ref[...]).astype(jnp.float32) * owned_row_ref[...]
+        return (node == node_row).astype(jnp.float32) * owned_row
 
     carried = [unit_load(0)]
     for block_index in range(1, block_count):
@@ -182,38 +214,52 @@
         solved = apply(pivot_ref[0, block_index], remainder)
         response_ref[block_index * block_size:(block_index + 1) * block_size, :] = solved
 
-    for strip in range(fields_ref.shape[1]):
+    _, _, lift_kernel, drag_kernel = kernel_planes(fields_ref.shape[-1])
+    strip_of_row = lax.broadcasted_iota(jnp.int32, (per_device, 2 * substeps), 0)
+    rows = jnp.zeros((per_device, 2 * substeps), jnp.float32)
+    for strip in range(per_device):
         vorticity, row = run_substeps(
             fields_ref[0, strip], fields_ref[1, strip], fields_ref[2, strip], None,
-            lift_ref[...], drag_ref[...], substeps,
+            lift_kernel, drag_kernel, substeps,
         )
         vorticity_ref[strip] = vorticity
-        rows_ref[strip:strip + 1, :] = row
+        rows = jnp.where(strip_of_row == strip, row, rows)
 
     node_onehot = (
-        node_col_ref[...] == lax.broadcasted_iota(jnp.int32, (strips, node_count), 1)
+        node_col == lax.broadcasted_iota(jnp.int32, (strips, node_count), 1).astype(jnp.float32)
     ).astype(jnp.float32)
     coupling = jnp.dot(node_onehot, response_ref[...], precision=EXACT_DOT, preferred_element_type=jnp.float32)
-    coupling_ref[...] = coupling * owned_col_ref[...]
-
-
-def start_step(strip_node, owned_here, pivot_inv, lower_block, upper_block, strip_fields, kernels, substeps):
-    _, _, lift_kernel, drag_kernel = kernels
+    coupling = coupling * owned_col
+    sent_rows = sent_ref.shape[0]
+    place = lax.broadcasted_iota(jnp.int32, (sent_rows, strips), 0) - group_position * strips
+    pick = (place == lax.broadcasted_iota(jnp.int32, (sent_rows, strips), 1)).astype(jnp.float32)
+    sent_ref[:, 0:2 * substeps] = jnp.dot(spread_ref[...], rows, precision=EXACT_DOT, preferred_element_type=jnp.float32)
+    sent_ref[:, 2 * substeps:] = jnp.dot(pick, coupling, precision=EXACT_DOT, preferred_element_type=jnp.float32)
+
+
+def spread_matrix(devices, per_device):
+    return (
+        jnp.arange(devices * per_device)[:, None] % per_device == jnp.arange(per_device)[None, :]
+    ).astype(jnp.float32)
+
+
+def start_step(riser_owner, strip_riser, strip_node, pivot_inv, lower_block, upper_block, strip_fields, devices, substeps):
     strips = strip_node.shape[0]
     node_count = pivot_inv.shape[1] * pivot_inv.shape[2]
     _, per_device, cells_y, cells_x = strip_fields.shape
+    vmem = pl.BlockSpec(memory_space=pltpu.VMEM)
     return pl.pallas_call(
         lambda *refs: start_kernel(*refs, substeps=substeps),
+        in_specs=[pl.BlockSpec(memory_space=pltpu.SMEM)] + [vmem] * 7,
         out_shape=[
             jax.ShapeDtypeStruct((node_count, strips), jnp.float32),
-            jax.ShapeDtypeStruct((strips, strips), jnp.float32),
             jax.ShapeDtypeStruct((per_device, cells_y, cells_x), jnp.float32),
-            jax.ShapeDtypeStruct((per_device, 2 * substeps), jnp.float32),
+            jax.ShapeDtypeStruct((devices * per_device, 2 * substeps + strips), jnp.float32),
         ],
         name="start_step",
     )(
-        strip_node[:, None], strip_node[None, :], owned_here[:, None], owned_here[None, :],
-        pivot_inv, lower_block, upper_block, strip_fields, lift_kernel, drag_kernel,
+        riser_owner, strip_riser, strip_node[None, :], spread_matrix(devices, per_device),
+        pivot_inv, lower_block, upper_block, strip_fields,
     )
 
 
@@ -229,36 +275,23 @@
     group_strips = strip_node.shape[0]
     substeps = NSUB
     total_strips = per_device * devices
-    kernels = make_kernels(grid_cells)
-    riser_match = (
-        strip_riser[:, 0][:, None] == jnp.arange(riser_count, dtype=jnp.int32)[None, :]
-    ).astype(jnp.int32)
-    owner_index = jnp.sum(riser_match * riser_owner[0][None, :], axis=1)
-    owned_here = (owner_index == position).astype(jnp.float32)
-    node_onehot = (
-        strip_node[:, None] == jnp.arange(node_count, dtype=jnp.int32)[None, :]
-    ).astype(jnp.float32)
+    kernels = None
     local_node = lax.dynamic_slice_in_dim(strip_node, position * per_device, per_device)
     top_taper = 1.0 - jnp.arange(node_count, dtype=jnp.float32) / node_count
     local_taper = 1.0 - local_node.astype(jnp.float32) / node_count
 
-    unit_response, coupling, first_vorticity, first_rows = start_step(
-        strip_node, owned_here, pivot_inv, lower_block, upper_block, strip_fields, kernels, substeps
+    unit_response, first_vorticity, first_sent = start_step(
+        riser_owner, strip_riser, strip_node, pivot_inv, lower_block, upper_block, strip_fields, devices, substeps
     )
-    coupling_out = jnp.where(
-        jnp.arange(group_count)[:, None, None] == group_position, coupling[None], 0.0
-    ).reshape(group_count * group_strips, group_strips)
 
     vorticity = strip_fields
     motion = jnp.zeros((per_device, 2 * substeps), jnp.float32)
     for coupled_step in range(COUPLED):
         if coupled_step == 0:
-            vorticity, force_rows = first_vorticity[None], first_rows
+            vorticity, sent = first_vorticity[None], first_sent
         else:
             vorticity, force_rows = strip_step_kernel(strip_fields, vorticity, motion, kernels, substeps)
-        sent = jnp.tile(force_rows, (devices, 1))
-        if coupled_step + 1 < COUPLED:
-            sent = jnp.concatenate([sent, coupling_out], axis=1)
+            sent = jnp.tile(force_rows, (devices, 1))
         received = lax.all_to_all(sent, ("group", "strip"), 0, 0, tiled=True)
         every_force = received[:, : 2 * substeps]
         offset = jnp.sum(every_force[:, substeps:], axis=0) / jnp.sqrt(jnp.float32(total_strips))
@@ -273,7 +306,7 @@
             motion = motion.at[:, substeps:].add(local_taper[:, None] * offset[None, :])
         else:
             displacement = lax.dot_general(
-                group_force * owned_here[:, None], unit_response, (((0,), (1,)), ((), ())), precision=EXACT_DOT
+                group_force, unit_response, (((0,), (1,)), ((), ())), precision=EXACT_DOT
             )
             displacement = displacement.at[substeps:, :].add(offset[:, None] * top_taper[None, :])
     return (vorticity, displacement[None])

time: 48.9 us -> 41.6 us (0.85)
  local copies, waits for them, and re-layouts: 7.22 us -> 4.28 us
  other arithmetic: 4.17 us -> 1.25 us
  between operations: 2.15 us -> 0.71 us
    broadcast_in_dim x4 -> x0, local copies, waits for them, and re-layouts: 1.57 us -> none  [the longest x3 0.88 us: local(): jnp.where(jnp.arange(group_count)[:, None, None] == group_position, coupl...]
    reduce_sum x2 -> x0, other arithmetic: 0.79 us -> none  [the longest x1 0.7 us: make_kernels(): drag_kernel = drag_kernel / jnp.sqrt(jnp.sum(drag_kernel * drag_kernel))]
    div x2 -> x0, other arithmetic: 0.76 us -> none  [the longest x1 0.75 us: make_kernels(): drag_kernel = drag_kernel / jnp.sqrt(jnp.sum(drag_kernel * drag_kernel))]
    mul x2 -> x0, other arithmetic: 0.74 us -> none  [the longest x1 0.73 us: make_kernels(): source_y = -near_y * bell_near]
    concatenate x1 -> x0, other arithmetic: 0.72 us -> none  [local(): sent = jnp.concatenate([sent, coupling_out], axis=1)]
    convert_element_type x1 -> x0, local copies, waits for them, and re-layouts: 0.68 us -> none  [local(): owned_here = (owner_index == position).astype(jnp.float32)]
    unnamed x17 -> x12, local copies, waits for them, and re-layouts: 3.3 us -> 2.64 us
  transfers between devices with their start and end apart: 2 -> 2, of which waited for: 2 -> 2; matrix products, arithmetic and copies ran while one was open for 2% -> 0% of each run, Pallas kernels for 0% -> 0%
where the time goes in v8:
time: 41.6 us; the launch traced here: 41.4 us
  waiting for transfers between devices  13.7 us (33%)
  Pallas kernels  10.8 us (26%)
  starting transfers between devices  9.86 us (24%)
  local copies, waits for them, and re-layouts  4.28 us (10%)
  other arithmetic  1.25 us (3%)
  between operations  0.71 us (2%)
  matrix products  0.68 us (2%)
    all_to_all x2, waiting for transfers between devices, local(): received = lax.all_to_all(sent, ('group', 'strip'), 0, 0, tiled=True)  13.7 us
    all_to_all x2, starting transfers between devices, local(): received = lax.all_to_all(sent, ('group', 'strip'), 0, 0, tiled=True)  9.86 us
    pallas_call x1, Pallas kernels, start_step(): pl.pallas_call(lambda *refs: start_kernel(*refs, substeps=substeps), in_s...  7.74 us
    pallas_call x1, Pallas kernels, strip_step_kernel(): pl.pallas_call(lambda *refs: stencil_kernel(*refs, substeps=substeps), gr...  3.09 us
    unnamed x12, local copies, waits for them, and re-layouts  2.64 us
  transfers between devices with their start and end apart: 2, of which 2 were waited for; matrix products, arithmetic and copies ran while one was open for 0% of the time, Pallas kernels for 0%

profile of v8, /device:TPU:0, one launch (start us, length us, event | category | flops | bytes accessed | tf_op | source)
XLA Modules:
  0.0 41.4 jit_solution(6407848375745766595)
XLA Ops:
  0.6 0.0 copy-start.4
  0.7 0.7 %fusion.2.refs_3_ = f32[64,2]{1,0:T(8,128)} fusion(s32[64]{0:T(128)S(1)} %and_select_fusion), kind=kLoop, calls=%fused_computation.6 | loop fusion | flops 256 | bytes 768 | tf_op jit(solution)/shard_map/convert_element_type | solution.py:243
  1.3 0.0 copy-done.4
  1.3 0.7 %copy.12.refs_1_ = s32[32,1]{1,0:T(8,128)} copy(s32[32,1]{0,1:T(1,128)S(1)} %copy-done.4) | data formatting | bytes 256 | tf_op args[1]
  2.0 7.7 %start_step.1 = (f32[1024,32]{1,0:T(8,128)}, f32[2,128,128]{2,1,0:T(8,128)}, f32[64,48]{1,0:T(8,128)}) custom-call(s32[1,4]{1,0:T(1,128)} %refs_0_.1, s32[32,1]{1,0:T(8,128)} %copy.12.refs_1_, s32[1,32]{1,0:T(1,128)} %bitcast.27, f32[64,2]{1,0:T(8,128)} %fusion.2.refs_3_, f32[1,8,128,128]{3,2,1,0:T(8,128)} %refs_4_.1, f32[1,7,128,128]{3,2,1,0:T(8,128)} %refs_5_.1, ...), custom_call_target="tpu_custom_call" | custom-call | tf_op jit(solution)/shard_map/start_step/pallas_call | solution.py:251
  9.8 7.3 %all-to-all-start = ((f32[32,2,48]{2,1,0:T(2,128)}), f32[32,2,48]{2,1,0:T(2,128)S(1)}, u32[]{:S(2)}, u32[]{:S(2)}) async-start(f32[32,2,48]{2,1,0:T(2,128)} %bitcast.24), calls=%async_computation | async-start | bytes 65536 | tf_op jit(solution)/shard_map/all_to_all | solution.py:295
  17.1 0.0 copy-start.3
  17.1 0.6 %copy-done.3 = s32[32]{0:T(128)S(1)} copy-done((s32[32]{0:T(128)S(1)}, s32[32]{0:T(128)}, u32[]{:S(2)}) %copy-start.3) | copy-done | bytes 152
  17.7 0.1 multiply_subtract_fusion.1
  17.8 6.5 %all-to-all-done = f32[32,2,48]{2,1,0:T(2,128)S(1)} async-done(((f32[32,2,48]{2,1,0:T(2,128)}), f32[32,2,48]{2,1,0:T(2,128)S(1)}, u32[]{:S(2)}, u32[]{:S(2)}) %all-to-all-start) | async-done | bytes 12320 | tf_op jit(solution)/shard_map/all_to_all | solution.py:295
  24.3 0.1 slice.61
  24.4 0.1 slice_reduce_fusion.1
  24.5 0.1 fusion.5
  24.7 0.1 multiply_add_fusion
  24.8 0.2 scatter-add.6
  25.0 0.1 reshape.101
  25.0 0.1 pad_subtract_fusion
  25.1 0.7 %reshape.102.refs_0_ = f32[2,16]{1,0:T(2,128)} reshape(f32[2,2,8]{2,1,0:T(2,128)S(1)} %pad_subtract_fusion) | data formatting | bytes 256 | tf_op jit(solution)/shard_map/reshape | solution.py:132
  25.8 0.0 copy-start
  25.8 3.1 %strip_stencil.1 = (f32[2,128,128]{2,1,0:T(8,128)}, f32[2,1,16]{2,1,0:T(1,128)}) custom-call(f32[2,16]{1,0:T(2,128)} %reshape.102.refs_0_, f32[1,2,128,128]{3,2,1,0:T(8,128)} %bitcast.23, f32[3,2,128,128]{3,2,1,0:T(8,128)} %refs_3_.1, f32[3,2,128,128]{3,2,1,0:T(8,128)} %refs_3_.1), custom_call_target="tpu_custom_call" | custom-call | tf_op jit(solution)/shard_map/strip_stencil/pallas_call | solution.py:136
  28.9 0.0 copy-start.2
  28.9 0.6 %copy-done.2 = f32[2,1,16]{2,1,0:T(1,128)S(1)} copy-done((f32[2,1,16]{2,1,0:T(1,128)S(1)}, f32[2,1,16]{2,1,0:T(1,128)}, u32[]{:S(2)}) %copy-start.2) | copy-done | bytes 152
  29.5 0.6 %tile.9 = f32[32,2,16]{2,1,0:T(2,128)} broadcast(f32[2,16]{1,0:T(2,128)S(1)} %bitcast.26), dimensions={1,2} | broadcast | bytes 4224 | tf_op jit(solution)/shard_map/tile | solution.py:294
  30.1 2.6 %all-to-all-start.1 = ((f32[32,2,16]{2,1,0:T(2,128)}), f32[32,2,16]{2,1,0:T(2,128)S(1)}, u32[]{:S(2)}, u32[]{:S(2)}) async-start(f32[32,2,16]{2,1,0:T(2,128)} %tile.9), calls=%async_computation.1 | async-start | bytes 65536 | tf_op jit(solution)/shard_map/all_to_all | solution.py:295
  32.7 7.2 %all-to-all-done.1 = f32[32,2,16]{2,1,0:T(2,128)S(1)} async-done(((f32[32,2,16]{2,1,0:T(2,128)}), f32[32,2,16]{2,1,0:T(2,128)S(1)}, u32[]{:S(2)}, u32[]{:S(2)}) %all-to-all-start.1) | async-done | bytes 4128 | tf_op jit(solution)/shard_map/all_to_all | solution.py:295
  40.0 0.1 slice_reduce_fusion
  40.0 0.0 copy-done
  40.1 0.5 %fusion.3 = f32[16,1024]{1,0:T(8,128)S(1)} fusion(f32[1024,32]{1,0:T(8,128)S(1)} %copy-done, f32[64,16]{1,0:T(8,128)S(1)} %bitcast.21, s32[]{:T(128)S(6)} %select_n.20), kind=kOutput, calls=%fused_computation.7 | convolution fusion | flops 6291456 | bytes 606212 | tf_op jit(solution)/shard_map/dot_general | solution.py:308
  40.6 0.1 fusion.1
  40.7 0.0 copy-start.1
  40.7 0.6 %copy-done.1 = f32[1,16,1024]{2,1,0:T(8,128)} copy-done((f32[1,16,1024]{2,1,0:T(8,128)}, f32[1,16,1024]{2,1,0:T(8,128)S(1)}, u32[]{:S(2)}) %copy-start.1) | copy-done | bytes 65560
  (6 shorter events, 0.1 us)
Async XLA Ops:
  0.6 0.7 %copy-start.4 = (s32[32,1]{0,1:T(1,128)S(1)}, s32[32,1]{0,1:T(1,128)}, u32[]{:S(2)}) copy-start(s32[32,1]{0,1:T(1,128)} %param.12) | copy-start | bytes 388
  9.8 14.6 %all-to-all-start = ((f32[32,2,48]{2,1,0:T(2,128)}), f32[32,2,48]{2,1,0:T(2,128)S(1)}, u32[]{:S(2)}, u32[]{:S(2)}) async-start(f32[32,2,48]{2,1,0:T(2,128)} %bitcast.24), calls=%async_computation | async-start | bytes 65536 | tf_op jit(solution)/shard_map/all_to_all | solution.py:295
  17.1 0.7 %copy-start.3 = (s32[32]{0:T(128)S(1)}, s32[32]{0:T(128)}, u32[]{:S(2)}) copy-start(s32[32]{0:T(128)} %param.13) | copy-start | bytes 388
  25.8 14.3 %copy-start = (f32[1024,32]{1,0:T(8,128)S(1)}, f32[1024,32]{1,0:T(8,128)}, u32[]{:S(2)}) copy-start(f32[1024,32]{1,0:T(8,128)} %get-tuple-element.35) | copy-start | bytes 393220
  28.9 0.6 %copy-start.2 = (f32[2,1,16]{2,1,0:T(1,128)S(1)}, f32[2,1,16]{2,1,0:T(1,128)}, u32[]{:S(2)}) copy-start(f32[2,1,16]{2,1,0:T(1,128)} %get-tuple-element.34) | copy-start | bytes 388
  30.1 9.8 %all-to-all-start.1 = ((f32[32,2,16]{2,1,0:T(2,128)}), f32[32,2,16]{2,1,0:T(2,128)S(1)}, u32[]{:S(2)}, u32[]{:S(2)}) async-start(f32[32,2,16]{2,1,0:T(2,128)} %tile.9), calls=%async_computation.1 | async-start | bytes 65536 | tf_op jit(solution)/shard_map/all_to_all | solution.py:295
  40.7 0.6 %copy-start.1 = (f32[1,16,1024]{2,1,0:T(8,128)}, f32[1,16,1024]{2,1,0:T(8,128)S(1)}, u32[]{:S(2)}) copy-start(f32[1,16,1024]{2,1,0:T(8,128)S(1)} %fusion.1) | copy-start | bytes 196612

commit v9 on v8

--- a/solution.py
+++ b/solution.py
@@ -1,3 +1,4 @@
+import numpy as np
 import jax
 import jax.numpy as jnp
 from jax import lax
@@ -186,13 +187,15 @@
     position = lax.axis_index("strip")
     group_position = lax.axis_index("group")
 
-    riser = riser_ref[...]
-    owner = jnp.zeros(riser.shape, jnp.int32)
-    for riser_index in range(owner_ref.shape[1]):
-        owner = jnp.where(riser == riser_index, owner_ref[0, riser_index], owner)
-    owned_col = (owner == position).astype(jnp.float32)
+    strip_lane = lax.broadcasted_iota(jnp.int32, (1, strips), 1)
+    strip_sublane = lax.broadcasted_iota(jnp.int32, (strips, 1), 0)
+    owned_row = jnp.zeros((1, strips), jnp.float32)
+    owned_col = jnp.zeros((strips, 1), jnp.float32)
+    for strip in range(strips):
+        held = jnp.where(owner_ref[0, riser_ref[strip, 0]] == position, 1.0, 0.0)
+        owned_row = jnp.where(strip_lane == strip, held, owned_row)
+        owned_col = jnp.where(strip_sublane == strip, held, owned_col)
     diagonal = lax.broadcasted_iota(jnp.int32, (strips, strips), 0) == lax.broadcasted_iota(jnp.int32, (strips, strips), 1)
-    owned_row = jnp.sum(jnp.where(diagonal, owned_col, 0.0), axis=0, keepdims=True)
     node_row = node_ref[...]
     node_col = jnp.sum(jnp.where(diagonal, node_row.astype(jnp.float32), 0.0), axis=1, keepdims=True)
 
@@ -239,8 +242,8 @@
 
 def spread_matrix(devices, per_device):
     return (
-        jnp.arange(devices * per_device)[:, None] % per_device == jnp.arange(per_device)[None, :]
-    ).astype(jnp.float32)
+        np.arange(devices * per_device)[:, None] % per_device == np.arange(per_device)[None, :]
+    ).astype(np.float32)
 
 
 def start_step(riser_owner, strip_riser, strip_node, pivot_inv, lower_block, upper_block, strip_fields, devices, substeps):
@@ -250,7 +253,7 @@
     vmem = pl.BlockSpec(memory_space=pltpu.VMEM)
     return pl.pallas_call(
         lambda *refs: start_kernel(*refs, substeps=substeps),
-        in_specs=[pl.BlockSpec(memory_space=pltpu.SMEM)] + [vmem] * 7,
+        in_specs=[pl.BlockSpec(memory_space=pltpu.SMEM)] * 2 + [vmem] * 6,
         out_shape=[
             jax.ShapeDtypeStruct((node_count, strips), jnp.float32),
             jax.ShapeDtypeStruct((per_device, cells_y, cells_x), jnp.float32),
@@ -261,6 +264,73 @@
         riser_owner, strip_riser, strip_node[None, :], spread_matrix(devices, per_device),
         pivot_inv, lower_block, upper_block, strip_fields,
     )
+
+
+def second_kernel(received_ref, node_ref, spread_ref, gather_ref, difference_ref, fields_ref, vorticity_ref,
+                  out_ref, sent_ref, *, substeps, node_count):
+    position = lax.axis_index("strip")
+    group_position = lax.axis_index("group")
+    total_strips, _ = received_ref.shape
+    strips = node_ref.shape[1]
+    per_device = fields_ref.shape[1]
+    every_force = received_ref[:, 0:2 * substeps]
+    offset = jnp.sum(every_force, axis=0, keepdims=True) / jnp.sqrt(jnp.float32(total_strips))
+    group_force = received_ref[pl.ds(group_position * strips, strips), 0:2 * substeps]
+    my_coupling = jnp.dot(
+        gather_ref[...], received_ref[:, 2 * substeps:], precision=EXACT_DOT, preferred_element_type=jnp.float32
+    )
+    motion = jnp.dot(my_coupling, group_force, precision=EXACT_DOT, preferred_element_type=jnp.float32)
+    mine = (
+        lax.broadcasted_iota(jnp.int32, (per_device, strips), 1)
+        == position * per_device + lax.broadcasted_iota(jnp.int32, (per_device, strips), 0)
+    )
+    local_node = jnp.sum(jnp.where(mine, node_ref[...].astype(jnp.float32), 0.0), axis=1, keepdims=True)
+    local_taper = 1.0 - local_node / node_count
+    lane = lax.broadcasted_iota(jnp.int32, (per_device, 2 * substeps), 1)
+    sublane = lax.broadcasted_iota(jnp.int32, (per_device, 2 * substeps), 0)
+    motion = motion + jnp.where(lane >= substeps, local_taper * offset, 0.0)
+    velocity = jnp.dot(motion, difference_ref[...], precision=EXACT_DOT, preferred_element_type=jnp.float32)
+
+    source_x, source_y, lift_kernel, drag_kernel = kernel_planes(fields_ref.shape[-1])
+    rows = jnp.zeros((per_device, 2 * substeps), jnp.float32)
+    for strip in range(per_device):
+        picks = [
+            jnp.sum(jnp.sum(jnp.where((sublane == strip) & (lane == column), velocity, 0.0), axis=0, keepdims=True), axis=1, keepdims=True)
+            for column in range(2 * substeps)
+        ]
+
+        def forcing_of(substep, picks=picks):
+            return picks[substep] * source_x - picks[substeps + substep] * source_y
+
+        vorticity, row = run_substeps(
+            vorticity_ref[strip], fields_ref[1, strip], fields_ref[2, strip], forcing_of,
+            lift_kernel, drag_kernel, substeps,
+        )
+        out_ref[strip] = vorticity
+        rows = jnp.where(sublane == strip, row, rows)
+    sent_ref[...] = jnp.dot(spread_ref[...], rows, precision=EXACT_DOT, preferred_element_type=jnp.float32)
+
+
+def difference_matrix(substeps):
+    columns = np.arange(2 * substeps)
+    same = columns[:, None] == columns[None, :]
+    before = (columns[:, None] + 1 == columns[None, :]) & (columns[None, :] % substeps != 0)
+    return same.astype(np.float32) - before.astype(np.float32)
+
+
+def second_step(received, strip_node, strip_fields, vorticity, devices, node_count, substeps):
+    _, per_device, cells_y, cells_x = strip_fields.shape
+    spread = spread_matrix(devices, per_device)
+    vmem = pl.BlockSpec(memory_space=pltpu.VMEM)
+    return pl.pallas_call(
+        lambda *refs: second_kernel(*refs, substeps=substeps, node_count=node_count),
+        in_specs=[vmem] * 7,
+        out_shape=[
+            jax.ShapeDtypeStruct((per_device, cells_y, cells_x), jnp.float32),
+            jax.ShapeDtypeStruct((devices * per_device, 2 * substeps), jnp.float32),
+        ],
+        name="second_step",
+    )(received, strip_node[None, :], spread, np.ascontiguousarray(spread.T), difference_matrix(substeps), strip_fields, vorticity)
 
 
 def local(strip_fields, strip_riser, strip_node, riser_owner, pivot_inv, lower_block, upper_block):
@@ -284,31 +354,15 @@
         riser_owner, strip_riser, strip_node, pivot_inv, lower_block, upper_block, strip_fields, devices, substeps
     )
 
-    vorticity = strip_fields
-    motion = jnp.zeros((per_device, 2 * substeps), jnp.float32)
-    for coupled_step in range(COUPLED):
-        if coupled_step == 0:
-            vorticity, sent = first_vorticity[None], first_sent
-        else:
-            vorticity, force_rows = strip_step_kernel(strip_fields, vorticity, motion, kernels, substeps)
-            sent = jnp.tile(force_rows, (devices, 1))
-        received = lax.all_to_all(sent, ("group", "strip"), 0, 0, tiled=True)
-        every_force = received[:, : 2 * substeps]
-        offset = jnp.sum(every_force[:, substeps:], axis=0) / jnp.sqrt(jnp.float32(total_strips))
-        group_force = lax.dynamic_slice_in_dim(every_force, group_position * group_strips, group_strips)
-        if coupled_step + 1 < COUPLED:
-            my_coupling = jnp.sum(
-                received[:, 2 * substeps :].reshape(devices, per_device, group_strips), axis=0
-            )
-            motion = lax.dot_general(
-                my_coupling, group_force, (((1,), (0,)), ((), ())), precision=EXACT_DOT
-            )
-            motion = motion.at[:, substeps:].add(local_taper[:, None] * offset[None, :])
-        else:
-            displacement = lax.dot_general(
-                group_force, unit_response, (((0,), (1,)), ((), ())), precision=EXACT_DOT
-            )
-            displacement = displacement.at[substeps:, :].add(offset[:, None] * top_taper[None, :])
+    received = lax.all_to_all(first_sent, ("group", "strip"), 0, 0, tiled=True)
+    vorticity, sent = second_step(received, strip_node, strip_fields, first_vorticity, devices, node_count, substeps)
+    received = lax.all_to_all(sent, ("group", "strip"), 0, 0, tiled=True)
+    offset = jnp.sum(received[:, substeps:], axis=0) / jnp.sqrt(jnp.float32(total_strips))
+    group_force = lax.dynamic_slice_in_dim(received, group_position * group_strips, group_strips)
+    displacement = lax.dot_general(
+        group_force, unit_response, (((0,), (1,)), ((), ())), precision=EXACT_DOT
+    )
+    displacement = displacement.at[substeps:, :].add(offset[:, None] * top_taper[None, :])
     return (vorticity, displacement[None])
 
 

time: 41.6 us -> 39.4 us (0.947)
  blocking collectives: 0 us -> 14.7 us
  starting transfers between devices: 9.86 us -> 2.57 us
  waiting for transfers between devices: 13.7 us -> 7.23 us
  local copies, waits for them, and re-layouts: 4.28 us -> 2 us
  other arithmetic: 1.25 us -> 0.18 us
  Pallas kernels: 10.8 us -> 11.3 us
    all_to_all x0 -> x1, blocking collectives: none -> 14.7 us  [local(): received = lax.all_to_all(first_sent, ('group', 'strip'), 0, 0, tiled=True)]
    all_to_all x2 -> x1, starting transfers between devices: 9.86 us -> 2.57 us  [local(): received = lax.all_to_all(sent, ('group', 'strip'), 0, 0, tiled=True)]
    all_to_all x2 -> x1, waiting for transfers between devices: 13.7 us -> 7.23 us  [local(): received = lax.all_to_all(sent, ('group', 'strip'), 0, 0, tiled=True)]
    reshape x2 -> x0, local copies, waits for them, and re-layouts: 0.74 us -> none  [the longest x1 0.66 us: strip_step_kernel(): velocity = (halves - earlier).reshape(strips, 2 * substeps)]
    convert_element_type x1 -> x0, other arithmetic: 0.69 us -> none  [spread_matrix(): return (jnp.arange(devices * per_device)[:, None] % per_device == jnp.ara...]
    unnamed x12 -> x6, local copies, waits for them, and re-layouts: 2.64 us -> 2 us
    another operation x1 -> x0, local copies, waits for them, and re-layouts: 0.62 us -> none  [local(): sent = jnp.tile(force_rows, (devices, 1))]
    pallas_call x1, Pallas kernels: 3.09 us -> 3.53 us  [second_step(): pl.pallas_call(lambda *refs: second_kernel(*refs, substeps=substeps, node...]
  transfers between devices with their start and end apart: 2 -> 1, of which waited for: 2 -> 1; matrix products, arithmetic and copies ran while one was open for 0% -> 0% of each run, Pallas kernels for 0% -> 0%
where the time goes in v9:
time: 39.4 us; the launch traced here: 39.1 us
  blocking collectives  14.7 us (37%)
  Pallas kernels  11.3 us (29%)
  waiting for transfers between devices  7.23 us (18%)
  starting transfers between devices  2.57 us (7%)
  local copies, waits for them, and re-layouts  2 us (5%)
  between operations  0.67 us (2%)
  matrix products  0.55 us (1%)
    all_to_all x1, blocking collectives, local(): received = lax.all_to_all(first_sent, ('group', 'strip'), 0, 0, tiled=True)  14.7 us
    pallas_call x1, Pallas kernels, start_step(): pl.pallas_call(lambda *refs: start_kernel(*refs, substeps=substeps), in_s...  7.75 us
    all_to_all x1, waiting for transfers between devices, local(): received = lax.all_to_all(sent, ('group', 'strip'), 0, 0, tiled=True)  7.23 us
    pallas_call x1, Pallas kernels, second_step(): pl.pallas_call(lambda *refs: second_kernel(*refs, substeps=substeps, node...  3.53 us
    all_to_all x1, starting transfers between devices, local(): received = lax.all_to_all(sent, ('group', 'strip'), 0, 0, tiled=True)  2.57 us
    unnamed x6, local copies, waits for them, and re-layouts  2 us
  transfers between devices with their start and end apart: 1, of which 1 were waited for; matrix products, arithmetic and copies ran while one was open for 0% of the time, Pallas kernels for 0%

profile of v9, /device:TPU:0, one launch (start us, length us, event | category | flops | bytes accessed | tf_op | source)
XLA Modules:
  0.0 39.1 jit_solution(178163652018234446)
XLA Ops:
  0.6 1.3 %copy.13.refs_1_ = s32[32,1]{1,0:T(8,128)} copy(s32[32,1]{0,1:T(1,128)} %param.14) | data formatting | bytes 256 | tf_op args[1]
  2.0 7.8 %start_step.1 = (f32[1024,32]{1,0:T(8,128)}, f32[2,128,128]{2,1,0:T(8,128)}, f32[64,48]{1,0:T(8,128)}) custom-call(s32[1,4]{1,0:T(1,128)} %refs_0_.1, s32[32,1]{1,0:T(8,128)} %copy.13.refs_1_, s32[1,32]{1,0:T(1,128)} %bitcast.17, f32[64,2]{1,0:T(8,128)} %constant.57.clone.refs_3_.refs_2_, f32[1,8,128,128]{3,2,1,0:T(8,128)} %refs_4_.2, ...), custom_call_target="tpu_custom_call" | custom-call | tf_op jit(solution)/shard_map/start_step/pallas_call | solution.py:254
  9.7 0.0 copy-start
  9.7 14.7 %all_to_all.23 = f32[32,2,48]{2,1,0:T(2,128)} all-to-all(f32[32,2,48]{2,1,0:T(2,128)} %bitcast.16), channel_id=1, replica_groups=mesh['group'=2,'strip'=16] {'group','strip'}, dimensions={0} | all-to-all | bytes 24576 | tf_op jit(solution)/shard_map/all_to_all | solution.py:357
  24.4 3.5 %second_step.1 = (f32[2,128,128]{2,1,0:T(8,128)}, f32[64,16]{1,0:T(8,128)}) custom-call(f32[64,48]{1,0:T(8,128)} %bitcast.14, s32[1,32]{1,0:T(1,128)} %bitcast.18, f32[64,2]{1,0:T(8,128)} %constant.57.clone.refs_3_.refs_2_, f32[2,64]{1,0:T(2,128)} %constant.58.clone.refs_3_, f32[16,16]{1,0:T(8,128)} %constant.59.clone.refs_4_, f32[3,2,128,128]{3,2,1,0:T(8,128)} %refs_5_.3, ...), custom_call_target="tpu_custom_call" | custom-call | tf_op jit(solution)/shard_map/second_step/pallas_call | solution.py:325
  27.9 2.6 %all-to-all-start.1 = ((f32[32,2,16]{2,1,0:T(2,128)}), f32[32,2,16]{2,1,0:T(2,128)S(1)}, u32[]{:S(2)}, u32[]{:S(2)}) async-start(f32[32,2,16]{2,1,0:T(2,128)} %bitcast.15), calls=%async_computation.1 | async-start | bytes 65536 | tf_op jit(solution)/shard_map/all_to_all | solution.py:359
  30.5 7.2 %all-to-all-done.1 = f32[32,2,16]{2,1,0:T(2,128)S(1)} async-done(((f32[32,2,16]{2,1,0:T(2,128)}), f32[32,2,16]{2,1,0:T(2,128)S(1)}, u32[]{:S(2)}, u32[]{:S(2)}) %all-to-all-start.1) | async-done | bytes 4128 | tf_op jit(solution)/shard_map/all_to_all | solution.py:359
  37.7 0.1 slice_reduce_fusion
  37.8 0.0 copy-done
  37.8 0.5 %fusion.2 = f32[16,1024]{1,0:T(8,128)S(1)} fusion(f32[1024,32]{1,0:T(8,128)S(1)} %copy-done, f32[64,16]{1,0:T(8,128)S(1)} %bitcast.13, s32[]{:T(128)S(6)} %select_n.3), kind=kOutput, calls=%fused_computation.4 | convolution fusion | flops 6291456 | bytes 606212 | tf_op jit(solution)/shard_map/dot_general | solution.py:362
  38.4 0.1 fusion.1
  38.5 0.0 copy-start.1
  38.5 0.6 %copy-done.1 = f32[1,16,1024]{2,1,0:T(8,128)} copy-done((f32[1,16,1024]{2,1,0:T(8,128)}, f32[1,16,1024]{2,1,0:T(8,128)S(1)}, u32[]{:S(2)}) %copy-start.1) | copy-done | bytes 65560
  (3 shorter events, 0.0 us)
Async XLA Ops:
  9.7 28.1 %copy-start = (f32[1024,32]{1,0:T(8,128)S(1)}, f32[1024,32]{1,0:T(8,128)}, u32[]{:S(2)}) copy-start(f32[1024,32]{1,0:T(8,128)} %get-tuple-element.23) | copy-start | bytes 393220
  27.9 9.8 %all-to-all-start.1 = ((f32[32,2,16]{2,1,0:T(2,128)}), f32[32,2,16]{2,1,0:T(2,128)S(1)}, u32[]{:S(2)}, u32[]{:S(2)}) async-start(f32[32,2,16]{2,1,0:T(2,128)} %bitcast.15), calls=%async_computation.1 | async-start | bytes 65536 | tf_op jit(solution)/shard_map/all_to_all | solution.py:359
  38.5 0.6 %copy-start.1 = (f32[1,16,1024]{2,1,0:T(8,128)}, f32[1,16,1024]{2,1,0:T(8,128)S(1)}, u32[]{:S(2)}) copy-start(f32[1,16,1024]{2,1,0:T(8,128)S(1)} %fusion.1) | copy-start | bytes 196612

commit v10 on v9

--- a/solution.py
+++ b/solution.py
@@ -192,7 +192,7 @@
     owned_row = jnp.zeros((1, strips), jnp.float32)
     owned_col = jnp.zeros((strips, 1), jnp.float32)
     for strip in range(strips):
-        held = jnp.where(owner_ref[0, riser_ref[strip, 0]] == position, 1.0, 0.0)
+        held = jnp.where(owner_ref[0, riser_ref[strip]] == position, 1.0, 0.0)
         owned_row = jnp.where(strip_lane == strip, held, owned_row)
         owned_col = jnp.where(strip_sublane == strip, held, owned_col)
     diagonal = lax.broadcasted_iota(jnp.int32, (strips, strips), 0) == lax.broadcasted_iota(jnp.int32, (strips, strips), 1)
@@ -261,7 +261,7 @@
         ],
         name="start_step",
     )(
-        riser_owner, strip_riser, strip_node[None, :], spread_matrix(devices, per_device),
+        riser_owner, strip_riser.reshape(strips), strip_node[None, :], spread_matrix(devices, per_device),
         pivot_inv, lower_block, upper_block, strip_fields,
     )
 
@@ -345,10 +345,7 @@
     group_strips = strip_node.shape[0]
     substeps = NSUB
     total_strips = per_device * devices
-    kernels = None
-    local_node = lax.dynamic_slice_in_dim(strip_node, position * per_device, per_device)
     top_taper = 1.0 - jnp.arange(node_count, dtype=jnp.float32) / node_count
-    local_taper = 1.0 - local_node.astype(jnp.float32) / node_count
 
     unit_response, first_vorticity, first_sent = start_step(
         riser_owner, strip_riser, strip_node, pivot_inv, lower_block, upper_block, strip_fields, devices, substeps

time: 39.4 us -> 38 us (0.964)
  local copies, waits for them, and re-layouts: 2 us -> 0.66 us
    unnamed x6 -> x5, local copies, waits for them, and re-layouts: 2 us -> 0.66 us
where the time goes in v10:
time: 38 us; the launch traced here: 37.8 us
  blocking collectives  14.7 us (39%)
  Pallas kernels  11.3 us (30%)
  waiting for transfers between devices  7.23 us (19%)
  starting transfers between devices  2.57 us (7%)
  between operations  0.67 us (2%)
  local copies, waits for them, and re-layouts  0.66 us (2%)
  matrix products  0.55 us (1%)
    all_to_all x1, blocking collectives, local(): received = lax.all_to_all(first_sent, ('group', 'strip'), 0, 0, tiled=True)  14.7 us
    pallas_call x1, Pallas kernels, start_step(): pl.pallas_call(lambda *refs: start_kernel(*refs, substeps=substeps), in_s...  7.75 us
    all_to_all x1, waiting for transfers between devices, local(): received = lax.all_to_all(sent, ('group', 'strip'), 0, 0, tiled=True)  7.23 us
    pallas_call x1, Pallas kernels, second_step(): pl.pallas_call(lambda *refs: second_kernel(*refs, substeps=substeps, node...  3.53 us
    all_to_all x1, starting transfers between devices, local(): received = lax.all_to_all(sent, ('group', 'strip'), 0, 0, tiled=True)  2.57 us
  transfers between devices with their start and end apart: 1, of which 1 were waited for; matrix products, arithmetic and copies ran while one was open for 0% of the time, Pallas kernels for 0%

profile of v10, /device:TPU:0, one launch (start us, length us, event | category | flops | bytes accessed | tf_op | source)
XLA Modules:
  0.0 37.8 jit_solution(9689531867795492898)
XLA Ops:
  0.6 7.8 %start_step.1 = (f32[1024,32]{1,0:T(8,128)}, f32[2,128,128]{2,1,0:T(8,128)}, f32[64,48]{1,0:T(8,128)}) custom-call(s32[1,4]{1,0:T(1,128)} %refs_0_.1, s32[32]{0:T(128)} %bitcast.20, s32[1,32]{1,0:T(1,128)} %bitcast.18, f32[64,2]{1,0:T(8,128)} %constant.57.clone.refs_3_.refs_2_, f32[1,8,128,128]{3,2,1,0:T(8,128)} %refs_4_.2, f32[1,7,128,128]{3,2,1,0:T(8,128)} %refs_5_.2, ...), custom_call_target="tpu_custom_call" | custom-call | tf_op jit(solution)/shard_map/start_step/pallas_call | solution.py:254
  8.4 0.0 copy-start
  8.4 14.7 %all_to_all.23 = f32[32,2,48]{2,1,0:T(2,128)} all-to-all(f32[32,2,48]{2,1,0:T(2,128)} %bitcast.17), channel_id=1, replica_groups=mesh['group'=2,'strip'=16] {'group','strip'}, dimensions={0} | all-to-all | bytes 24576 | tf_op jit(solution)/shard_map/all_to_all | solution.py:354
  23.0 3.5 %second_step.1 = (f32[2,128,128]{2,1,0:T(8,128)}, f32[64,16]{1,0:T(8,128)}) custom-call(f32[64,48]{1,0:T(8,128)} %bitcast.15, s32[1,32]{1,0:T(1,128)} %bitcast.19, f32[64,2]{1,0:T(8,128)} %constant.57.clone.refs_3_.refs_2_, f32[2,64]{1,0:T(2,128)} %constant.58.clone.refs_3_, f32[16,16]{1,0:T(8,128)} %constant.59.clone.refs_4_, f32[3,2,128,128]{3,2,1,0:T(8,128)} %refs_5_.3, ...), custom_call_target="tpu_custom_call" | custom-call | tf_op jit(solution)/shard_map/second_step/pallas_call | solution.py:325
  26.6 2.6 %all-to-all-start.1 = ((f32[32,2,16]{2,1,0:T(2,128)}), f32[32,2,16]{2,1,0:T(2,128)S(1)}, u32[]{:S(2)}, u32[]{:S(2)}) async-start(f32[32,2,16]{2,1,0:T(2,128)} %bitcast.16), calls=%async_computation.1 | async-start | bytes 65536 | tf_op jit(solution)/shard_map/all_to_all | solution.py:356
  29.2 7.2 %all-to-all-done.1 = f32[32,2,16]{2,1,0:T(2,128)S(1)} async-done(((f32[32,2,16]{2,1,0:T(2,128)}), f32[32,2,16]{2,1,0:T(2,128)S(1)}, u32[]{:S(2)}, u32[]{:S(2)}) %all-to-all-start.1) | async-done | bytes 4128 | tf_op jit(solution)/shard_map/all_to_all | solution.py:356
  36.4 0.1 slice_reduce_fusion
  36.5 0.0 copy-done
  36.5 0.5 %fusion.2 = f32[16,1024]{1,0:T(8,128)S(1)} fusion(f32[1024,32]{1,0:T(8,128)S(1)} %copy-done, f32[64,16]{1,0:T(8,128)S(1)} %bitcast.14, s32[]{:T(128)S(6)} %select_n.3), kind=kOutput, calls=%fused_computation.4 | convolution fusion | flops 6291456 | bytes 606212 | tf_op jit(solution)/shard_map/dot_general | solution.py:359
  37.1 0.1 fusion.1
  37.2 0.0 copy-start.1
  37.2 0.6 %copy-done.1 = f32[1,16,1024]{2,1,0:T(8,128)} copy-done((f32[1,16,1024]{2,1,0:T(8,128)}, f32[1,16,1024]{2,1,0:T(8,128)S(1)}, u32[]{:S(2)}) %copy-start.1) | copy-done | bytes 65560
  (3 shorter events, 0.0 us)
Async XLA Ops:
  8.4 28.1 %copy-start = (f32[1024,32]{1,0:T(8,128)S(1)}, f32[1024,32]{1,0:T(8,128)}, u32[]{:S(2)}) copy-start(f32[1024,32]{1,0:T(8,128)} %get-tuple-element.23) | copy-start | bytes 393220
  26.6 9.8 %all-to-all-start.1 = ((f32[32,2,16]{2,1,0:T(2,128)}), f32[32,2,16]{2,1,0:T(2,128)S(1)}, u32[]{:S(2)}, u32[]{:S(2)}) async-start(f32[32,2,16]{2,1,0:T(2,128)} %bitcast.16), calls=%async_computation.1 | async-start | bytes 65536 | tf_op jit(solution)/shard_map/all_to_all | solution.py:356
  37.2 0.6 %copy-start.1 = (f32[1,16,1024]{2,1,0:T(8,128)}, f32[1,16,1024]{2,1,0:T(8,128)S(1)}, u32[]{:S(2)}) copy-start(f32[1,16,1024]{2,1,0:T(8,128)S(1)} %fusion.1) | copy-start | bytes 196612

commit v11 on v10

--- a/solution.py
+++ b/solution.py
@@ -177,10 +177,28 @@
     return jnp.concatenate(solved, axis=1)
 
 
-def start_kernel(owner_ref, riser_ref, node_ref, spread_ref, pivot_ref, lower_ref, upper_ref, fields_ref,
-                 response_ref, vorticity_ref, sent_ref, *, substeps):
-    block_count = pivot_ref.shape[1]
-    block_size = pivot_ref.shape[2]
+def start_kernel(owner_ref, riser_ref, node_ref, spread_ref, pivot_hbm, lower_hbm, upper_hbm, fields_ref,
+                 response_ref, vorticity_ref, sent_ref, pivot_ref, lower_ref, upper_ref, copy_sems, *, substeps):
+    block_count = pivot_hbm.shape[1]
+    block_size = pivot_hbm.shape[2]
+    pending = {}
+
+    def fetch(name, source, target, block_index):
+        copy = pltpu.make_async_copy(source.at[0, block_index], target.at[block_index], copy_sems.at[len(pending)])
+        copy.start()
+        pending[(name, block_index)] = copy
+
+    for block_index in range(block_count - 1):
+        fetch("pivot", pivot_hbm, pivot_ref, block_index)
+        fetch("lower", lower_hbm, lower_ref, block_index)
+    fetch("pivot", pivot_hbm, pivot_ref, block_count - 1)
+    for block_index in range(block_count - 2, -1, -1):
+        fetch("upper", upper_hbm, upper_ref, block_index)
+
+    def block(name, ref, block_index):
+        pending.pop((name, block_index)).wait()
+        return ref[block_index]
+
     node_count = block_count * block_size
     strips = node_ref.shape[1]
     per_device = fields_ref.shape[1]
@@ -208,13 +226,13 @@
 
     carried = [unit_load(0)]
     for block_index in range(1, block_count):
-        pivoted = apply(pivot_ref[0, block_index - 1], carried[-1])
-        carried.append(unit_load(block_index) - apply(lower_ref[0, block_index - 1], pivoted))
-    solved = apply(pivot_ref[0, block_count - 1], carried[-1])
+        pivoted = apply(block("pivot", pivot_ref, block_index - 1), carried[-1])
+        carried.append(unit_load(block_index) - apply(block("lower", lower_ref, block_index - 1), pivoted))
+    solved = apply(block("pivot", pivot_ref, block_count - 1), carried[-1])
     response_ref[(block_count - 1) * block_size:, :] = solved
     for block_index in range(block_count - 2, -1, -1):
-        remainder = carried[block_index] - apply(upper_ref[0, block_index], solved)
-        solved = apply(pivot_ref[0, block_index], remainder)
+        remainder = carried[block_index] - apply(block("upper", upper_ref, block_index), solved)
+        solved = apply(pivot_ref[block_index], remainder)
         response_ref[block_index * block_size:(block_index + 1) * block_size, :] = solved
 
     _, _, lift_kernel, drag_kernel = kernel_planes(fields_ref.shape[-1])
@@ -251,9 +269,17 @@
     node_count = pivot_inv.shape[1] * pivot_inv.shape[2]
     _, per_device, cells_y, cells_x = strip_fields.shape
     vmem = pl.BlockSpec(memory_space=pltpu.VMEM)
+    hbm = pl.BlockSpec(memory_space=pl.ANY)
+    block_count, block_size = pivot_inv.shape[1], pivot_inv.shape[2]
     return pl.pallas_call(
         lambda *refs: start_kernel(*refs, substeps=substeps),
-        in_specs=[pl.BlockSpec(memory_space=pltpu.SMEM)] * 2 + [vmem] * 6,
+        in_specs=[pl.BlockSpec(memory_space=pltpu.SMEM)] * 2 + [vmem] * 2 + [hbm] * 3 + [vmem],
+        scratch_shapes=[
+            pltpu.VMEM((block_count, block_size, block_size), jnp.float32),
+            pltpu.VMEM((block_count - 1, block_size, block_size), jnp.float32),
+            pltpu.VMEM((block_count - 1, block_size, block_size), jnp.float32),
+            pltpu.SemaphoreType.DMA((3 * block_count - 2,)),
+        ],
         out_shape=[
             jax.ShapeDtypeStruct((node_count, strips), jnp.float32),
             jax.ShapeDtypeStruct((per_device, cells_y, cells_x), jnp.float32),

time: 38 us -> 39.6 us (1.042)
  Pallas kernels: 11.3 us -> 12.7 us
    pallas_call x1, Pallas kernels: 7.75 us -> 9.2 us  [start_step(): pl.pallas_call(lambda *refs: start_kernel(*refs, substeps=substeps), in_s...]
where the time goes in v11:
time: 39.6 us; the launch traced here: 39.3 us
  blocking collectives  14.7 us (37%)
  Pallas kernels  12.7 us (32%)
  waiting for transfers between devices  7.23 us (18%)
  starting transfers between devices  2.57 us (6%)
  between operations  0.69 us (2%)
  local copies, waits for them, and re-layouts  0.66 us (2%)
  matrix products  0.55 us (1%)
    all_to_all x1, blocking collectives, local(): received = lax.all_to_all(first_sent, ('group', 'strip'), 0, 0, tiled=True)  14.7 us
    pallas_call x1, Pallas kernels, start_step(): pl.pallas_call(lambda *refs: start_kernel(*refs, substeps=substeps), in_s...  9.2 us
    all_to_all x1, waiting for transfers between devices, local(): received = lax.all_to_all(sent, ('group', 'strip'), 0, 0, tiled=True)  7.23 us
    pallas_call x1, Pallas kernels, second_step(): pl.pallas_call(lambda *refs: second_kernel(*refs, substeps=substeps, node...  3.53 us
    all_to_all x1, starting transfers between devices, local(): received = lax.all_to_all(sent, ('group', 'strip'), 0, 0, tiled=True)  2.57 us
  transfers between devices with their start and end apart: 1, of which 1 were waited for; matrix products, arithmetic and copies ran while one was open for 0% of the time, Pallas kernels for 0%

profile of v11, /device:TPU:0, one launch (start us, length us, event | category | flops | bytes accessed | tf_op | source)
XLA Modules:
  0.0 39.3 jit_solution(1428809217900627148)
XLA Ops:
  0.6 9.2 %start_step.1 = (f32[1024,32]{1,0:T(8,128)}, f32[2,128,128]{2,1,0:T(8,128)}, f32[64,48]{1,0:T(8,128)}) custom-call(s32[1,4]{1,0:T(1,128)} %refs_0_.1, s32[32]{0:T(128)} %bitcast.20, s32[1,32]{1,0:T(1,128)} %bitcast.18, f32[64,2]{1,0:T(8,128)} %constant.57.clone.refs_3_.refs_2_, f32[1,8,128,128]{3,2,1,0:T(8,128)} %refs_4_.2, f32[1,7,128,128]{3,2,1,0:T(8,128)} %refs_5_.2, ...), custom_call_target="tpu_custom_call" | custom-call | tf_op jit(solution)/shard_map/start_step/pallas_call | solution.py:274
  9.8 0.0 copy-start
  9.9 14.7 %all_to_all.23 = f32[32,2,48]{2,1,0:T(2,128)} all-to-all(f32[32,2,48]{2,1,0:T(2,128)} %bitcast.17), channel_id=1, replica_groups=mesh['group'=2,'strip'=16] {'group','strip'}, dimensions={0} | all-to-all | bytes 24576 | tf_op jit(solution)/shard_map/all_to_all | solution.py:380
  24.5 3.5 %second_step.1 = (f32[2,128,128]{2,1,0:T(8,128)}, f32[64,16]{1,0:T(8,128)}) custom-call(f32[64,48]{1,0:T(8,128)} %bitcast.15, s32[1,32]{1,0:T(1,128)} %bitcast.19, f32[64,2]{1,0:T(8,128)} %constant.57.clone.refs_3_.refs_2_, f32[2,64]{1,0:T(2,128)} %constant.58.clone.refs_3_, f32[16,16]{1,0:T(8,128)} %constant.59.clone.refs_4_, f32[3,2,128,128]{3,2,1,0:T(8,128)} %refs_5_.3, ...), custom_call_target="tpu_custom_call" | custom-call | tf_op jit(solution)/shard_map/second_step/pallas_call | solution.py:351
  28.1 2.6 %all-to-all-start.1 = ((f32[32,2,16]{2,1,0:T(2,128)}), f32[32,2,16]{2,1,0:T(2,128)S(1)}, u32[]{:S(2)}, u32[]{:S(2)}) async-start(f32[32,2,16]{2,1,0:T(2,128)} %bitcast.16), calls=%async_computation.1 | async-start | bytes 65536 | tf_op jit(solution)/shard_map/all_to_all | solution.py:382
  30.6 7.2 %all-to-all-done.1 = f32[32,2,16]{2,1,0:T(2,128)S(1)} async-done(((f32[32,2,16]{2,1,0:T(2,128)}), f32[32,2,16]{2,1,0:T(2,128)S(1)}, u32[]{:S(2)}, u32[]{:S(2)}) %all-to-all-start.1) | async-done | bytes 4128 | tf_op jit(solution)/shard_map/all_to_all | solution.py:382
  37.9 0.1 slice_reduce_fusion
  38.0 0.0 copy-done
  38.0 0.5 %fusion.2 = f32[16,1024]{1,0:T(8,128)S(1)} fusion(f32[1024,32]{1,0:T(8,128)S(1)} %copy-done, f32[64,16]{1,0:T(8,128)S(1)} %bitcast.14, s32[]{:T(128)S(6)} %select_n.3), kind=kOutput, calls=%fused_computation.4 | convolution fusion | flops 6291456 | bytes 606212 | tf_op jit(solution)/shard_map/dot_general | solution.py:385
  38.6 0.1 fusion.1
  38.6 0.0 copy-start.1
  38.6 0.6 %copy-done.1 = f32[1,16,1024]{2,1,0:T(8,128)} copy-done((f32[1,16,1024]{2,1,0:T(8,128)}, f32[1,16,1024]{2,1,0:T(8,128)S(1)}, u32[]{:S(2)}) %copy-start.1) | copy-done | bytes 65560
  (3 shorter events, 0.0 us)
Async XLA Ops:
  9.8 28.1 %copy-start = (f32[1024,32]{1,0:T(8,128)S(1)}, f32[1024,32]{1,0:T(8,128)}, u32[]{:S(2)}) copy-start(f32[1024,32]{1,0:T(8,128)} %get-tuple-element.23) | copy-start | bytes 393220
  28.1 9.8 %all-to-all-start.1 = ((f32[32,2,16]{2,1,0:T(2,128)}), f32[32,2,16]{2,1,0:T(2,128)S(1)}, u32[]{:S(2)}, u32[]{:S(2)}) async-start(f32[32,2,16]{2,1,0:T(2,128)} %bitcast.16), calls=%async_computation.1 | async-start | bytes 65536 | tf_op jit(solution)/shard_map/all_to_all | solution.py:382
  38.6 0.6 %copy-start.1 = (f32[1,16,1024]{2,1,0:T(8,128)}, f32[1,16,1024]{2,1,0:T(8,128)S(1)}, u32[]{:S(2)}) copy-start(f32[1,16,1024]{2,1,0:T(8,128)S(1)} %fusion.1) | copy-start | bytes 196612

commit v12 on v10

--- a/solution.py
+++ b/solution.py
@@ -206,15 +206,19 @@
         node = block_index * block_size + lax.broadcasted_iota(jnp.int32, (block_size, strips), 0)
         return (node == node_row).astype(jnp.float32) * owned_row
 
+    def product(left, right):
+        return jnp.dot(left, right, precision=EXACT_DOT, preferred_element_type=jnp.float32)
+
+    forward = [None] + [product(lower_ref[0, i - 1], pivot_ref[0, i - 1]) for i in range(1, block_count)]
+    backward = [product(pivot_ref[0, i], upper_ref[0, i]) for i in range(block_count - 1)]
     carried = [unit_load(0)]
     for block_index in range(1, block_count):
-        pivoted = apply(pivot_ref[0, block_index - 1], carried[-1])
-        carried.append(unit_load(block_index) - apply(lower_ref[0, block_index - 1], pivoted))
-    solved = apply(pivot_ref[0, block_count - 1], carried[-1])
+        carried.append(unit_load(block_index) - apply(forward[block_index], carried[-1]))
+    pivoted = [apply(pivot_ref[0, i], carried[i]) for i in range(block_count)]
+    solved = pivoted[block_count - 1]
     response_ref[(block_count - 1) * block_size:, :] = solved
     for block_index in range(block_count - 2, -1, -1):
-        remainder = carried[block_index] - apply(upper_ref[0, block_index], solved)
-        solved = apply(pivot_ref[0, block_index], remainder)
+        solved = pivoted[block_index] - apply(backward[block_index], solved)
         response_ref[block_index * block_size:(block_index + 1) * block_size, :] = solved
 
     _, _, lift_kernel, drag_kernel = kernel_planes(fields_ref.shape[-1])

time: 38 us -> 36.5 us (0.961)
  Pallas kernels: 11.3 us -> 9.69 us
    pallas_call x1, Pallas kernels: 7.75 us -> 6.16 us  [start_step(): pl.pallas_call(lambda *refs: start_kernel(*refs, substeps=substeps), in_s...]
where the time goes in v12:
time: 36.5 us; the launch traced here: 36.2 us
  blocking collectives  14.7 us (40%)
  Pallas kernels  9.69 us (27%)
  waiting for transfers between devices  7.23 us (20%)
  starting transfers between devices  2.57 us (7%)
  between operations  0.67 us (2%)
  local copies, waits for them, and re-layouts  0.66 us (2%)
  matrix products  0.55 us (2%)
    all_to_all x1, blocking collectives, local(): received = lax.all_to_all(first_sent, ('group', 'strip'), 0, 0, tiled=True)  14.7 us
    all_to_all x1, waiting for transfers between devices, local(): received = lax.all_to_all(sent, ('group', 'strip'), 0, 0, tiled=True)  7.23 us
    pallas_call x1, Pallas kernels, start_step(): pl.pallas_call(lambda *refs: start_kernel(*refs, substeps=substeps), in_s...  6.16 us
    pallas_call x1, Pallas kernels, second_step(): pl.pallas_call(lambda *refs: second_kernel(*refs, substeps=substeps, node...  3.53 us
    all_to_all x1, starting transfers between devices, local(): received = lax.all_to_all(sent, ('group', 'strip'), 0, 0, tiled=True)  2.57 us
  transfers between devices with their start and end apart: 1, of which 1 were waited for; matrix products, arithmetic and copies ran while one was open for 0% of the time, Pallas kernels for 0%

profile of v12, /device:TPU:0, one launch (start us, length us, event | category | flops | bytes accessed | tf_op | source)
XLA Modules:
  0.0 36.2 jit_solution(17954148479931585655)
XLA Ops:
  0.6 6.2 %start_step.1 = (f32[1024,32]{1,0:T(8,128)}, f32[2,128,128]{2,1,0:T(8,128)}, f32[64,48]{1,0:T(8,128)}) custom-call(s32[1,4]{1,0:T(1,128)} %refs_0_.1, s32[32]{0:T(128)} %bitcast.20, s32[1,32]{1,0:T(1,128)} %bitcast.18, f32[64,2]{1,0:T(8,128)} %constant.57.clone.refs_3_.refs_2_, f32[1,8,128,128]{3,2,1,0:T(8,128)} %refs_4_.2, f32[1,7,128,128]{3,2,1,0:T(8,128)} %refs_5_.2, ...), custom_call_target="tpu_custom_call" | custom-call | tf_op jit(solution)/shard_map/start_step/pallas_call | solution.py:258
  6.8 0.0 copy-start
  6.8 14.7 %all_to_all.23 = f32[32,2,48]{2,1,0:T(2,128)} all-to-all(f32[32,2,48]{2,1,0:T(2,128)} %bitcast.17), channel_id=1, replica_groups=mesh['group'=2,'strip'=16] {'group','strip'}, dimensions={0} | all-to-all | bytes 24576 | tf_op jit(solution)/shard_map/all_to_all | solution.py:358
  21.5 3.5 %second_step.1 = (f32[2,128,128]{2,1,0:T(8,128)}, f32[64,16]{1,0:T(8,128)}) custom-call(f32[64,48]{1,0:T(8,128)} %bitcast.15, s32[1,32]{1,0:T(1,128)} %bitcast.19, f32[64,2]{1,0:T(8,128)} %constant.57.clone.refs_3_.refs_2_, f32[2,64]{1,0:T(2,128)} %constant.58.clone.refs_3_, f32[16,16]{1,0:T(8,128)} %constant.59.clone.refs_4_, f32[3,2,128,128]{3,2,1,0:T(8,128)} %refs_5_.3, ...), custom_call_target="tpu_custom_call" | custom-call | tf_op jit(solution)/shard_map/second_step/pallas_call | solution.py:329
  25.0 2.6 %all-to-all-start.1 = ((f32[32,2,16]{2,1,0:T(2,128)}), f32[32,2,16]{2,1,0:T(2,128)S(1)}, u32[]{:S(2)}, u32[]{:S(2)}) async-start(f32[32,2,16]{2,1,0:T(2,128)} %bitcast.16), calls=%async_computation.1 | async-start | bytes 65536 | tf_op jit(solution)/shard_map/all_to_all | solution.py:360
  27.6 7.2 %all-to-all-done.1 = f32[32,2,16]{2,1,0:T(2,128)S(1)} async-done(((f32[32,2,16]{2,1,0:T(2,128)}), f32[32,2,16]{2,1,0:T(2,128)S(1)}, u32[]{:S(2)}, u32[]{:S(2)}) %all-to-all-start.1) | async-done | bytes 4128 | tf_op jit(solution)/shard_map/all_to_all | solution.py:360
  34.8 0.1 slice_reduce_fusion
  34.9 0.0 copy-done
  34.9 0.5 %fusion.2 = f32[16,1024]{1,0:T(8,128)S(1)} fusion(f32[1024,32]{1,0:T(8,128)S(1)} %copy-done, f32[64,16]{1,0:T(8,128)S(1)} %bitcast.14, s32[]{:T(128)S(6)} %select_n.3), kind=kOutput, calls=%fused_computation.4 | convolution fusion | flops 6291456 | bytes 606212 | tf_op jit(solution)/shard_map/dot_general | solution.py:363
  35.5 0.1 fusion.1
  35.6 0.0 copy-start.1
  35.6 0.6 %copy-done.1 = f32[1,16,1024]{2,1,0:T(8,128)} copy-done((f32[1,16,1024]{2,1,0:T(8,128)}, f32[1,16,1024]{2,1,0:T(8,128)S(1)}, u32[]{:S(2)}) %copy-start.1) | copy-done | bytes 65560
  (3 shorter events, 0.0 us)
Async XLA Ops:
  6.8 28.1 %copy-start = (f32[1024,32]{1,0:T(8,128)S(1)}, f32[1024,32]{1,0:T(8,128)}, u32[]{:S(2)}) copy-start(f32[1024,32]{1,0:T(8,128)} %get-tuple-element.23) | copy-start | bytes 393220
  25.0 9.8 %all-to-all-start.1 = ((f32[32,2,16]{2,1,0:T(2,128)}), f32[32,2,16]{2,1,0:T(2,128)S(1)}, u32[]{:S(2)}, u32[]{:S(2)}) async-start(f32[32,2,16]{2,1,0:T(2,128)} %bitcast.16), calls=%async_computation.1 | async-start | bytes 65536 | tf_op jit(solution)/shard_map/all_to_all | solution.py:360
  35.6 0.6 %copy-start.1 = (f32[1,16,1024]{2,1,0:T(8,128)}, f32[1,16,1024]{2,1,0:T(8,128)S(1)}, u32[]{:S(2)}) copy-start(f32[1,16,1024]{2,1,0:T(8,128)S(1)} %fusion.1) | copy-start | bytes 196612

commit v13 on v12

--- a/solution.py
+++ b/solution.py
@@ -337,6 +337,33 @@
     )(received, strip_node[None, :], spread, np.ascontiguousarray(spread.T), difference_matrix(substeps), strip_fields, vorticity)
 
 
+def finish_kernel(received_ref, response_ref, out_ref, *, substeps):
+    group_position = lax.axis_index("group")
+    total_strips = received_ref.shape[0]
+    node_count, strips = response_ref.shape
+    rows = 2 * substeps
+    offset = jnp.sum(received_ref[...], axis=0, keepdims=True) / jnp.sqrt(jnp.float32(total_strips))
+    group_force = received_ref[pl.ds(group_position * strips, strips), :]
+    displacement = lax.dot_general(
+        group_force, response_ref[...], (((0,), (1,)), ((), ())),
+        precision=EXACT_DOT, preferred_element_type=jnp.float32,
+    )
+    diagonal = lax.broadcasted_iota(jnp.int32, (rows, rows), 0) == lax.broadcasted_iota(jnp.int32, (rows, rows), 1)
+    offset_col = jnp.sum(jnp.where(diagonal, offset, 0.0), axis=1, keepdims=True)
+    taper = 1.0 - lax.broadcasted_iota(jnp.int32, (1, node_count), 1).astype(jnp.float32) / node_count
+    row = lax.broadcasted_iota(jnp.int32, (rows, node_count), 0)
+    out_ref[0] = displacement + jnp.where(row >= substeps, offset_col * taper, 0.0)
+
+
+def finish_step(received, unit_response, substeps):
+    node_count = unit_response.shape[0]
+    return pl.pallas_call(
+        lambda *refs: finish_kernel(*refs, substeps=substeps),
+        out_shape=jax.ShapeDtypeStruct((1, 2 * substeps, node_count), jnp.float32),
+        name="finish_step",
+    )(received, unit_response)
+
+
 def local(strip_fields, strip_riser, strip_node, riser_owner, pivot_inv, lower_block, upper_block):
     position = lax.axis_index("strip")
     group_position = lax.axis_index("group")
@@ -358,13 +385,8 @@
     received = lax.all_to_all(first_sent, ("group", "strip"), 0, 0, tiled=True)
     vorticity, sent = second_step(received, strip_node, strip_fields, first_vorticity, devices, node_count, substeps)
     received = lax.all_to_all(sent, ("group", "strip"), 0, 0, tiled=True)
-    offset = jnp.sum(received[:, substeps:], axis=0) / jnp.sqrt(jnp.float32(total_strips))
-    group_force = lax.dynamic_slice_in_dim(received, group_position * group_strips, group_strips)
-    displacement = lax.dot_general(
-        group_force, unit_response, (((0,), (1,)), ((), ())), precision=EXACT_DOT
-    )
-    displacement = displacement.at[substeps:, :].add(offset[:, None] * top_taper[None, :])
-    return (vorticity, displacement[None])
+    displacement = finish_step(received, unit_response, substeps)
+    return (vorticity, displacement)
 
 
 def solution(mesh):

time: 36.5 us -> 38 us (1.041)
  blocking collectives: 14.7 us -> 25.2 us
  waiting for transfers between devices: 7.23 us -> 0 us
  starting transfers between devices: 2.57 us -> 0 us
  Pallas kernels: 9.69 us -> 12 us
  local copies, waits for them, and re-layouts: 0.66 us -> 0 us
  matrix products: 0.55 us -> 0 us
    all_to_all x0 -> x1, blocking collectives: none -> 10.5 us  [local(): received = lax.all_to_all(sent, ('group', 'strip'), 0, 0, tiled=True)]
    all_to_all x1 -> x0, waiting for transfers between devices: 7.23 us -> none  [local(): received = lax.all_to_all(sent, ('group', 'strip'), 0, 0, tiled=True)]
    all_to_all x1 -> x0, starting transfers between devices: 2.57 us -> none  [local(): received = lax.all_to_all(sent, ('group', 'strip'), 0, 0, tiled=True)]
    pallas_call x0 -> x1, Pallas kernels: none -> 2.27 us  [finish_step(): pl.pallas_call(lambda *refs: finish_kernel(*refs, substeps=substeps), out...]
    unnamed x5 -> x0, local copies, waits for them, and re-layouts: 0.66 us -> none
    dot_general x1 -> x0, matrix products: 0.55 us -> none  [local(): lax.dot_general(group_force, unit_response, (((0,), (1,)), ((), ())), pre...]
  transfers between devices with their start and end apart: 1 -> 0, of which waited for: 1 -> 0; matrix products, arithmetic and copies ran while one was open for 0% -> 0% of each run, Pallas kernels for 0% -> 0%
where the time goes in v13:
time: 38 us; the launch traced here: 37.8 us
  blocking collectives  25.2 us (66%)
  Pallas kernels  12 us (32%)
  between operations  0.63 us (2%)
    all_to_all x1, blocking collectives, local(): received = lax.all_to_all(first_sent, ('group', 'strip'), 0, 0, tiled=True)  14.7 us
    all_to_all x1, blocking collectives, local(): received = lax.all_to_all(sent, ('group', 'strip'), 0, 0, tiled=True)  10.5 us
    pallas_call x1, Pallas kernels, start_step(): pl.pallas_call(lambda *refs: start_kernel(*refs, substeps=substeps), in_s...  6.16 us
    pallas_call x1, Pallas kernels, second_step(): pl.pallas_call(lambda *refs: second_kernel(*refs, substeps=substeps, node...  3.53 us
    pallas_call x1, Pallas kernels, finish_step(): pl.pallas_call(lambda *refs: finish_kernel(*refs, substeps=substeps), out...  2.27 us

profile of v13, /device:TPU:0, one launch (start us, length us, event | category | flops | bytes accessed | tf_op | source)
XLA Modules:
  0.0 37.8 jit_solution(9793973607134482768)
XLA Ops:
  0.6 6.2 %start_step.1 = (f32[1024,32]{1,0:T(8,128)}, f32[2,128,128]{2,1,0:T(8,128)}, f32[64,48]{1,0:T(8,128)}) custom-call(s32[1,4]{1,0:T(1,128)} %refs_0_.1, s32[32]{0:T(128)} %bitcast.12, s32[1,32]{1,0:T(1,128)} %bitcast.10, f32[64,2]{1,0:T(8,128)} %constant.6.clone.refs_3_.refs_2_, f32[1,8,128,128]{3,2,1,0:T(8,128)} %refs_4_.2, f32[1,7,128,128]{3,2,1,0:T(8,128)} %refs_5_.2, ...), custom_call_target="tpu_custom_call" | custom-call | tf_op jit(solution)/shard_map/start_step/pallas_call | solution.py:258
  6.8 14.7 %all_to_all.22 = f32[32,2,48]{2,1,0:T(2,128)} all-to-all(f32[32,2,48]{2,1,0:T(2,128)} %bitcast.9), channel_id=1, replica_groups=mesh['group'=2,'strip'=16] {'group','strip'}, dimensions={0} | all-to-all | bytes 24576 | tf_op jit(solution)/shard_map/all_to_all | solution.py:385
  21.5 3.5 %second_step.1 = (f32[2,128,128]{2,1,0:T(8,128)}, f32[64,16]{1,0:T(8,128)}) custom-call(f32[64,48]{1,0:T(8,128)} %bitcast.7, s32[1,32]{1,0:T(1,128)} %bitcast.11, f32[64,2]{1,0:T(8,128)} %constant.6.clone.refs_3_.refs_2_, f32[2,64]{1,0:T(2,128)} %constant.7.clone.refs_3_, f32[16,16]{1,0:T(8,128)} %constant.8.clone.refs_4_, f32[3,2,128,128]{3,2,1,0:T(8,128)} %refs_5_.3, ...), custom_call_target="tpu_custom_call" | custom-call | tf_op jit(solution)/shard_map/second_step/pallas_call | solution.py:329
  25.0 10.5 %all_to_all.23 = f32[32,2,16]{2,1,0:T(2,128)} all-to-all(f32[32,2,16]{2,1,0:T(2,128)} %bitcast.8), channel_id=1, replica_groups=mesh['group'=2,'strip'=16] {'group','strip'}, dimensions={0} | all-to-all | bytes 8192 | tf_op jit(solution)/shard_map/all_to_all | solution.py:387
  35.5 2.3 %finish_step.1 = f32[1,16,1024]{2,1,0:T(8,128)} custom-call(f32[64,16]{1,0:T(8,128)} %bitcast.6, f32[1024,32]{1,0:T(8,128)} %get-tuple-element.11.refs_1_), custom_call_target="tpu_custom_call" | custom-call | tf_op jit(solution)/shard_map/finish_step/pallas_call | solution.py:360

commit v14 on v12

--- a/solution.py
+++ b/solution.py
@@ -87,21 +87,23 @@
     rows_across, cols_across = vorticity.shape
     lane = lax.broadcasted_iota(jnp.int32, (1, 2 * substeps), 1)
     row = jnp.zeros((1, 2 * substeps), jnp.float32)
+    along_x = (TIME_STEP * 0.5) * flow_x
+    along_y = (TIME_STEP * 0.5) * flow_y
     for substep in range(substeps):
         right_cell = pltpu.roll(vorticity, cols_across - 1, 1)
         left_cell = pltpu.roll(vorticity, 1, 1)
         upper_cell = pltpu.roll(vorticity, rows_across - 1, 0)
         lower_cell = pltpu.roll(vorticity, 1, 0)
-        laplacian = right_cell + left_cell + upper_cell + lower_cell - 4.0 * vorticity
-        tendency = (
-            VISCOSITY * laplacian
-            - flow_x * (0.5 * (right_cell - left_cell))
-            - flow_y * (0.5 * (upper_cell - lower_cell))
+        laplacian = (right_cell + left_cell) + (upper_cell + lower_cell) - 4.0 * vorticity
+        step = (
+            (TIME_STEP * VISCOSITY) * laplacian
+            - along_x * (right_cell - left_cell)
+            - along_y * (upper_cell - lower_cell)
         )
         if forcing_of is None:
-            vorticity = vorticity + TIME_STEP * tendency
+            vorticity = vorticity + step
         else:
-            vorticity = vorticity + TIME_STEP * tendency + COUPLING * forcing_of(substep)
+            vorticity = vorticity + step + forcing_of(substep)
         lift = jnp.sum(jnp.sum(vorticity * lift_kernel, axis=0, keepdims=True), axis=1, keepdims=True)
         drag = jnp.sum(jnp.sum(vorticity * drag_kernel, axis=0, keepdims=True), axis=1, keepdims=True)
         row = row + jnp.where(lane == substep, lift, 0.0) + jnp.where(lane == substeps + substep, drag, 0.0)
@@ -113,7 +115,7 @@
     source_x, source_y, lift_kernel, drag_kernel = kernel_planes(vorticity_ref.shape[-1])
 
     def forcing_of(substep):
-        return (
+        return COUPLING * (
             velocity_ref[strip, substep] * source_x
             - velocity_ref[strip, substeps + substep] * source_y
         )
@@ -296,6 +298,8 @@
     velocity = jnp.dot(motion, difference_ref[...], precision=EXACT_DOT, preferred_element_type=jnp.float32)
 
     source_x, source_y, lift_kernel, drag_kernel = kernel_planes(fields_ref.shape[-1])
+    coupled_x = COUPLING * source_x
+    coupled_y = COUPLING * source_y
     rows = jnp.zeros((per_device, 2 * substeps), jnp.float32)
     for strip in range(per_device):
         picks = [
@@ -304,7 +308,7 @@
         ]
 
         def forcing_of(substep, picks=picks):
-            return picks[substep] * source_x - picks[substeps + substep] * source_y
+            return picks[substep] * coupled_x - picks[substeps + substep] * coupled_y
 
         vorticity, row = run_substeps(
             vorticity_ref[strip], fields_ref[1, strip], fields_ref[2, strip], forcing_of,

time: 36.5 us -> 36.5 us (level)
  no operation moved by 1% of the time
where the time goes in v14:
time: 36.5 us; the launch traced here: 36.3 us
  blocking collectives  14.7 us (40%)
  Pallas kernels  9.74 us (27%)
  waiting for transfers between devices  7.23 us (20%)
  starting transfers between devices  2.57 us (7%)
  between operations  0.67 us (2%)
  local copies, waits for them, and re-layouts  0.66 us (2%)
  matrix products  0.55 us (2%)
    all_to_all x1, blocking collectives, local(): received = lax.all_to_all(first_sent, ('group', 'strip'), 0, 0, tiled=True)  14.7 us
    all_to_all x1, waiting for transfers between devices, local(): received = lax.all_to_all(sent, ('group', 'strip'), 0, 0, tiled=True)  7.23 us
    pallas_call x1, Pallas kernels, start_step(): pl.pallas_call(lambda *refs: start_kernel(*refs, substeps=substeps), in_s...  6.2 us
    pallas_call x1, Pallas kernels, second_step(): pl.pallas_call(lambda *refs: second_kernel(*refs, substeps=substeps, node...  3.54 us
    all_to_all x1, starting transfers between devices, local(): received = lax.all_to_all(sent, ('group', 'strip'), 0, 0, tiled=True)  2.57 us
  transfers between devices with their start and end apart: 1, of which 1 were waited for; matrix products, arithmetic and copies ran while one was open for 0% of the time, Pallas kernels for 0%

profile of v14, /device:TPU:0, one launch (start us, length us, event | category | flops | bytes accessed | tf_op | source)
XLA Modules:
  0.0 36.3 jit_solution(12767002634831349778)
XLA Ops:
  0.6 6.2 %start_step.1 = (f32[1024,32]{1,0:T(8,128)}, f32[2,128,128]{2,1,0:T(8,128)}, f32[64,48]{1,0:T(8,128)}) custom-call(s32[1,4]{1,0:T(1,128)} %refs_0_.1, s32[32]{0:T(128)} %bitcast.20, s32[1,32]{1,0:T(1,128)} %bitcast.18, f32[64,2]{1,0:T(8,128)} %constant.57.clone.refs_3_.refs_2_, f32[1,8,128,128]{3,2,1,0:T(8,128)} %refs_4_.2, f32[1,7,128,128]{3,2,1,0:T(8,128)} %refs_5_.2, ...), custom_call_target="tpu_custom_call" | custom-call | tf_op jit(solution)/shard_map/start_step/pallas_call | solution.py:260
  6.8 0.0 copy-start
  6.8 14.7 %all_to_all.23 = f32[32,2,48]{2,1,0:T(2,128)} all-to-all(f32[32,2,48]{2,1,0:T(2,128)} %bitcast.17), channel_id=1, replica_groups=mesh['group'=2,'strip'=16] {'group','strip'}, dimensions={0} | all-to-all | bytes 24576 | tf_op jit(solution)/shard_map/all_to_all | solution.py:362
  21.5 3.5 %second_step.1 = (f32[2,128,128]{2,1,0:T(8,128)}, f32[64,16]{1,0:T(8,128)}) custom-call(f32[64,48]{1,0:T(8,128)} %bitcast.15, s32[1,32]{1,0:T(1,128)} %bitcast.19, f32[64,2]{1,0:T(8,128)} %constant.57.clone.refs_3_.refs_2_, f32[2,64]{1,0:T(2,128)} %constant.58.clone.refs_3_, f32[16,16]{1,0:T(8,128)} %constant.59.clone.refs_4_, f32[3,2,128,128]{3,2,1,0:T(8,128)} %refs_5_.3, ...), custom_call_target="tpu_custom_call" | custom-call | tf_op jit(solution)/shard_map/second_step/pallas_call | solution.py:333
  25.0 2.6 %all-to-all-start.1 = ((f32[32,2,16]{2,1,0:T(2,128)}), f32[32,2,16]{2,1,0:T(2,128)S(1)}, u32[]{:S(2)}, u32[]{:S(2)}) async-start(f32[32,2,16]{2,1,0:T(2,128)} %bitcast.16), calls=%async_computation.1 | async-start | bytes 65536 | tf_op jit(solution)/shard_map/all_to_all | solution.py:364
  27.6 7.2 %all-to-all-done.1 = f32[32,2,16]{2,1,0:T(2,128)S(1)} async-done(((f32[32,2,16]{2,1,0:T(2,128)}), f32[32,2,16]{2,1,0:T(2,128)S(1)}, u32[]{:S(2)}, u32[]{:S(2)}) %all-to-all-start.1) | async-done | bytes 4128 | tf_op jit(solution)/shard_map/all_to_all | solution.py:364
  34.9 0.1 slice_reduce_fusion
  35.0 0.0 copy-done
  35.0 0.5 %fusion.2 = f32[16,1024]{1,0:T(8,128)S(1)} fusion(f32[1024,32]{1,0:T(8,128)S(1)} %copy-done, f32[64,16]{1,0:T(8,128)S(1)} %bitcast.14, s32[]{:T(128)S(6)} %select_n.3), kind=kOutput, calls=%fused_computation.4 | convolution fusion | flops 6291456 | bytes 606212 | tf_op jit(solution)/shard_map/dot_general | solution.py:367
  35.6 0.1 fusion.1
  35.6 0.0 copy-start.1
  35.6 0.6 %copy-done.1 = f32[1,16,1024]{2,1,0:T(8,128)} copy-done((f32[1,16,1024]{2,1,0:T(8,128)}, f32[1,16,1024]{2,1,0:T(8,128)S(1)}, u32[]{:S(2)}) %copy-start.1) | copy-done | bytes 65560
  (3 shorter events, 0.0 us)
Async XLA Ops:
  6.8 28.1 %copy-start = (f32[1024,32]{1,0:T(8,128)S(1)}, f32[1024,32]{1,0:T(8,128)}, u32[]{:S(2)}) copy-start(f32[1024,32]{1,0:T(8,128)} %get-tuple-element.23) | copy-start | bytes 393220
  25.0 9.8 %all-to-all-start.1 = ((f32[32,2,16]{2,1,0:T(2,128)}), f32[32,2,16]{2,1,0:T(2,128)S(1)}, u32[]{:S(2)}, u32[]{:S(2)}) async-start(f32[32,2,16]{2,1,0:T(2,128)} %bitcast.16), calls=%async_computation.1 | async-start | bytes 65536 | tf_op jit(solution)/shard_map/all_to_all | solution.py:364
  35.6 0.6 %copy-start.1 = (f32[1,16,1024]{2,1,0:T(8,128)}, f32[1,16,1024]{2,1,0:T(8,128)S(1)}, u32[]{:S(2)}) copy-start(f32[1,16,1024]{2,1,0:T(8,128)S(1)} %fusion.1) | copy-start | bytes 196612

commit v15 on v14

--- a/solution.py
+++ b/solution.py
@@ -209,7 +209,7 @@
         return (node == node_row).astype(jnp.float32) * owned_row
 
     def product(left, right):
-        return jnp.dot(left, right, precision=EXACT_DOT, preferred_element_type=jnp.float32)
+        return jnp.dot(left, right, precision=lax.Precision.HIGH, preferred_element_type=jnp.float32)
 
     forward = [None] + [product(lower_ref[0, i - 1], pivot_ref[0, i - 1]) for i in range(1, block_count)]
     backward = [product(pivot_ref[0, i], upper_ref[0, i]) for i in range(block_count - 1)]

time: 36.5 us -> 36.1 us (0.989)
  Pallas kernels: 9.74 us -> 9.33 us
    pallas_call x1, Pallas kernels: 6.2 us -> 5.8 us  [start_step(): pl.pallas_call(lambda *refs: start_kernel(*refs, substeps=substeps), in_s...]
where the time goes in v15:
time: 36.1 us; the launch traced here: 35.9 us
  blocking collectives  14.7 us (41%)
  Pallas kernels  9.33 us (26%)
  waiting for transfers between devices  7.23 us (20%)
  starting transfers between devices  2.57 us (7%)
  between operations  0.67 us (2%)
  local copies, waits for them, and re-layouts  0.66 us (2%)
  matrix products  0.55 us (2%)
    all_to_all x1, blocking collectives, local(): received = lax.all_to_all(first_sent, ('group', 'strip'), 0, 0, tiled=True)  14.7 us
    all_to_all x1, waiting for transfers between devices, local(): received = lax.all_to_all(sent, ('group', 'strip'), 0, 0, tiled=True)  7.23 us
    pallas_call x1, Pallas kernels, start_step(): pl.pallas_call(lambda *refs: start_kernel(*refs, substeps=substeps), in_s...  5.8 us
    pallas_call x1, Pallas kernels, second_step(): pl.pallas_call(lambda *refs: second_kernel(*refs, substeps=substeps, node...  3.53 us
    all_to_all x1, starting transfers between devices, local(): received = lax.all_to_all(sent, ('group', 'strip'), 0, 0, tiled=True)  2.57 us
  transfers between devices with their start and end apart: 1, of which 1 were waited for; matrix products, arithmetic and copies ran while one was open for 0% of the time, Pallas kernels for 0%

profile of v15, /device:TPU:0, one launch (start us, length us, event | category | flops | bytes accessed | tf_op | source)
XLA Modules:
  0.0 35.9 jit_solution(6383438112687968408)
XLA Ops:
  0.6 5.8 %start_step.1 = (f32[1024,32]{1,0:T(8,128)}, f32[2,128,128]{2,1,0:T(8,128)}, f32[64,48]{1,0:T(8,128)}) custom-call(s32[1,4]{1,0:T(1,128)} %refs_0_.1, s32[32]{0:T(128)} %bitcast.20, s32[1,32]{1,0:T(1,128)} %bitcast.18, f32[64,2]{1,0:T(8,128)} %constant.57.clone.refs_3_.refs_2_, f32[1,8,128,128]{3,2,1,0:T(8,128)} %refs_4_.2, f32[1,7,128,128]{3,2,1,0:T(8,128)} %refs_5_.2, ...), custom_call_target="tpu_custom_call" | custom-call | tf_op jit(solution)/shard_map/start_step/pallas_call | solution.py:260
  6.4 0.0 copy-start
  6.4 14.7 %all_to_all.23 = f32[32,2,48]{2,1,0:T(2,128)} all-to-all(f32[32,2,48]{2,1,0:T(2,128)} %bitcast.17), channel_id=1, replica_groups=mesh['group'=2,'strip'=16] {'group','strip'}, dimensions={0} | all-to-all | bytes 24576 | tf_op jit(solution)/shard_map/all_to_all | solution.py:362
  21.1 3.5 %second_step.1 = (f32[2,128,128]{2,1,0:T(8,128)}, f32[64,16]{1,0:T(8,128)}) custom-call(f32[64,48]{1,0:T(8,128)} %bitcast.15, s32[1,32]{1,0:T(1,128)} %bitcast.19, f32[64,2]{1,0:T(8,128)} %constant.57.clone.refs_3_.refs_2_, f32[2,64]{1,0:T(2,128)} %constant.58.clone.refs_3_, f32[16,16]{1,0:T(8,128)} %constant.59.clone.refs_4_, f32[3,2,128,128]{3,2,1,0:T(8,128)} %refs_5_.3, ...), custom_call_target="tpu_custom_call" | custom-call | tf_op jit(solution)/shard_map/second_step/pallas_call | solution.py:333
  24.6 2.6 %all-to-all-start.1 = ((f32[32,2,16]{2,1,0:T(2,128)}), f32[32,2,16]{2,1,0:T(2,128)S(1)}, u32[]{:S(2)}, u32[]{:S(2)}) async-start(f32[32,2,16]{2,1,0:T(2,128)} %bitcast.16), calls=%async_computation.1 | async-start | bytes 65536 | tf_op jit(solution)/shard_map/all_to_all | solution.py:364
  27.2 7.2 %all-to-all-done.1 = f32[32,2,16]{2,1,0:T(2,128)S(1)} async-done(((f32[32,2,16]{2,1,0:T(2,128)}), f32[32,2,16]{2,1,0:T(2,128)S(1)}, u32[]{:S(2)}, u32[]{:S(2)}) %all-to-all-start.1) | async-done | bytes 4128 | tf_op jit(solution)/shard_map/all_to_all | solution.py:364
  34.5 0.1 slice_reduce_fusion
  34.6 0.0 copy-done
  34.6 0.5 %fusion.2 = f32[16,1024]{1,0:T(8,128)S(1)} fusion(f32[1024,32]{1,0:T(8,128)S(1)} %copy-done, f32[64,16]{1,0:T(8,128)S(1)} %bitcast.14, s32[]{:T(128)S(6)} %select_n.3), kind=kOutput, calls=%fused_computation.4 | convolution fusion | flops 6291456 | bytes 606212 | tf_op jit(solution)/shard_map/dot_general | solution.py:367
  35.2 0.1 fusion.1
  35.2 0.0 copy-start.1
  35.2 0.6 %copy-done.1 = f32[1,16,1024]{2,1,0:T(8,128)} copy-done((f32[1,16,1024]{2,1,0:T(8,128)}, f32[1,16,1024]{2,1,0:T(8,128)S(1)}, u32[]{:S(2)}) %copy-start.1) | copy-done | bytes 65560
  (3 shorter events, 0.0 us)
Async XLA Ops:
  6.4 28.1 %copy-start = (f32[1024,32]{1,0:T(8,128)S(1)}, f32[1024,32]{1,0:T(8,128)}, u32[]{:S(2)}) copy-start(f32[1024,32]{1,0:T(8,128)} %get-tuple-element.23) | copy-start | bytes 393220
  24.6 9.8 %all-to-all-start.1 = ((f32[32,2,16]{2,1,0:T(2,128)}), f32[32,2,16]{2,1,0:T(2,128)S(1)}, u32[]{:S(2)}, u32[]{:S(2)}) async-start(f32[32,2,16]{2,1,0:T(2,128)} %bitcast.16), calls=%async_computation.1 | async-start | bytes 65536 | tf_op jit(solution)/shard_map/all_to_all | solution.py:364
  35.2 0.6 %copy-start.1 = (f32[1,16,1024]{2,1,0:T(8,128)}, f32[1,16,1024]{2,1,0:T(8,128)S(1)}, u32[]{:S(2)}) copy-start(f32[1,16,1024]{2,1,0:T(8,128)S(1)} %fusion.1) | copy-start | bytes 196612

commit v16 on v15

--- a/solution.py
+++ b/solution.py
@@ -302,10 +302,7 @@
     coupled_y = COUPLING * source_y
     rows = jnp.zeros((per_device, 2 * substeps), jnp.float32)
     for strip in range(per_device):
-        picks = [
-            jnp.sum(jnp.sum(jnp.where((sublane == strip) & (lane == column), velocity, 0.0), axis=0, keepdims=True), axis=1, keepdims=True)
-            for column in range(2 * substeps)
-        ]
+        picks = [velocity[strip:strip + 1, column:column + 1] for column in range(2 * substeps)]
 
         def forcing_of(substep, picks=picks):
             return picks[substep] * coupled_x - picks[substeps + substep] * coupled_y

time: 36.1 us -> 36.1 us (level)
  no operation moved by 1% of the time
where the time goes in v16:
time: 36.1 us; the launch traced here: 35.9 us
  blocking collectives  14.7 us (41%)
  Pallas kernels  9.36 us (26%)
  waiting for transfers between devices  7.23 us (20%)
  starting transfers between devices  2.57 us (7%)
  between operations  0.67 us (2%)
  local copies, waits for them, and re-layouts  0.66 us (2%)
  matrix products  0.55 us (2%)
    all_to_all x1, blocking collectives, local(): received = lax.all_to_all(first_sent, ('group', 'strip'), 0, 0, tiled=True)  14.7 us
    all_to_all x1, waiting for transfers between devices, local(): received = lax.all_to_all(sent, ('group', 'strip'), 0, 0, tiled=True)  7.23 us
    pallas_call x1, Pallas kernels, start_step(): pl.pallas_call(lambda *refs: start_kernel(*refs, substeps=substeps), in_s...  5.8 us
    pallas_call x1, Pallas kernels, second_step(): pl.pallas_call(lambda *refs: second_kernel(*refs, substeps=substeps, node...  3.56 us
    all_to_all x1, starting transfers between devices, local(): received = lax.all_to_all(sent, ('group', 'strip'), 0, 0, tiled=True)  2.57 us
  transfers between devices with their start and end apart: 1, of which 1 were waited for; matrix products, arithmetic and copies ran while one was open for 0% of the time, Pallas kernels for 0%

profile of v16, /device:TPU:0, one launch (start us, length us, event | category | flops | bytes accessed | tf_op | source)
XLA Modules:
  0.0 35.9 jit_solution(5595617722802473677)
XLA Ops:
  0.6 5.8 %start_step.1 = (f32[1024,32]{1,0:T(8,128)}, f32[2,128,128]{2,1,0:T(8,128)}, f32[64,48]{1,0:T(8,128)}) custom-call(s32[1,4]{1,0:T(1,128)} %refs_0_.1, s32[32]{0:T(128)} %bitcast.20, s32[1,32]{1,0:T(1,128)} %bitcast.18, f32[64,2]{1,0:T(8,128)} %constant.57.clone.refs_3_.refs_2_, f32[1,8,128,128]{3,2,1,0:T(8,128)} %refs_4_.2, f32[1,7,128,128]{3,2,1,0:T(8,128)} %refs_5_.2, ...), custom_call_target="tpu_custom_call" | custom-call | tf_op jit(solution)/shard_map/start_step/pallas_call | solution.py:260
  6.4 0.0 copy-start
  6.4 14.7 %all_to_all.23 = f32[32,2,48]{2,1,0:T(2,128)} all-to-all(f32[32,2,48]{2,1,0:T(2,128)} %bitcast.17), channel_id=1, replica_groups=mesh['group'=2,'strip'=16] {'group','strip'}, dimensions={0} | all-to-all | bytes 24576 | tf_op jit(solution)/shard_map/all_to_all | solution.py:359
  21.1 3.6 %second_step.1 = (f32[2,128,128]{2,1,0:T(8,128)}, f32[64,16]{1,0:T(8,128)}) custom-call(f32[64,48]{1,0:T(8,128)} %bitcast.15, s32[1,32]{1,0:T(1,128)} %bitcast.19, f32[64,2]{1,0:T(8,128)} %constant.57.clone.refs_3_.refs_2_, f32[2,64]{1,0:T(2,128)} %constant.58.clone.refs_3_, f32[16,16]{1,0:T(8,128)} %constant.59.clone.refs_4_, f32[3,2,128,128]{3,2,1,0:T(8,128)} %refs_5_.3, ...), custom_call_target="tpu_custom_call" | custom-call | tf_op jit(solution)/shard_map/second_step/pallas_call | solution.py:330
  24.7 2.6 %all-to-all-start.1 = ((f32[32,2,16]{2,1,0:T(2,128)}), f32[32,2,16]{2,1,0:T(2,128)S(1)}, u32[]{:S(2)}, u32[]{:S(2)}) async-start(f32[32,2,16]{2,1,0:T(2,128)} %bitcast.16), calls=%async_computation.1 | async-start | bytes 65536 | tf_op jit(solution)/shard_map/all_to_all | solution.py:361
  27.3 7.2 %all-to-all-done.1 = f32[32,2,16]{2,1,0:T(2,128)S(1)} async-done(((f32[32,2,16]{2,1,0:T(2,128)}), f32[32,2,16]{2,1,0:T(2,128)S(1)}, u32[]{:S(2)}, u32[]{:S(2)}) %all-to-all-start.1) | async-done | bytes 4128 | tf_op jit(solution)/shard_map/all_to_all | solution.py:361
  34.5 0.1 slice_reduce_fusion
  34.6 0.0 copy-done
  34.6 0.5 %fusion.2 = f32[16,1024]{1,0:T(8,128)S(1)} fusion(f32[1024,32]{1,0:T(8,128)S(1)} %copy-done, f32[64,16]{1,0:T(8,128)S(1)} %bitcast.14, s32[]{:T(128)S(6)} %select_n.3), kind=kOutput, calls=%fused_computation.4 | convolution fusion | flops 6291456 | bytes 606212 | tf_op jit(solution)/shard_map/dot_general | solution.py:364
  35.2 0.1 fusion.1
  35.3 0.0 copy-start.1
  35.3 0.6 %copy-done.1 = f32[1,16,1024]{2,1,0:T(8,128)} copy-done((f32[1,16,1024]{2,1,0:T(8,128)}, f32[1,16,1024]{2,1,0:T(8,128)S(1)}, u32[]{:S(2)}) %copy-start.1) | copy-done | bytes 65560
  (3 shorter events, 0.0 us)
Async XLA Ops:
  6.4 28.2 %copy-start = (f32[1024,32]{1,0:T(8,128)S(1)}, f32[1024,32]{1,0:T(8,128)}, u32[]{:S(2)}) copy-start(f32[1024,32]{1,0:T(8,128)} %get-tuple-element.23) | copy-start | bytes 393220
  24.7 9.8 %all-to-all-start.1 = ((f32[32,2,16]{2,1,0:T(2,128)}), f32[32,2,16]{2,1,0:T(2,128)S(1)}, u32[]{:S(2)}, u32[]{:S(2)}) async-start(f32[32,2,16]{2,1,0:T(2,128)} %bitcast.16), calls=%async_computation.1 | async-start | bytes 65536 | tf_op jit(solution)/shard_map/all_to_all | solution.py:361
  35.3 0.6 %copy-start.1 = (f32[1,16,1024]{2,1,0:T(8,128)}, f32[1,16,1024]{2,1,0:T(8,128)S(1)}, u32[]{:S(2)}) copy-start(f32[1,16,1024]{2,1,0:T(8,128)S(1)} %fusion.1) | copy-start | bytes 196612

commit v17 on v15

--- a/solution.py
+++ b/solution.py
@@ -237,13 +237,13 @@
     node_onehot = (
         node_col == lax.broadcasted_iota(jnp.int32, (strips, node_count), 1).astype(jnp.float32)
     ).astype(jnp.float32)
-    coupling = jnp.dot(node_onehot, response_ref[...], precision=EXACT_DOT, preferred_element_type=jnp.float32)
+    coupling = jnp.dot(node_onehot, response_ref[...], precision=lax.Precision.HIGH, preferred_element_type=jnp.float32)
     coupling = coupling * owned_col
     sent_rows = sent_ref.shape[0]
     place = lax.broadcasted_iota(jnp.int32, (sent_rows, strips), 0) - group_position * strips
     pick = (place == lax.broadcasted_iota(jnp.int32, (sent_rows, strips), 1)).astype(jnp.float32)
-    sent_ref[:, 0:2 * substeps] = jnp.dot(spread_ref[...], rows, precision=EXACT_DOT, preferred_element_type=jnp.float32)
-    sent_ref[:, 2 * substeps:] = jnp.dot(pick, coupling, precision=EXACT_DOT, preferred_element_type=jnp.float32)
+    sent_ref[:, 0:2 * substeps] = jnp.dot(spread_ref[...], rows, precision=lax.Precision.HIGH, preferred_element_type=jnp.float32)
+    sent_ref[:, 2 * substeps:] = jnp.dot(pick, coupling, precision=lax.Precision.HIGH, preferred_element_type=jnp.float32)
 
 
 def spread_matrix(devices, per_device):
@@ -283,9 +283,9 @@
     offset = jnp.sum(every_force, axis=0, keepdims=True) / jnp.sqrt(jnp.float32(total_strips))
     group_force = received_ref[pl.ds(group_position * strips, strips), 0:2 * substeps]
     my_coupling = jnp.dot(
-        gather_ref[...], received_ref[:, 2 * substeps:], precision=EXACT_DOT, preferred_element_type=jnp.float32
-    )
-    motion = jnp.dot(my_coupling, group_force, precision=EXACT_DOT, preferred_element_type=jnp.float32)
+        gather_ref[...], received_ref[:, 2 * substeps:], precision=lax.Precision.HIGH, preferred_element_type=jnp.float32
+    )
+    motion = jnp.dot(my_coupling, group_force, precision=lax.Precision.HIGH, preferred_element_type=jnp.float32)
     mine = (
         lax.broadcasted_iota(jnp.int32, (per_device, strips), 1)
         == position * per_device + lax.broadcasted_iota(jnp.int32, (per_device, strips), 0)
@@ -316,7 +316,7 @@
         )
         out_ref[strip] = vorticity
         rows = jnp.where(sublane == strip, row, rows)
-    sent_ref[...] = jnp.dot(spread_ref[...], rows, precision=EXACT_DOT, preferred_element_type=jnp.float32)
+    sent_ref[...] = jnp.dot(spread_ref[...], rows, precision=lax.Precision.HIGH, preferred_element_type=jnp.float32)
 
 
 def difference_matrix(substeps):

time: 36.1 us -> 35.8 us (level)
  no operation moved by 1% of the time
where the time goes in v17:
time: 35.8 us; the launch traced here: 35.6 us
  blocking collectives  14.7 us (41%)
  Pallas kernels  9.08 us (25%)
  waiting for transfers between devices  7.23 us (20%)
  starting transfers between devices  2.57 us (7%)
  between operations  0.67 us (2%)
  local copies, waits for them, and re-layouts  0.66 us (2%)
  matrix products  0.55 us (2%)
    all_to_all x1, blocking collectives, local(): received = lax.all_to_all(first_sent, ('group', 'strip'), 0, 0, tiled=True)  14.7 us
    all_to_all x1, waiting for transfers between devices, local(): received = lax.all_to_all(sent, ('group', 'strip'), 0, 0, tiled=True)  7.23 us
    pallas_call x1, Pallas kernels, start_step(): pl.pallas_call(lambda *refs: start_kernel(*refs, substeps=substeps), in_s...  5.62 us
    pallas_call x1, Pallas kernels, second_step(): pl.pallas_call(lambda *refs: second_kernel(*refs, substeps=substeps, node...  3.46 us
    all_to_all x1, starting transfers between devices, local(): received = lax.all_to_all(sent, ('group', 'strip'), 0, 0, tiled=True)  2.57 us
  transfers between devices with their start and end apart: 1, of which 1 were waited for; matrix products, arithmetic and copies ran while one was open for 0% of the time, Pallas kernels for 0%

profile of v17, /device:TPU:0, one launch (start us, length us, event | category | flops | bytes accessed | tf_op | source)
XLA Modules:
  0.0 35.6 jit_solution(92175277767234827)
XLA Ops:
  0.6 5.6 %start_step.1 = (f32[1024,32]{1,0:T(8,128)}, f32[2,128,128]{2,1,0:T(8,128)}, f32[64,48]{1,0:T(8,128)}) custom-call(s32[1,4]{1,0:T(1,128)} %refs_0_.1, s32[32]{0:T(128)} %bitcast.20, s32[1,32]{1,0:T(1,128)} %bitcast.18, f32[64,2]{1,0:T(8,128)} %constant.57.clone.refs_3_.refs_2_, f32[1,8,128,128]{3,2,1,0:T(8,128)} %refs_4_.2, f32[1,7,128,128]{3,2,1,0:T(8,128)} %refs_5_.2, ...), custom_call_target="tpu_custom_call" | custom-call | tf_op jit(solution)/shard_map/start_step/pallas_call | solution.py:260
  6.3 0.0 copy-start
  6.3 14.7 %all_to_all.23 = f32[32,2,48]{2,1,0:T(2,128)} all-to-all(f32[32,2,48]{2,1,0:T(2,128)} %bitcast.17), channel_id=1, replica_groups=mesh['group'=2,'strip'=16] {'group','strip'}, dimensions={0} | all-to-all | bytes 24576 | tf_op jit(solution)/shard_map/all_to_all | solution.py:362
  20.9 3.5 %second_step.1 = (f32[2,128,128]{2,1,0:T(8,128)}, f32[64,16]{1,0:T(8,128)}) custom-call(f32[64,48]{1,0:T(8,128)} %bitcast.15, s32[1,32]{1,0:T(1,128)} %bitcast.19, f32[64,2]{1,0:T(8,128)} %constant.57.clone.refs_3_.refs_2_, f32[2,64]{1,0:T(2,128)} %constant.58.clone.refs_3_, f32[16,16]{1,0:T(8,128)} %constant.59.clone.refs_4_, f32[3,2,128,128]{3,2,1,0:T(8,128)} %refs_5_.3, ...), custom_call_target="tpu_custom_call" | custom-call | tf_op jit(solution)/shard_map/second_step/pallas_call | solution.py:333
  24.4 2.6 %all-to-all-start.1 = ((f32[32,2,16]{2,1,0:T(2,128)}), f32[32,2,16]{2,1,0:T(2,128)S(1)}, u32[]{:S(2)}, u32[]{:S(2)}) async-start(f32[32,2,16]{2,1,0:T(2,128)} %bitcast.16), calls=%async_computation.1 | async-start | bytes 65536 | tf_op jit(solution)/shard_map/all_to_all | solution.py:364
  27.0 7.2 %all-to-all-done.1 = f32[32,2,16]{2,1,0:T(2,128)S(1)} async-done(((f32[32,2,16]{2,1,0:T(2,128)}), f32[32,2,16]{2,1,0:T(2,128)S(1)}, u32[]{:S(2)}, u32[]{:S(2)}) %all-to-all-start.1) | async-done | bytes 4128 | tf_op jit(solution)/shard_map/all_to_all | solution.py:364
  34.2 0.1 slice_reduce_fusion
  34.3 0.0 copy-done
  34.3 0.5 %fusion.2 = f32[16,1024]{1,0:T(8,128)S(1)} fusion(f32[1024,32]{1,0:T(8,128)S(1)} %copy-done, f32[64,16]{1,0:T(8,128)S(1)} %bitcast.14, s32[]{:T(128)S(6)} %select_n.3), kind=kOutput, calls=%fused_computation.4 | convolution fusion | flops 6291456 | bytes 606212 | tf_op jit(solution)/shard_map/dot_general | solution.py:367
  34.9 0.1 fusion.1
  35.0 0.0 copy-start.1
  35.0 0.6 %copy-done.1 = f32[1,16,1024]{2,1,0:T(8,128)} copy-done((f32[1,16,1024]{2,1,0:T(8,128)}, f32[1,16,1024]{2,1,0:T(8,128)S(1)}, u32[]{:S(2)}) %copy-start.1) | copy-done | bytes 65560
  (3 shorter events, 0.0 us)
Async XLA Ops:
  6.3 28.0 %copy-start = (f32[1024,32]{1,0:T(8,128)S(1)}, f32[1024,32]{1,0:T(8,128)}, u32[]{:S(2)}) copy-start(f32[1024,32]{1,0:T(8,128)} %get-tuple-element.23) | copy-start | bytes 393220
  24.4 9.8 %all-to-all-start.1 = ((f32[32,2,16]{2,1,0:T(2,128)}), f32[32,2,16]{2,1,0:T(2,128)S(1)}, u32[]{:S(2)}, u32[]{:S(2)}) async-start(f32[32,2,16]{2,1,0:T(2,128)} %bitcast.16), calls=%async_computation.1 | async-start | bytes 65536 | tf_op jit(solution)/shard_map/all_to_all | solution.py:364
  35.0 0.6 %copy-start.1 = (f32[1,16,1024]{2,1,0:T(8,128)}, f32[1,16,1024]{2,1,0:T(8,128)S(1)}, u32[]{:S(2)}) copy-start(f32[1,16,1024]{2,1,0:T(8,128)S(1)} %fusion.1) | copy-start | bytes 196612

commit v18 on v15

--- a/solution.py
+++ b/solution.py
@@ -362,12 +362,13 @@
     received = lax.all_to_all(first_sent, ("group", "strip"), 0, 0, tiled=True)
     vorticity, sent = second_step(received, strip_node, strip_fields, first_vorticity, devices, node_count, substeps)
     received = lax.all_to_all(sent, ("group", "strip"), 0, 0, tiled=True)
-    offset = jnp.sum(received[:, substeps:], axis=0) / jnp.sqrt(jnp.float32(total_strips))
+    offset = jnp.sum(received, axis=0) / jnp.sqrt(jnp.float32(total_strips))
     group_force = lax.dynamic_slice_in_dim(received, group_position * group_strips, group_strips)
     displacement = lax.dot_general(
         group_force, unit_response, (((0,), (1,)), ((), ())), precision=EXACT_DOT
     )
-    displacement = displacement.at[substeps:, :].add(offset[:, None] * top_taper[None, :])
+    lower_half = (jnp.arange(2 * substeps) >= substeps)[:, None]
+    displacement = displacement + jnp.where(lower_half, offset[:, None] * top_taper[None, :], 0.0)
     return (vorticity, displacement[None])
 
 

time: 36.1 us -> 36.4 us (level)
  blocking collectives: 14.7 us -> 0 us
  starting transfers between devices: 2.57 us -> 9.85 us
  waiting for transfers between devices: 7.23 us -> 14.5 us
  matrix products: 0.55 us -> 1.2 us
    all_to_all x1 -> x0, blocking collectives: 14.7 us -> none  [local(): received = lax.all_to_all(first_sent, ('group', 'strip'), 0, 0, tiled=True)]
    all_to_all x0 -> x1, starting transfers between devices: none -> 7.3 us  [local(): received = lax.all_to_all(first_sent, ('group', 'strip'), 0, 0, tiled=True)]
    all_to_all x0 -> x1, waiting for transfers between devices: none -> 7.24 us  [local(): received = lax.all_to_all(first_sent, ('group', 'strip'), 0, 0, tiled=True)]
    dot_general x1, matrix products: 0.55 us -> 1.2 us  [local(): lax.dot_general(group_force, unit_response, (((0,), (1,)), ((), ())), pre...]
  transfers between devices with their start and end apart: 1 -> 2, of which waited for: 1 -> 2; matrix products, arithmetic and copies ran while one was open for 0% -> 0% of each run, Pallas kernels for 0% -> 0%
where the time goes in v18:
time: 36.4 us; the launch traced here: 36.2 us
  waiting for transfers between devices  14.5 us (40%)
  starting transfers between devices  9.85 us (27%)
  Pallas kernels  9.32 us (26%)
  matrix products  1.2 us (3%)
  between operations  0.67 us (2%)
  local copies, waits for them, and re-layouts  0.62 us (2%)
    all_to_all x1, starting transfers between devices, local(): received = lax.all_to_all(first_sent, ('group', 'strip'), 0, 0, tiled=True)  7.3 us
    all_to_all x1, waiting for transfers between devices, local(): received = lax.all_to_all(first_sent, ('group', 'strip'), 0, 0, tiled=True)  7.24 us
    all_to_all x1, waiting for transfers between devices, local(): received = lax.all_to_all(sent, ('group', 'strip'), 0, 0, tiled=True)  7.23 us
    pallas_call x1, Pallas kernels, start_step(): pl.pallas_call(lambda *refs: start_kernel(*refs, substeps=substeps), in_s...  5.8 us
    pallas_call x1, Pallas kernels, second_step(): pl.pallas_call(lambda *refs: second_kernel(*refs, substeps=substeps, node...  3.52 us
    all_to_all x1, starting transfers between devices, local(): received = lax.all_to_all(sent, ('group', 'strip'), 0, 0, tiled=True)  2.55 us
    dot_general x1, matrix products, local(): lax.dot_general(group_force, unit_response, (((0,), (1,)), ((), ())), pre...  1.2 us
  transfers between devices with their start and end apart: 2, of which 2 were waited for; matrix products, arithmetic and copies ran while one was open for 0% of the time, Pallas kernels for 0%

profile of v18, /device:TPU:0, one launch (start us, length us, event | category | flops | bytes accessed | tf_op | source)
XLA Modules:
  0.0 36.2 jit_solution(3715619126687169067)
XLA Ops:
  0.6 5.8 %start_step.1 = (f32[1024,32]{1,0:T(8,128)}, f32[2,128,128]{2,1,0:T(8,128)}, f32[64,48]{1,0:T(8,128)}) custom-call(s32[1,4]{1,0:T(1,128)} %refs_0_.1, s32[32]{0:T(128)} %bitcast.15, s32[1,32]{1,0:T(1,128)} %bitcast.13, f32[64,2]{1,0:T(8,128)} %constant.30.clone.refs_3_.refs_2_, f32[1,8,128,128]{3,2,1,0:T(8,128)} %refs_4_.2, f32[1,7,128,128]{3,2,1,0:T(8,128)} %refs_5_.2, ...), custom_call_target="tpu_custom_call" | custom-call | tf_op jit(solution)/shard_map/start_step/pallas_call | solution.py:260
  6.4 0.0 copy-start
  6.4 7.3 %all-to-all-start = ((f32[32,2,48]{2,1,0:T(2,128)}), f32[32,2,48]{2,1,0:T(2,128)S(1)}, u32[]{:S(2)}, u32[]{:S(2)}) async-start(f32[32,2,48]{2,1,0:T(2,128)} %bitcast.12), calls=%async_computation | async-start | bytes 65536 | tf_op jit(solution)/shard_map/all_to_all | solution.py:362
  13.8 7.2 %all-to-all-done = f32[32,2,48]{2,1,0:T(2,128)S(1)} async-done(((f32[32,2,48]{2,1,0:T(2,128)}), f32[32,2,48]{2,1,0:T(2,128)S(1)}, u32[]{:S(2)}, u32[]{:S(2)}) %all-to-all-start) | async-done | bytes 12320 | tf_op jit(solution)/shard_map/all_to_all | solution.py:362
  21.0 0.0 copy-start.1
  21.0 0.6 %copy-done.1 = f32[32,2,48]{2,1,0:T(2,128)} copy-done((f32[32,2,48]{2,1,0:T(2,128)}, f32[32,2,48]{2,1,0:T(2,128)S(1)}, u32[]{:S(2)}) %copy-start.1) | copy-done | bytes 12312
  21.6 3.5 %second_step.1 = (f32[2,128,128]{2,1,0:T(8,128)}, f32[64,16]{1,0:T(8,128)}) custom-call(f32[64,48]{1,0:T(8,128)} %bitcast.10, s32[1,32]{1,0:T(1,128)} %bitcast.14, f32[64,2]{1,0:T(8,128)} %constant.30.clone.refs_3_.refs_2_, f32[2,64]{1,0:T(2,128)} %constant.31.clone.refs_3_, f32[16,16]{1,0:T(8,128)} %constant.32.clone.refs_4_, f32[3,2,128,128]{3,2,1,0:T(8,128)} %refs_5_.3, ...), custom_call_target="tpu_custom_call" | custom-call | tf_op jit(solution)/shard_map/second_step/pallas_call | solution.py:333
  25.1 2.5 %all-to-all-start.1 = ((f32[32,2,16]{2,1,0:T(2,128)}), f32[32,2,16]{2,1,0:T(2,128)S(1)}, u32[]{:S(2)}, u32[]{:S(2)}) async-start(f32[32,2,16]{2,1,0:T(2,128)} %bitcast.11), calls=%async_computation.1 | async-start | bytes 65536 | tf_op jit(solution)/shard_map/all_to_all | solution.py:364
  27.7 7.2 %all-to-all-done.1 = f32[32,2,16]{2,1,0:T(2,128)S(1)} async-done(((f32[32,2,16]{2,1,0:T(2,128)}), f32[32,2,16]{2,1,0:T(2,128)S(1)}, u32[]{:S(2)}, u32[]{:S(2)}) %all-to-all-start.1) | async-done | bytes 4128 | tf_op jit(solution)/shard_map/all_to_all | solution.py:364
  34.9 0.1 reduce_sum.9
  35.0 0.0 copy-done
  35.0 1.2 %fusion = f32[1,16,1024]{2,1,0:T(8,128)} fusion(f32[1024,32]{1,0:T(8,128)S(1)} %copy-done, f32[1024]{0:T(1024)S(1)} %multiply_subtract_fusion, f32[16]{0:T(128)S(1)} %broadcast_multiply_fusion, pred[16]{0:T(512)(128)(4,1)S(1)} %iota_compare_fusion, f32[64,16]{1,0:T(8,128)S(1)} %bitcast.9, s32[]{:T(128)S(6)} %select_n.7), kind=kOutput, calls=%fused_computation.1 | convolution fusion | flops 6340608 | bytes 611332 | tf_op jit(solution)/shard_map/dot_general | solution.py:367
  (3 shorter events, 0.0 us)
Async XLA Ops:
  6.4 28.6 %copy-start = (f32[1024,32]{1,0:T(8,128)S(1)}, f32[1024,32]{1,0:T(8,128)}, u32[]{:S(2)}) copy-start(f32[1024,32]{1,0:T(8,128)} %get-tuple-element.11) | copy-start | bytes 393220
  6.4 14.6 %all-to-all-start = ((f32[32,2,48]{2,1,0:T(2,128)}), f32[32,2,48]{2,1,0:T(2,128)S(1)}, u32[]{:S(2)}, u32[]{:S(2)}) async-start(f32[32,2,48]{2,1,0:T(2,128)} %bitcast.12), calls=%async_computation | async-start | bytes 65536 | tf_op jit(solution)/shard_map/all_to_all | solution.py:362
  21.0 0.6 %copy-start.1 = (f32[32,2,48]{2,1,0:T(2,128)}, f32[32,2,48]{2,1,0:T(2,128)S(1)}, u32[]{:S(2)}) copy-start(f32[32,2,48]{2,1,0:T(2,128)S(1)} %all-to-all-done) | copy-start | bytes 36868
  25.1 9.8 %all-to-all-start.1 = ((f32[32,2,16]{2,1,0:T(2,128)}), f32[32,2,16]{2,1,0:T(2,128)S(1)}, u32[]{:S(2)}, u32[]{:S(2)}) async-start(f32[32,2,16]{2,1,0:T(2,128)} %bitcast.11), calls=%async_computation.1 | async-start | bytes 65536 | tf_op jit(solution)/shard_map/all_to_all | solution.py:364

commit v19 on v15

--- a/solution.py
+++ b/solution.py
@@ -85,8 +85,8 @@
 
 def run_substeps(vorticity, flow_x, flow_y, forcing_of, lift_kernel, drag_kernel, substeps):
     rows_across, cols_across = vorticity.shape
-    lane = lax.broadcasted_iota(jnp.int32, (1, 2 * substeps), 1)
-    row = jnp.zeros((1, 2 * substeps), jnp.float32)
+    sample = lax.broadcasted_iota(jnp.int32, (2 * substeps, cols_across), 0)
+    partial = jnp.zeros((2 * substeps, cols_across), jnp.float32)
     along_x = (TIME_STEP * 0.5) * flow_x
     along_y = (TIME_STEP * 0.5) * flow_y
     for substep in range(substeps):
@@ -104,9 +104,16 @@
             vorticity = vorticity + step
         else:
             vorticity = vorticity + step + forcing_of(substep)
-        lift = jnp.sum(jnp.sum(vorticity * lift_kernel, axis=0, keepdims=True), axis=1, keepdims=True)
-        drag = jnp.sum(jnp.sum(vorticity * drag_kernel, axis=0, keepdims=True), axis=1, keepdims=True)
-        row = row + jnp.where(lane == substep, lift, 0.0) + jnp.where(lane == substeps + substep, drag, 0.0)
+        lift = jnp.sum(vorticity * lift_kernel, axis=0, keepdims=True)
+        drag = jnp.sum(vorticity * drag_kernel, axis=0, keepdims=True)
+        partial = jnp.where(sample == substep, lift, partial)
+        partial = jnp.where(sample == substeps + substep, drag, partial)
+    column = jnp.sum(partial, axis=1, keepdims=True)
+    diagonal = (
+        lax.broadcasted_iota(jnp.int32, (2 * substeps, 2 * substeps), 0)
+        == lax.broadcasted_iota(jnp.int32, (2 * substeps, 2 * substeps), 1)
+    )
+    row = jnp.sum(jnp.where(diagonal, column, 0.0), axis=0, keepdims=True)
     return vorticity, row
 
 

time: 36.1 us -> 36.2 us (level)
  no operation moved by 1% of the time
where the time goes in v19:
time: 36.2 us; the launch traced here: 35.9 us
  blocking collectives  14.7 us (41%)
  Pallas kernels  9.4 us (26%)
  waiting for transfers between devices  7.23 us (20%)
  starting transfers between devices  2.57 us (7%)
  between operations  0.67 us (2%)
  local copies, waits for them, and re-layouts  0.66 us (2%)
  matrix products  0.55 us (2%)
    all_to_all x1, blocking collectives, local(): received = lax.all_to_all(first_sent, ('group', 'strip'), 0, 0, tiled=True)  14.7 us
    all_to_all x1, waiting for transfers between devices, local(): received = lax.all_to_all(sent, ('group', 'strip'), 0, 0, tiled=True)  7.23 us
    pallas_call x1, Pallas kernels, start_step(): pl.pallas_call(lambda *refs: start_kernel(*refs, substeps=substeps), in_s...  5.84 us
    pallas_call x1, Pallas kernels, second_step(): pl.pallas_call(lambda *refs: second_kernel(*refs, substeps=substeps, node...  3.56 us
    all_to_all x1, starting transfers between devices, local(): received = lax.all_to_all(sent, ('group', 'strip'), 0, 0, tiled=True)  2.57 us
  transfers between devices with their start and end apart: 1, of which 1 were waited for; matrix products, arithmetic and copies ran while one was open for 0% of the time, Pallas kernels for 0%

profile of v19, /device:TPU:0, one launch (start us, length us, event | category | flops | bytes accessed | tf_op | source)
XLA Modules:
  0.0 35.9 jit_solution(11401090179059694885)
XLA Ops:
  0.6 5.8 %start_step.1 = (f32[1024,32]{1,0:T(8,128)}, f32[2,128,128]{2,1,0:T(8,128)}, f32[64,48]{1,0:T(8,128)}) custom-call(s32[1,4]{1,0:T(1,128)} %refs_0_.1, s32[32]{0:T(128)} %bitcast.20, s32[1,32]{1,0:T(1,128)} %bitcast.18, f32[64,2]{1,0:T(8,128)} %constant.57.clone.refs_3_.refs_2_, f32[1,8,128,128]{3,2,1,0:T(8,128)} %refs_4_.2, f32[1,7,128,128]{3,2,1,0:T(8,128)} %refs_5_.2, ...), custom_call_target="tpu_custom_call" | custom-call | tf_op jit(solution)/shard_map/start_step/pallas_call | solution.py:267
  6.5 0.0 copy-start
  6.5 14.7 %all_to_all.23 = f32[32,2,48]{2,1,0:T(2,128)} all-to-all(f32[32,2,48]{2,1,0:T(2,128)} %bitcast.17), channel_id=1, replica_groups=mesh['group'=2,'strip'=16] {'group','strip'}, dimensions={0} | all-to-all | bytes 24576 | tf_op jit(solution)/shard_map/all_to_all | solution.py:369
  21.1 3.6 %second_step.1 = (f32[2,128,128]{2,1,0:T(8,128)}, f32[64,16]{1,0:T(8,128)}) custom-call(f32[64,48]{1,0:T(8,128)} %bitcast.15, s32[1,32]{1,0:T(1,128)} %bitcast.19, f32[64,2]{1,0:T(8,128)} %constant.57.clone.refs_3_.refs_2_, f32[2,64]{1,0:T(2,128)} %constant.58.clone.refs_3_, f32[16,16]{1,0:T(8,128)} %constant.59.clone.refs_4_, f32[3,2,128,128]{3,2,1,0:T(8,128)} %refs_5_.3, ...), custom_call_target="tpu_custom_call" | custom-call | tf_op jit(solution)/shard_map/second_step/pallas_call | solution.py:340
  24.7 2.6 %all-to-all-start.1 = ((f32[32,2,16]{2,1,0:T(2,128)}), f32[32,2,16]{2,1,0:T(2,128)S(1)}, u32[]{:S(2)}, u32[]{:S(2)}) async-start(f32[32,2,16]{2,1,0:T(2,128)} %bitcast.16), calls=%async_computation.1 | async-start | bytes 65536 | tf_op jit(solution)/shard_map/all_to_all | solution.py:371
  27.3 7.2 %all-to-all-done.1 = f32[32,2,16]{2,1,0:T(2,128)S(1)} async-done(((f32[32,2,16]{2,1,0:T(2,128)}), f32[32,2,16]{2,1,0:T(2,128)S(1)}, u32[]{:S(2)}, u32[]{:S(2)}) %all-to-all-start.1) | async-done | bytes 4128 | tf_op jit(solution)/shard_map/all_to_all | solution.py:371
  34.5 0.1 slice_reduce_fusion
  34.6 0.0 copy-done
  34.6 0.5 %fusion.2 = f32[16,1024]{1,0:T(8,128)S(1)} fusion(f32[1024,32]{1,0:T(8,128)S(1)} %copy-done, f32[64,16]{1,0:T(8,128)S(1)} %bitcast.14, s32[]{:T(128)S(6)} %select_n.3), kind=kOutput, calls=%fused_computation.4 | convolution fusion | flops 6291456 | bytes 606212 | tf_op jit(solution)/shard_map/dot_general | solution.py:374
  35.2 0.1 fusion.1
  35.3 0.0 copy-start.1
  35.3 0.6 %copy-done.1 = f32[1,16,1024]{2,1,0:T(8,128)} copy-done((f32[1,16,1024]{2,1,0:T(8,128)}, f32[1,16,1024]{2,1,0:T(8,128)S(1)}, u32[]{:S(2)}) %copy-start.1) | copy-done | bytes 65560
  (3 shorter events, 0.0 us)
Async XLA Ops:
  6.5 28.2 %copy-start = (f32[1024,32]{1,0:T(8,128)S(1)}, f32[1024,32]{1,0:T(8,128)}, u32[]{:S(2)}) copy-start(f32[1024,32]{1,0:T(8,128)} %get-tuple-element.23) | copy-start | bytes 393220
  24.7 9.8 %all-to-all-start.1 = ((f32[32,2,16]{2,1,0:T(2,128)}), f32[32,2,16]{2,1,0:T(2,128)S(1)}, u32[]{:S(2)}, u32[]{:S(2)}) async-start(f32[32,2,16]{2,1,0:T(2,128)} %bitcast.16), calls=%async_computation.1 | async-start | bytes 65536 | tf_op jit(solution)/shard_map/all_to_all | solution.py:371
  35.3 0.6 %copy-start.1 = (f32[1,16,1024]{2,1,0:T(8,128)}, f32[1,16,1024]{2,1,0:T(8,128)S(1)}, u32[]{:S(2)}) copy-start(f32[1,16,1024]{2,1,0:T(8,128)S(1)} %fusion.1) | copy-start | bytes 196612

commit v20 on v15

--- a/solution.py
+++ b/solution.py
@@ -83,7 +83,7 @@
     return (source_x, source_y, lift_kernel, drag_kernel)
 
 
-def run_substeps(vorticity, flow_x, flow_y, forcing_of, lift_kernel, drag_kernel, substeps):
+def run_substeps(vorticity, flow_x, flow_y, forcing_of, lift_kernel, drag_kernel, substeps, halo_ref=None):
     rows_across, cols_across = vorticity.shape
     lane = lax.broadcasted_iota(jnp.int32, (1, 2 * substeps), 1)
     row = jnp.zeros((1, 2 * substeps), jnp.float32)
@@ -92,8 +92,15 @@
     for substep in range(substeps):
         right_cell = pltpu.roll(vorticity, cols_across - 1, 1)
         left_cell = pltpu.roll(vorticity, 1, 1)
-        upper_cell = pltpu.roll(vorticity, rows_across - 1, 0)
-        lower_cell = pltpu.roll(vorticity, 1, 0)
+        if halo_ref is None:
+            upper_cell = pltpu.roll(vorticity, rows_across - 1, 0)
+            lower_cell = pltpu.roll(vorticity, 1, 0)
+        else:
+            halo_ref[8:8 + rows_across, :] = vorticity
+            halo_ref[7:8, :] = vorticity[rows_across - 1:rows_across, :]
+            halo_ref[8 + rows_across:9 + rows_across, :] = vorticity[0:1, :]
+            upper_cell = halo_ref[9:9 + rows_across, :]
+            lower_cell = halo_ref[7:7 + rows_across, :]
         laplacian = (right_cell + left_cell) + (upper_cell + lower_cell) - 4.0 * vorticity
         step = (
             (TIME_STEP * VISCOSITY) * laplacian
@@ -273,7 +280,7 @@
 
 
 def second_kernel(received_ref, node_ref, spread_ref, gather_ref, difference_ref, fields_ref, vorticity_ref,
-                  out_ref, sent_ref, *, substeps, node_count):
+                  out_ref, sent_ref, halo_ref, *, substeps, node_count):
     position = lax.axis_index("strip")
     group_position = lax.axis_index("group")
     total_strips, _ = received_ref.shape
@@ -312,7 +319,7 @@
 
         vorticity, row = run_substeps(
             vorticity_ref[strip], fields_ref[1, strip], fields_ref[2, strip], forcing_of,
-            lift_kernel, drag_kernel, substeps,
+            lift_kernel, drag_kernel, substeps, halo_ref.at[strip],
         )
         out_ref[strip] = vorticity
         rows = jnp.where(sublane == strip, row, rows)
@@ -337,6 +344,7 @@
             jax.ShapeDtypeStruct((per_device, cells_y, cells_x), jnp.float32),
             jax.ShapeDtypeStruct((devices * per_device, 2 * substeps), jnp.float32),
         ],
+        scratch_shapes=[pltpu.VMEM((per_device, cells_y + 16, cells_x), jnp.float32)],
         name="second_step",
     )(received, strip_node[None, :], spread, np.ascontiguousarray(spread.T), difference_matrix(substeps), strip_fields, vorticity)
 

time: 36.1 us -> 36 us (level)
  no operation moved by 1% of the time
where the time goes in v20:
time: 36 us; the launch traced here: 35.8 us
  blocking collectives  14.7 us (41%)
  Pallas kernels  9.26 us (26%)
  waiting for transfers between devices  7.23 us (20%)
  starting transfers between devices  2.57 us (7%)
  between operations  0.67 us (2%)
  local copies, waits for them, and re-layouts  0.66 us (2%)
  matrix products  0.55 us (2%)
    all_to_all x1, blocking collectives, local(): received = lax.all_to_all(first_sent, ('group', 'strip'), 0, 0, tiled=True)  14.7 us
    all_to_all x1, waiting for transfers between devices, local(): received = lax.all_to_all(sent, ('group', 'strip'), 0, 0, tiled=True)  7.23 us
    pallas_call x1, Pallas kernels, start_step(): pl.pallas_call(lambda *refs: start_kernel(*refs, substeps=substeps), in_s...  5.8 us
    pallas_call x1, Pallas kernels, second_step(): pl.pallas_call(lambda *refs: second_kernel(*refs, substeps=substeps, node...  3.46 us
    all_to_all x1, starting transfers between devices, local(): received = lax.all_to_all(sent, ('group', 'strip'), 0, 0, tiled=True)  2.57 us
  transfers between devices with their start and end apart: 1, of which 1 were waited for; matrix products, arithmetic and copies ran while one was open for 0% of the time, Pallas kernels for 0%

profile of v20, /device:TPU:0, one launch (start us, length us, event | category | flops | bytes accessed | tf_op | source)
XLA Modules:
  0.0 35.8 jit_solution(15030458264027791539)
XLA Ops:
  0.6 5.8 %start_step.1 = (f32[1024,32]{1,0:T(8,128)}, f32[2,128,128]{2,1,0:T(8,128)}, f32[64,48]{1,0:T(8,128)}) custom-call(s32[1,4]{1,0:T(1,128)} %refs_0_.1, s32[32]{0:T(128)} %bitcast.20, s32[1,32]{1,0:T(1,128)} %bitcast.18, f32[64,2]{1,0:T(8,128)} %constant.57.clone.refs_3_.refs_2_, f32[1,8,128,128]{3,2,1,0:T(8,128)} %refs_4_.2, f32[1,7,128,128]{3,2,1,0:T(8,128)} %refs_5_.2, ...), custom_call_target="tpu_custom_call" | custom-call | tf_op jit(solution)/shard_map/start_step/pallas_call | solution.py:267
  6.4 0.0 copy-start
  6.4 14.7 %all_to_all.23 = f32[32,2,48]{2,1,0:T(2,128)} all-to-all(f32[32,2,48]{2,1,0:T(2,128)} %bitcast.17), channel_id=1, replica_groups=mesh['group'=2,'strip'=16] {'group','strip'}, dimensions={0} | all-to-all | bytes 24576 | tf_op jit(solution)/shard_map/all_to_all | solution.py:370
  21.1 3.5 %second_step.1 = (f32[2,128,128]{2,1,0:T(8,128)}, f32[64,16]{1,0:T(8,128)}) custom-call(f32[64,48]{1,0:T(8,128)} %bitcast.15, s32[1,32]{1,0:T(1,128)} %bitcast.19, f32[64,2]{1,0:T(8,128)} %constant.57.clone.refs_3_.refs_2_, f32[2,64]{1,0:T(2,128)} %constant.58.clone.refs_3_, f32[16,16]{1,0:T(8,128)} %constant.59.clone.refs_4_, f32[3,2,128,128]{3,2,1,0:T(8,128)} %refs_5_.3, ...), custom_call_target="tpu_custom_call" | custom-call | tf_op jit(solution)/shard_map/second_step/pallas_call | solution.py:340
  24.6 2.6 %all-to-all-start.1 = ((f32[32,2,16]{2,1,0:T(2,128)}), f32[32,2,16]{2,1,0:T(2,128)S(1)}, u32[]{:S(2)}, u32[]{:S(2)}) async-start(f32[32,2,16]{2,1,0:T(2,128)} %bitcast.16), calls=%async_computation.1 | async-start | bytes 65536 | tf_op jit(solution)/shard_map/all_to_all | solution.py:372
  27.2 7.2 %all-to-all-done.1 = f32[32,2,16]{2,1,0:T(2,128)S(1)} async-done(((f32[32,2,16]{2,1,0:T(2,128)}), f32[32,2,16]{2,1,0:T(2,128)S(1)}, u32[]{:S(2)}, u32[]{:S(2)}) %all-to-all-start.1) | async-done | bytes 4128 | tf_op jit(solution)/shard_map/all_to_all | solution.py:372
  34.4 0.1 slice_reduce_fusion
  34.5 0.0 copy-done
  34.5 0.5 %fusion.2 = f32[16,1024]{1,0:T(8,128)S(1)} fusion(f32[1024,32]{1,0:T(8,128)S(1)} %copy-done, f32[64,16]{1,0:T(8,128)S(1)} %bitcast.14, s32[]{:T(128)S(6)} %select_n.3), kind=kOutput, calls=%fused_computation.4 | convolution fusion | flops 6291456 | bytes 606212 | tf_op jit(solution)/shard_map/dot_general | solution.py:375
  35.1 0.1 fusion.1
  35.2 0.0 copy-start.1
  35.2 0.6 %copy-done.1 = f32[1,16,1024]{2,1,0:T(8,128)} copy-done((f32[1,16,1024]{2,1,0:T(8,128)}, f32[1,16,1024]{2,1,0:T(8,128)S(1)}, u32[]{:S(2)}) %copy-start.1) | copy-done | bytes 65560
  (3 shorter events, 0.0 us)
Async XLA Ops:
  6.4 28.1 %copy-start = (f32[1024,32]{1,0:T(8,128)S(1)}, f32[1024,32]{1,0:T(8,128)}, u32[]{:S(2)}) copy-start(f32[1024,32]{1,0:T(8,128)} %get-tuple-element.23) | copy-start | bytes 393220
  24.6 9.8 %all-to-all-start.1 = ((f32[32,2,16]{2,1,0:T(2,128)}), f32[32,2,16]{2,1,0:T(2,128)S(1)}, u32[]{:S(2)}, u32[]{:S(2)}) async-start(f32[32,2,16]{2,1,0:T(2,128)} %bitcast.16), calls=%async_computation.1 | async-start | bytes 65536 | tf_op jit(solution)/shard_map/all_to_all | solution.py:372
  35.2 0.6 %copy-start.1 = (f32[1,16,1024]{2,1,0:T(8,128)}, f32[1,16,1024]{2,1,0:T(8,128)S(1)}, u32[]{:S(2)}) copy-start(f32[1,16,1024]{2,1,0:T(8,128)S(1)} %fusion.1) | copy-start | bytes 196612

commit v21 on v15

--- a/solution.py
+++ b/solution.py
@@ -272,13 +272,13 @@
     )
 
 
-def second_kernel(received_ref, node_ref, spread_ref, gather_ref, difference_ref, fields_ref, vorticity_ref,
+def second_kernel(received_ref, node_ref, spread_ref, gather_ref, difference_ref, flow_x_ref, flow_y_ref, vorticity_ref,
                   out_ref, sent_ref, *, substeps, node_count):
     position = lax.axis_index("strip")
     group_position = lax.axis_index("group")
     total_strips, _ = received_ref.shape
     strips = node_ref.shape[1]
-    per_device = fields_ref.shape[1]
+    per_device = flow_x_ref.shape[1]
     every_force = received_ref[:, 0:2 * substeps]
     offset = jnp.sum(every_force, axis=0, keepdims=True) / jnp.sqrt(jnp.float32(total_strips))
     group_force = received_ref[pl.ds(group_position * strips, strips), 0:2 * substeps]
@@ -297,7 +297,7 @@
     motion = motion + jnp.where(lane >= substeps, local_taper * offset, 0.0)
     velocity = jnp.dot(motion, difference_ref[...], precision=EXACT_DOT, preferred_element_type=jnp.float32)
 
-    source_x, source_y, lift_kernel, drag_kernel = kernel_planes(fields_ref.shape[-1])
+    source_x, source_y, lift_kernel, drag_kernel = kernel_planes(flow_x_ref.shape[-1])
     coupled_x = COUPLING * source_x
     coupled_y = COUPLING * source_y
     rows = jnp.zeros((per_device, 2 * substeps), jnp.float32)
@@ -311,7 +311,7 @@
             return picks[substep] * coupled_x - picks[substeps + substep] * coupled_y
 
         vorticity, row = run_substeps(
-            vorticity_ref[strip], fields_ref[1, strip], fields_ref[2, strip], forcing_of,
+            vorticity_ref[strip], flow_x_ref[0, strip], flow_y_ref[0, strip], forcing_of,
             lift_kernel, drag_kernel, substeps,
         )
         out_ref[strip] = vorticity
@@ -332,13 +332,18 @@
     vmem = pl.BlockSpec(memory_space=pltpu.VMEM)
     return pl.pallas_call(
         lambda *refs: second_kernel(*refs, substeps=substeps, node_count=node_count),
-        in_specs=[vmem] * 7,
+        grid=(1,),
+        in_specs=[vmem] * 5 + [
+            pl.BlockSpec((1, per_device, cells_y, cells_x), lambda step: (1, 0, 0, 0)),
+            pl.BlockSpec((1, per_device, cells_y, cells_x), lambda step: (2, 0, 0, 0)),
+            vmem,
+        ],
         out_shape=[
             jax.ShapeDtypeStruct((per_device, cells_y, cells_x), jnp.float32),
             jax.ShapeDtypeStruct((devices * per_device, 2 * substeps), jnp.float32),
         ],
         name="second_step",
-    )(received, strip_node[None, :], spread, np.ascontiguousarray(spread.T), difference_matrix(substeps), strip_fields, vorticity)
+    )(received, strip_node[None, :], spread, np.ascontiguousarray(spread.T), difference_matrix(substeps), strip_fields, strip_fields, vorticity)
 
 
 def local(strip_fields, strip_riser, strip_node, riser_owner, pivot_inv, lower_block, upper_block):

time: 36.1 us -> 36.2 us (level)
  no operation moved by 1% of the time
where the time goes in v21:
time: 36.2 us; the launch traced here: 35.9 us
  blocking collectives  14.7 us (41%)
  Pallas kernels  9.4 us (26%)
  waiting for transfers between devices  7.23 us (20%)
  starting transfers between devices  2.57 us (7%)
  between operations  0.67 us (2%)
  local copies, waits for them, and re-layouts  0.66 us (2%)
  matrix products  0.55 us (2%)
    all_to_all x1, blocking collectives, local(): received = lax.all_to_all(first_sent, ('group', 'strip'), 0, 0, tiled=True)  14.7 us
    all_to_all x1, waiting for transfers between devices, local(): received = lax.all_to_all(sent, ('group', 'strip'), 0, 0, tiled=True)  7.23 us
    pallas_call x1, Pallas kernels, start_step(): pl.pallas_call(lambda *refs: start_kernel(*refs, substeps=substeps), in_s...  5.8 us
    pallas_call x1, Pallas kernels, second_step(): pl.pallas_call(lambda *refs: second_kernel(*refs, substeps=substeps, node...  3.6 us
    all_to_all x1, starting transfers between devices, local(): received = lax.all_to_all(sent, ('group', 'strip'), 0, 0, tiled=True)  2.57 us
  transfers between devices with their start and end apart: 1, of which 1 were waited for; matrix products, arithmetic and copies ran while one was open for 0% of the time, Pallas kernels for 0%

profile of v21, /device:TPU:0, one launch (start us, length us, event | category | flops | bytes accessed | tf_op | source)
XLA Modules:
  0.0 35.9 jit_solution(5193213180245168935)
XLA Ops:
  0.6 5.8 %start_step.1 = (f32[1024,32]{1,0:T(8,128)}, f32[2,128,128]{2,1,0:T(8,128)}, f32[64,48]{1,0:T(8,128)}) custom-call(s32[1,4]{1,0:T(1,128)} %refs_0_.1, s32[32]{0:T(128)} %bitcast.20, s32[1,32]{1,0:T(1,128)} %bitcast.18, f32[64,2]{1,0:T(8,128)} %constant.57.clone.refs_3_.refs_2_, f32[1,8,128,128]{3,2,1,0:T(8,128)} %refs_4_.2, f32[1,7,128,128]{3,2,1,0:T(8,128)} %refs_5_.2, ...), custom_call_target="tpu_custom_call" | custom-call | tf_op jit(solution)/shard_map/start_step/pallas_call | solution.py:260
  6.4 14.7 %all_to_all.23 = f32[32,2,48]{2,1,0:T(2,128)} all-to-all(f32[32,2,48]{2,1,0:T(2,128)} %bitcast.17), channel_id=1, replica_groups=mesh['group'=2,'strip'=16] {'group','strip'}, dimensions={0} | all-to-all | bytes 24576 | tf_op jit(solution)/shard_map/all_to_all | solution.py:367
  21.1 0.0 copy-start
  21.1 3.6 %second_step.1 = (f32[2,128,128]{2,1,0:T(8,128)}, f32[64,16]{1,0:T(8,128)}) custom-call(f32[64,48]{1,0:T(8,128)} %bitcast.15, s32[1,32]{1,0:T(1,128)} %bitcast.19, f32[64,2]{1,0:T(8,128)} %constant.57.clone.refs_3_.refs_2_, f32[2,64]{1,0:T(2,128)} %constant.58.clone.refs_3_, f32[16,16]{1,0:T(8,128)} %constant.59.clone.refs_4_, f32[3,2,128,128]{3,2,1,0:T(8,128)} %refs_6_.3, ...), custom_call_target="tpu_custom_call" | custom-call | tf_op jit(solution)/shard_map/second_step/pallas_call | solution.py:333
  24.7 2.6 %all-to-all-start.1 = ((f32[32,2,16]{2,1,0:T(2,128)}), f32[32,2,16]{2,1,0:T(2,128)S(1)}, u32[]{:S(2)}, u32[]{:S(2)}) async-start(f32[32,2,16]{2,1,0:T(2,128)} %bitcast.16), calls=%async_computation.1 | async-start | bytes 65536 | tf_op jit(solution)/shard_map/all_to_all | solution.py:369
  27.3 7.2 %all-to-all-done.1 = f32[32,2,16]{2,1,0:T(2,128)S(1)} async-done(((f32[32,2,16]{2,1,0:T(2,128)}), f32[32,2,16]{2,1,0:T(2,128)S(1)}, u32[]{:S(2)}, u32[]{:S(2)}) %all-to-all-start.1) | async-done | bytes 4128 | tf_op jit(solution)/shard_map/all_to_all | solution.py:369
  34.5 0.1 slice_reduce_fusion
  34.6 0.0 copy-done
  34.6 0.5 %fusion.2 = f32[16,1024]{1,0:T(8,128)S(1)} fusion(f32[1024,32]{1,0:T(8,128)S(1)} %copy-done, f32[64,16]{1,0:T(8,128)S(1)} %bitcast.14, s32[]{:T(128)S(6)} %select_n.3), kind=kOutput, calls=%fused_computation.4 | convolution fusion | flops 6291456 | bytes 606212 | tf_op jit(solution)/shard_map/dot_general | solution.py:372
  35.2 0.1 fusion.1
  35.3 0.0 copy-start.1
  35.3 0.6 %copy-done.1 = f32[1,16,1024]{2,1,0:T(8,128)} copy-done((f32[1,16,1024]{2,1,0:T(8,128)}, f32[1,16,1024]{2,1,0:T(8,128)S(1)}, u32[]{:S(2)}) %copy-start.1) | copy-done | bytes 65560
  (3 shorter events, 0.0 us)
Async XLA Ops:
  21.1 13.5 %copy-start = (f32[1024,32]{1,0:T(8,128)S(1)}, f32[1024,32]{1,0:T(8,128)}, u32[]{:S(2)}) copy-start(f32[1024,32]{1,0:T(8,128)} %get-tuple-element.23) | copy-start | bytes 393220
  24.7 9.8 %all-to-all-start.1 = ((f32[32,2,16]{2,1,0:T(2,128)}), f32[32,2,16]{2,1,0:T(2,128)S(1)}, u32[]{:S(2)}, u32[]{:S(2)}) async-start(f32[32,2,16]{2,1,0:T(2,128)} %bitcast.16), calls=%async_computation.1 | async-start | bytes 65536 | tf_op jit(solution)/shard_map/all_to_all | solution.py:369
  35.3 0.6 %copy-start.1 = (f32[1,16,1024]{2,1,0:T(8,128)}, f32[1,16,1024]{2,1,0:T(8,128)S(1)}, u32[]{:S(2)}) copy-start(f32[1,16,1024]{2,1,0:T(8,128)S(1)} %fusion.1) | copy-start | bytes 196612

commit v22 on v21

--- a/solution.py
+++ b/solution.py
@@ -272,18 +272,32 @@
     )
 
 
-def second_kernel(received_ref, node_ref, spread_ref, gather_ref, difference_ref, flow_x_ref, flow_y_ref, vorticity_ref,
+def second_kernel(received_ref, node_ref, flow_x_ref, flow_y_ref, vorticity_ref,
                   out_ref, sent_ref, *, substeps, node_count):
     position = lax.axis_index("strip")
     group_position = lax.axis_index("group")
     total_strips, _ = received_ref.shape
     strips = node_ref.shape[1]
     per_device = flow_x_ref.shape[1]
+    sent_rows = received_ref.shape[0]
+    spread = (
+        lax.rem(lax.broadcasted_iota(jnp.int32, (sent_rows, per_device), 0), per_device)
+        == lax.broadcasted_iota(jnp.int32, (sent_rows, per_device), 1)
+    ).astype(jnp.float32)
+    gather = (
+        lax.rem(lax.broadcasted_iota(jnp.int32, (per_device, sent_rows), 1), per_device)
+        == lax.broadcasted_iota(jnp.int32, (per_device, sent_rows), 0)
+    ).astype(jnp.float32)
+    column_in = lax.broadcasted_iota(jnp.int32, (2 * substeps, 2 * substeps), 0)
+    column_out = lax.broadcasted_iota(jnp.int32, (2 * substeps, 2 * substeps), 1)
+    difference = (column_in == column_out).astype(jnp.float32) - (
+        (column_in + 1 == column_out) & (column_out != substeps)
+    ).astype(jnp.float32)
     every_force = received_ref[:, 0:2 * substeps]
     offset = jnp.sum(every_force, axis=0, keepdims=True) / jnp.sqrt(jnp.float32(total_strips))
     group_force = received_ref[pl.ds(group_position * strips, strips), 0:2 * substeps]
     my_coupling = jnp.dot(
-        gather_ref[...], received_ref[:, 2 * substeps:], precision=EXACT_DOT, preferred_element_type=jnp.float32
+        gather, received_ref[:, 2 * substeps:], precision=EXACT_DOT, preferred_element_type=jnp.float32
     )
     motion = jnp.dot(my_coupling, group_force, precision=EXACT_DOT, preferred_element_type=jnp.float32)
     mine = (
@@ -295,7 +309,7 @@
     lane = lax.broadcasted_iota(jnp.int32, (per_device, 2 * substeps), 1)
     sublane = lax.broadcasted_iota(jnp.int32, (per_device, 2 * substeps), 0)
     motion = motion + jnp.where(lane >= substeps, local_taper * offset, 0.0)
-    velocity = jnp.dot(motion, difference_ref[...], precision=EXACT_DOT, preferred_element_type=jnp.float32)
+    velocity = jnp.dot(motion, difference, precision=EXACT_DOT, preferred_element_type=jnp.float32)
 
     source_x, source_y, lift_kernel, drag_kernel = kernel_planes(flow_x_ref.shape[-1])
     coupled_x = COUPLING * source_x
@@ -316,7 +330,7 @@
         )
         out_ref[strip] = vorticity
         rows = jnp.where(sublane == strip, row, rows)
-    sent_ref[...] = jnp.dot(spread_ref[...], rows, precision=EXACT_DOT, preferred_element_type=jnp.float32)
+    sent_ref[...] = jnp.dot(spread, rows, precision=EXACT_DOT, preferred_element_type=jnp.float32)
 
 
 def difference_matrix(substeps):
@@ -333,7 +347,7 @@
     return pl.pallas_call(
         lambda *refs: second_kernel(*refs, substeps=substeps, node_count=node_count),
         grid=(1,),
-        in_specs=[vmem] * 5 + [
+        in_specs=[vmem] * 2 + [
             pl.BlockSpec((1, per_device, cells_y, cells_x), lambda step: (1, 0, 0, 0)),
             pl.BlockSpec((1, per_device, cells_y, cells_x), lambda step: (2, 0, 0, 0)),
             vmem,
@@ -343,7 +357,7 @@
             jax.ShapeDtypeStruct((devices * per_device, 2 * substeps), jnp.float32),
         ],
         name="second_step",
-    )(received, strip_node[None, :], spread, np.ascontiguousarray(spread.T), difference_matrix(substeps), strip_fields, strip_fields, vorticity)
+    )(received, strip_node[None, :], strip_fields, strip_fields, vorticity)
 
 
 def local(strip_fields, strip_riser, strip_node, riser_owner, pivot_inv, lower_block, upper_block):

time: 36.2 us -> 36.1 us (level)
  no operation moved by 1% of the time
where the time goes in v22:
time: 36.1 us; the launch traced here: 35.9 us
  blocking collectives  14.7 us (41%)
  Pallas kernels  9.35 us (26%)
  waiting for transfers between devices  7.23 us (20%)
  starting transfers between devices  2.57 us (7%)
  between operations  0.67 us (2%)
  local copies, waits for them, and re-layouts  0.66 us (2%)
  matrix products  0.55 us (2%)
    all_to_all x1, blocking collectives, local(): received = lax.all_to_all(first_sent, ('group', 'strip'), 0, 0, tiled=True)  14.7 us
    all_to_all x1, waiting for transfers between devices, local(): received = lax.all_to_all(sent, ('group', 'strip'), 0, 0, tiled=True)  7.23 us
    pallas_call x1, Pallas kernels, start_step(): pl.pallas_call(lambda *refs: start_kernel(*refs, substeps=substeps), in_s...  5.8 us
    pallas_call x1, Pallas kernels, second_step(): pl.pallas_call(lambda *refs: second_kernel(*refs, substeps=substeps, node...  3.55 us
    all_to_all x1, starting transfers between devices, local(): received = lax.all_to_all(sent, ('group', 'strip'), 0, 0, tiled=True)  2.57 us
  transfers between devices with their start and end apart: 1, of which 1 were waited for; matrix products, arithmetic and copies ran while one was open for 0% of the time, Pallas kernels for 0%

profile of v22, /device:TPU:0, one launch (start us, length us, event | category | flops | bytes accessed | tf_op | source)
XLA Modules:
  0.0 35.9 jit_solution(17410456741873446579)
XLA Ops:
  0.6 5.8 %start_step.1 = (f32[1024,32]{1,0:T(8,128)}, f32[2,128,128]{2,1,0:T(8,128)}, f32[64,48]{1,0:T(8,128)}) custom-call(s32[1,4]{1,0:T(1,128)} %refs_0_.1, s32[32]{0:T(128)} %bitcast.20, s32[1,32]{1,0:T(1,128)} %bitcast.18, f32[64,2]{1,0:T(8,128)} %constant.53.clone.refs_3_, f32[1,8,128,128]{3,2,1,0:T(8,128)} %refs_4_.1, f32[1,7,128,128]{3,2,1,0:T(8,128)} %refs_5_.1, ...), custom_call_target="tpu_custom_call" | custom-call | tf_op jit(solution)/shard_map/start_step/pallas_call | solution.py:260
  6.4 14.7 %all_to_all.23 = f32[32,2,48]{2,1,0:T(2,128)} all-to-all(f32[32,2,48]{2,1,0:T(2,128)} %bitcast.17), channel_id=1, replica_groups=mesh['group'=2,'strip'=16] {'group','strip'}, dimensions={0} | all-to-all | bytes 24576 | tf_op jit(solution)/shard_map/all_to_all | solution.py:381
  21.1 0.0 copy-start
  21.1 3.6 %second_step.1 = (f32[2,128,128]{2,1,0:T(8,128)}, f32[64,16]{1,0:T(8,128)}) custom-call(f32[64,48]{1,0:T(8,128)} %bitcast.15, s32[1,32]{1,0:T(1,128)} %bitcast.19, f32[3,2,128,128]{3,2,1,0:T(8,128)} %refs_3_.2, f32[3,2,128,128]{3,2,1,0:T(8,128)} %refs_3_.2, f32[2,128,128]{2,1,0:T(8,128)} %get-tuple-element.20.refs_4_), custom_call_target="tpu_custom_call" | custom-call | tf_op jit(solution)/shard_map/second_step/pallas_call | solution.py:347
  24.7 2.6 %all-to-all-start.1 = ((f32[32,2,16]{2,1,0:T(2,128)}), f32[32,2,16]{2,1,0:T(2,128)S(1)}, u32[]{:S(2)}, u32[]{:S(2)}) async-start(f32[32,2,16]{2,1,0:T(2,128)} %bitcast.16), calls=%async_computation.1 | async-start | bytes 65536 | tf_op jit(solution)/shard_map/all_to_all | solution.py:383
  27.2 7.2 %all-to-all-done.1 = f32[32,2,16]{2,1,0:T(2,128)S(1)} async-done(((f32[32,2,16]{2,1,0:T(2,128)}), f32[32,2,16]{2,1,0:T(2,128)S(1)}, u32[]{:S(2)}, u32[]{:S(2)}) %all-to-all-start.1) | async-done | bytes 4128 | tf_op jit(solution)/shard_map/all_to_all | solution.py:383
  34.5 0.1 slice_reduce_fusion
  34.6 0.0 copy-done
  34.6 0.5 %fusion.2 = f32[16,1024]{1,0:T(8,128)S(1)} fusion(f32[1024,32]{1,0:T(8,128)S(1)} %copy-done, f32[64,16]{1,0:T(8,128)S(1)} %bitcast.14, s32[]{:T(128)S(6)} %select_n.3), kind=kOutput, calls=%fused_computation.4 | convolution fusion | flops 6291456 | bytes 606212 | tf_op jit(solution)/shard_map/dot_general | solution.py:386
  35.2 0.1 fusion.1
  35.2 0.0 copy-start.1
  35.3 0.6 %copy-done.1 = f32[1,16,1024]{2,1,0:T(8,128)} copy-done((f32[1,16,1024]{2,1,0:T(8,128)}, f32[1,16,1024]{2,1,0:T(8,128)S(1)}, u32[]{:S(2)}) %copy-start.1) | copy-done | bytes 65560
  (3 shorter events, 0.0 us)
Async XLA Ops:
  21.1 13.5 %copy-start = (f32[1024,32]{1,0:T(8,128)S(1)}, f32[1024,32]{1,0:T(8,128)}, u32[]{:S(2)}) copy-start(f32[1024,32]{1,0:T(8,128)} %get-tuple-element.23) | copy-start | bytes 393220
  24.7 9.8 %all-to-all-start.1 = ((f32[32,2,16]{2,1,0:T(2,128)}), f32[32,2,16]{2,1,0:T(2,128)S(1)}, u32[]{:S(2)}, u32[]{:S(2)}) async-start(f32[32,2,16]{2,1,0:T(2,128)} %bitcast.16), calls=%async_computation.1 | async-start | bytes 65536 | tf_op jit(solution)/shard_map/all_to_all | solution.py:383
  35.2 0.6 %copy-start.1 = (f32[1,16,1024]{2,1,0:T(8,128)}, f32[1,16,1024]{2,1,0:T(8,128)S(1)}, u32[]{:S(2)}) copy-start(f32[1,16,1024]{2,1,0:T(8,128)S(1)} %fusion.1) | copy-start | bytes 196612

commit v23 on v21

--- a/solution.py
+++ b/solution.py
@@ -179,7 +179,7 @@
     return jnp.concatenate(solved, axis=1)
 
 
-def start_kernel(owner_ref, riser_ref, node_ref, spread_ref, pivot_ref, lower_ref, upper_ref, fields_ref,
+def start_kernel(owner_ref, riser_ref, node_ref, pivot_ref, lower_ref, upper_ref, fields_ref,
                  response_ref, vorticity_ref, sent_ref, *, substeps):
     block_count = pivot_ref.shape[1]
     block_size = pivot_ref.shape[2]
@@ -242,7 +242,11 @@
     sent_rows = sent_ref.shape[0]
     place = lax.broadcasted_iota(jnp.int32, (sent_rows, strips), 0) - group_position * strips
     pick = (place == lax.broadcasted_iota(jnp.int32, (sent_rows, strips), 1)).astype(jnp.float32)
-    sent_ref[:, 0:2 * substeps] = jnp.dot(spread_ref[...], rows, precision=EXACT_DOT, preferred_element_type=jnp.float32)
+    spread = (
+        lax.rem(lax.broadcasted_iota(jnp.int32, (sent_rows, per_device), 0), per_device)
+        == lax.broadcasted_iota(jnp.int32, (sent_rows, per_device), 1)
+    ).astype(jnp.float32)
+    sent_ref[:, 0:2 * substeps] = jnp.dot(spread, rows, precision=EXACT_DOT, preferred_element_type=jnp.float32)
     sent_ref[:, 2 * substeps:] = jnp.dot(pick, coupling, precision=EXACT_DOT, preferred_element_type=jnp.float32)
 
 
@@ -259,7 +263,7 @@
     vmem = pl.BlockSpec(memory_space=pltpu.VMEM)
     return pl.pallas_call(
         lambda *refs: start_kernel(*refs, substeps=substeps),
-        in_specs=[pl.BlockSpec(memory_space=pltpu.SMEM)] * 2 + [vmem] * 6,
+        in_specs=[pl.BlockSpec(memory_space=pltpu.SMEM)] * 2 + [vmem] * 5,
         out_shape=[
             jax.ShapeDtypeStruct((node_count, strips), jnp.float32),
             jax.ShapeDtypeStruct((per_device, cells_y, cells_x), jnp.float32),
@@ -267,7 +271,7 @@
         ],
         name="start_step",
     )(
-        riser_owner, strip_riser.reshape(strips), strip_node[None, :], spread_matrix(devices, per_device),
+        riser_owner, strip_riser.reshape(strips), strip_node[None, :],
         pivot_inv, lower_block, upper_block, strip_fields,
     )
 

time: 36.2 us -> 36.1 us (level)
  no operation moved by 1% of the time
where the time goes in v23:
time: 36.1 us; the launch traced here: 35.9 us
  blocking collectives  14.7 us (41%)
  Pallas kernels  9.37 us (26%)
  waiting for transfers between devices  7.23 us (20%)
  starting transfers between devices  2.57 us (7%)
  between operations  0.67 us (2%)
  local copies, waits for them, and re-layouts  0.66 us (2%)
  matrix products  0.55 us (2%)
    all_to_all x1, blocking collectives, local(): received = lax.all_to_all(first_sent, ('group', 'strip'), 0, 0, tiled=True)  14.7 us
    all_to_all x1, waiting for transfers between devices, local(): received = lax.all_to_all(sent, ('group', 'strip'), 0, 0, tiled=True)  7.23 us
    pallas_call x1, Pallas kernels, start_step(): pl.pallas_call(lambda *refs: start_kernel(*refs, substeps=substeps), in_s...  5.77 us
    pallas_call x1, Pallas kernels, second_step(): pl.pallas_call(lambda *refs: second_kernel(*refs, substeps=substeps, node...  3.6 us
    all_to_all x1, starting transfers between devices, local(): received = lax.all_to_all(sent, ('group', 'strip'), 0, 0, tiled=True)  2.57 us
  transfers between devices with their start and end apart: 1, of which 1 were waited for; matrix products, arithmetic and copies ran while one was open for 0% of the time, Pallas kernels for 0%

profile of v23, /device:TPU:0, one launch (start us, length us, event | category | flops | bytes accessed | tf_op | source)
XLA Modules:
  0.0 35.9 jit_solution(15201105918082603130)
XLA Ops:
  0.6 5.8 %start_step.1 = (f32[1024,32]{1,0:T(8,128)}, f32[2,128,128]{2,1,0:T(8,128)}, f32[64,48]{1,0:T(8,128)}) custom-call(s32[1,4]{1,0:T(1,128)} %refs_0_.1, s32[32]{0:T(128)} %bitcast.20, s32[1,32]{1,0:T(1,128)} %bitcast.18, f32[1,8,128,128]{3,2,1,0:T(8,128)} %refs_3_.2, f32[1,7,128,128]{3,2,1,0:T(8,128)} %refs_4_.2, f32[1,7,128,128]{3,2,1,0:T(8,128)} %refs_5_.2, ...), custom_call_target="tpu_custom_call" | custom-call | tf_op jit(solution)/shard_map/start_step/pallas_call | solution.py:264
  6.4 14.7 %all_to_all.23 = f32[32,2,48]{2,1,0:T(2,128)} all-to-all(f32[32,2,48]{2,1,0:T(2,128)} %bitcast.17), channel_id=1, replica_groups=mesh['group'=2,'strip'=16] {'group','strip'}, dimensions={0} | all-to-all | bytes 24576 | tf_op jit(solution)/shard_map/all_to_all | solution.py:371
  21.1 0.0 copy-start
  21.1 3.6 %second_step.1 = (f32[2,128,128]{2,1,0:T(8,128)}, f32[64,16]{1,0:T(8,128)}) custom-call(f32[64,48]{1,0:T(8,128)} %bitcast.15, s32[1,32]{1,0:T(1,128)} %bitcast.19, f32[64,2]{1,0:T(8,128)} %constant.57.clone.refs_2_, f32[2,64]{1,0:T(2,128)} %constant.58.clone.refs_3_, f32[16,16]{1,0:T(8,128)} %constant.59.clone.refs_4_, f32[3,2,128,128]{3,2,1,0:T(8,128)} %refs_6_.3, ...), custom_call_target="tpu_custom_call" | custom-call | tf_op jit(solution)/shard_map/second_step/pallas_call | solution.py:337
  24.7 2.6 %all-to-all-start.1 = ((f32[32,2,16]{2,1,0:T(2,128)}), f32[32,2,16]{2,1,0:T(2,128)S(1)}, u32[]{:S(2)}, u32[]{:S(2)}) async-start(f32[32,2,16]{2,1,0:T(2,128)} %bitcast.16), calls=%async_computation.1 | async-start | bytes 65536 | tf_op jit(solution)/shard_map/all_to_all | solution.py:373
  27.3 7.2 %all-to-all-done.1 = f32[32,2,16]{2,1,0:T(2,128)S(1)} async-done(((f32[32,2,16]{2,1,0:T(2,128)}), f32[32,2,16]{2,1,0:T(2,128)S(1)}, u32[]{:S(2)}, u32[]{:S(2)}) %all-to-all-start.1) | async-done | bytes 4128 | tf_op jit(solution)/shard_map/all_to_all | solution.py:373
  34.5 0.1 slice_reduce_fusion
  34.6 0.0 copy-done
  34.6 0.5 %fusion.2 = f32[16,1024]{1,0:T(8,128)S(1)} fusion(f32[1024,32]{1,0:T(8,128)S(1)} %copy-done, f32[64,16]{1,0:T(8,128)S(1)} %bitcast.14, s32[]{:T(128)S(6)} %select_n.3), kind=kOutput, calls=%fused_computation.4 | convolution fusion | flops 6291456 | bytes 606212 | tf_op jit(solution)/shard_map/dot_general | solution.py:376
  35.2 0.1 fusion.1
  35.3 0.0 copy-start.1
  35.3 0.6 %copy-done.1 = f32[1,16,1024]{2,1,0:T(8,128)} copy-done((f32[1,16,1024]{2,1,0:T(8,128)}, f32[1,16,1024]{2,1,0:T(8,128)S(1)}, u32[]{:S(2)}) %copy-start.1) | copy-done | bytes 65560
  (3 shorter events, 0.0 us)
Async XLA Ops:
  21.1 13.5 %copy-start = (f32[1024,32]{1,0:T(8,128)S(1)}, f32[1024,32]{1,0:T(8,128)}, u32[]{:S(2)}) copy-start(f32[1024,32]{1,0:T(8,128)} %get-tuple-element.23) | copy-start | bytes 393220
  24.7 9.8 %all-to-all-start.1 = ((f32[32,2,16]{2,1,0:T(2,128)}), f32[32,2,16]{2,1,0:T(2,128)S(1)}, u32[]{:S(2)}, u32[]{:S(2)}) async-start(f32[32,2,16]{2,1,0:T(2,128)} %bitcast.16), calls=%async_computation.1 | async-start | bytes 65536 | tf_op jit(solution)/shard_map/all_to_all | solution.py:373
  35.3 0.6 %copy-start.1 = (f32[1,16,1024]{2,1,0:T(8,128)}, f32[1,16,1024]{2,1,0:T(8,128)S(1)}, u32[]{:S(2)}) copy-start(f32[1,16,1024]{2,1,0:T(8,128)S(1)} %fusion.1) | copy-start | bytes 196612
